TPU v7x, 128 devices: a whole 4x4x4 slice. The times are simulated.
128 devices in a mesh: gx: 128 (over y, x, z, core).
Axes of the slice: x: 4, y: 4, z: 4, core: 2. Of those that a mesh axis runs over, the one named last changes fastest.
Arguments:
- right_side: float32 [1024, 256, 256], P('gx'), may hold values from -6 to 6, as said below
- density: float32 [1024, 256, 256], P('gx'), may hold values from 0.25 to 4
Outputs:
- pressure: float32 [1024, 256, 256], P('gx')
- pending: float32 [1024, 256, 256], P('gx')
Inputs may be any that keep to these rules, and one draw needn't show every extreme that they name: `right_side`: rough values in every cell.
All inputs are finite; a program needn't handle non-finite values.
Results may differ from a plain program's by a relative error of at most 0.0003.
Values sent between devices are 32-bit elements; how exact they have to be, the bound alone decides.
No kernel may reach another device: no remote copies, remote signals or barrier semaphores. Data moves between devices by JAX's collectives and lax.ppermute only.
A program may use at most 128 MiB of HBM per device.

v0:
```python
import math

import jax
import jax.numpy as jnp
from jax import lax
from jax.experimental import pallas as pl
from jax.experimental.pallas import tpu as pltpu
from jax.sharding import PartitionSpec as P

SWEEPS = 3
TOP_SWEEPS = 6
CYCLES = 2


OMEGA = 0.8
EXACT = lax.Precision.HIGHEST


def recv(value, steps, cyclic):
    count = lax.axis_size("gx")
    if cyclic:
        pairs = [(i, (i + steps) % count) for i in range(count)]
    else:
        pairs = [(i, i + steps) for i in range(count) if 0 <= i + steps < count]
    return lax.ppermute(value, "gx", pairs)


def inside(per_device, ghosts, length):
    count = lax.axis_size("gx")
    first = lax.axis_index("gx") * per_device - ghosts
    index = first + jnp.arange(length, dtype=jnp.int32)
    keep = (index >= 0) & (index < count * per_device)
    return keep.astype(jnp.float32)[:, None, None]


def exchange(to_right, to_left, steps, cyclic=False):
    arrays_r, arrays_l = list(to_right), list(to_left)
    shapes = [a.shape for a in arrays_r]
    stacked = all(shape[1:] == shapes[0][1:] for shape in shapes)
    if stacked:
        flat_r = jnp.concatenate(arrays_r)
        flat_l = jnp.concatenate(arrays_l)
    else:
        flat_r = jnp.concatenate([a.reshape(-1) for a in arrays_r])
        flat_l = jnp.concatenate([a.reshape(-1) for a in arrays_l])
    got_l, got_r = recv(flat_r, steps, cyclic), recv(flat_l, -steps, cyclic)

    def split(flat):
        out, at = [], 0
        for shape in shapes:
            if stacked:
                out.append(flat[at:at + shape[0]])
                at += shape[0]
            else:
                size = math.prod(shape)
                out.append(flat[at:at + size].reshape(shape))
                at += size
        return out

    return split(got_l), split(got_r)


def pair_matrix(extent):
    rows = jnp.arange(extent, dtype=jnp.int32)[:, None] // 2
    cols = jnp.arange(extent // 2, dtype=jnp.int32)[None, :]
    return (rows == cols).astype(jnp.float32)


def shrink_sides(field):
    extent_y = field.shape[1]
    extent_z = field.shape[2]
    along_z = jnp.einsum("xyz,zw->xyw", field, pair_matrix(extent_z), precision=EXACT)
    return jnp.einsum("xyw,yv->xvw", along_z, pair_matrix(extent_y), precision=EXACT)


def grow_sides(field):
    extent_y = field.shape[1]
    extent_z = field.shape[2]
    along_z = jnp.einsum("xyw,zw->xyz", field, pair_matrix(2 * extent_z), precision=EXACT)
    return jnp.einsum("xvz,yv->xyz", along_z, pair_matrix(2 * extent_y), precision=EXACT)


def coarsen(field):
    extent_x, extent_y, extent_z = field.shape
    planes = field.reshape(extent_x // 2, 2, extent_y, extent_z).sum(axis=1)
    return shrink_sides(planes) * 0.125


def refine(field):
    extent_x, extent_y, extent_z = field.shape
    wider = grow_sides(field)
    spread = jnp.broadcast_to(wider[:, None], (extent_x, 2, 2 * extent_y, 2 * extent_z))
    return spread.reshape(2 * extent_x, 2 * extent_y, 2 * extent_z)


def make_coefs(rho_ext, inv_spacing):
    two_s = 2.0 * inv_spacing
    center = rho_ext[1:-1]
    safe = jnp.where(center > 0, center, 1.0)
    padded = jnp.pad(center, ((0, 0), (1, 1), (1, 1)), mode="edge")
    near = [
        rho_ext[:-2],
        rho_ext[2:],
        padded[:, :-2, 1:-1],
        padded[:, 2:, 1:-1],
        padded[:, 1:-1, :-2],
        padded[:, 1:-1, 2:],
    ]
    faces = [two_s / (safe + jnp.where(nb > 0, nb, safe)) for nb in near]
    diag = faces[0] + faces[1] + faces[2] + faces[3] + faces[4] + faces[5]
    lo, hi = rho_ext[:-1], rho_ext[1:]
    kxo = jnp.where((lo > 0) & (hi > 0), two_s / (lo + hi), 0.0)
    return {
        "kxo": kxo,
        "kyl": faces[2],
        "kyh": faces[3],
        "kzl": faces[4],
        "kzh": faces[5],
        "w": OMEGA / diag,
        "diag": diag,
    }


def side_terms(field, co, lo, hi):
    padded = jnp.pad(field, ((0, 0), (1, 1), (1, 1)))
    return (
        co["kyl"][lo:hi] * padded[:, :-2, 1:-1]
        + co["kyh"][lo:hi] * padded[:, 2:, 1:-1]
        + co["kzl"][lo:hi] * padded[:, 1:-1, :-2]
        + co["kzh"][lo:hi] * padded[:, 1:-1, 2:]
    )


def smooth(resid, co, sweeps):
    length = resid.shape[0]
    kxo = co["kxo"][1:-1]
    update = co["w"] * resid
    for sweep_no in range(1, sweeps):
        lo, hi = sweep_no, length - sweep_no
        inner = update[1:-1]
        off = (
            kxo[lo - 1:hi - 1] * update[:-2]
            + kxo[lo:hi] * update[2:]
            + side_terms(inner, co, lo, hi)
        )
        update = (1.0 - OMEGA) * inner + co["w"][lo:hi] * (resid[lo:hi] + off)
    return update


ROWS = 16
PAD = 8
VMEM_LIMIT = 64 * 1024 * 1024


def _zero_pads(buf):
    extent_y, extent_z = buf.shape[1] - 2 * PAD, buf.shape[2]
    zeros = jnp.zeros((PAD, extent_z), jnp.float32)

    def body(p, carry):
        buf[p, pl.ds(0, PAD), :] = zeros
        buf[p, pl.ds(PAD + extent_y, PAD), :] = zeros
        return carry

    lax.fori_loop(0, buf.shape[0], body, 0)


def _plane_loop(first, last, extent_y, body):
    chunks = extent_y // ROWS

    def step(i, carry):
        q = first + i // chunks
        y0 = pl.multiple_of((i % chunks) * ROWS, ROWS)
        body(q, y0)
        return carry

    lax.fori_loop(0, (last - first) * chunks, step, 0)


def _neighbour_sum(src, at, y0, kxo_lo, kxo_hi, kyl, kyh, kzl, kzh):
    extent_z = src.shape[2]
    center = src[at, pl.ds(PAD + y0, ROWS), :]
    below = pltpu.roll(src[at, pl.ds(y0, ROWS + PAD), :], 1, 0)[PAD:PAD + ROWS]
    above = pltpu.roll(src[at, pl.ds(PAD + y0, ROWS + PAD), :], ROWS + PAD - 1, 0)[:ROWS]
    left = pltpu.roll(center, 1, 1)
    right = pltpu.roll(center, extent_z - 1, 1)
    off = (
        kxo_lo * src[at - 1, pl.ds(PAD + y0, ROWS), :]
        + kxo_hi * src[at + 1, pl.ds(PAD + y0, ROWS), :]
        + kyl * below
        + kyh * above
        + kzl * left
        + kzh * right
    )
    return center, off


def _smooth_in_vmem(resid, kxo, kyl, kyh, kzl, kzh, w, out, bufs, sweeps):
    length, extent_y = resid.shape[0], resid.shape[1]
    for buf in bufs:
        _zero_pads(buf)

    def first(q, y0):
        rows = pl.ds(y0, ROWS)
        bufs[0][q, pl.ds(PAD + y0, ROWS), :] = w[q, rows, :] * resid[q, rows, :]

    _plane_loop(0, length, extent_y, first)
    for sweep_no in range(1, sweeps):
        src = bufs[(sweep_no - 1) % 2]
        src_at = sweep_no - 1
        last = sweep_no == sweeps - 1
        dst = out if last else bufs[sweep_no % 2]
        dst_at = sweep_no

        def body(q, y0, src=src, src_at=src_at, dst=dst, dst_at=dst_at, last=last):
            rows = pl.ds(y0, ROWS)
            center, off = _neighbour_sum(
                src, q - src_at, y0, kxo[q - 1, rows, :], kxo[q, rows, :],
                kyl[q, rows, :], kyh[q, rows, :], kzl[q, rows, :], kzh[q, rows, :],
            )
            new = (1.0 - OMEGA) * center + w[q, rows, :] * (resid[q, rows, :] + off)
            if last:
                dst[q - dst_at, rows, :] = new
            else:
                dst[q - dst_at, pl.ds(PAD + y0, ROWS), :] = new

        _plane_loop(sweep_no, length - sweep_no, extent_y, body)


def _fine_first_kernel(resid, kxo, kyl, kyh, kzl, kzh, w, out, buf_a, buf_b):
    _smooth_in_vmem(resid, kxo, kyl, kyh, kzl, kzh, w, out, (buf_a, buf_b), SWEEPS)


def _fine_second_kernel(
    fine_ext, rhs, kxo_full, kyl, kyh, kzl, kzh, w, diag, out, resid_out, held, resid, buf_a, buf_b
):
    planes, extent_y = fine_ext.shape[0], fine_ext.shape[1]
    _zero_pads(held)

    def copy_in(q, y0):
        held[q, pl.ds(PAD + y0, ROWS), :] = fine_ext[q, pl.ds(y0, ROWS), :]

    _plane_loop(0, planes, extent_y, copy_in)

    def residual(q, y0):
        rows = pl.ds(y0, ROWS)
        center, off = _neighbour_sum(
            held, q + 1, y0, kxo_full[q, rows, :], kxo_full[q + 1, rows, :],
            kyl[q, rows, :], kyh[q, rows, :], kzl[q, rows, :], kzh[q, rows, :],
        )
        resid[q, rows, :] = rhs[q, rows, :] - (diag[q, rows, :] * center - off)

    _plane_loop(0, planes - 2, extent_y, residual)
    ghosts = SWEEPS - 1

    def copy_out(q, y0):
        rows = pl.ds(y0, ROWS)
        resid_out[q - ghosts, rows, :] = resid[q, rows, :]

    _plane_loop(ghosts, planes - 2 - ghosts, extent_y, copy_out)
    _smooth_in_vmem(
        resid, kxo_full.at[1:-1], kyl, kyh, kzl, kzh, w, out, (buf_a, buf_b), SWEEPS
    )


def _vmem_call(kernel, outs, scratch, *args):
    return pl.pallas_call(
        kernel,
        out_shape=outs,
        in_specs=[pl.BlockSpec(memory_space=pltpu.VMEM)] * len(args),
        out_specs=(
            [pl.BlockSpec(memory_space=pltpu.VMEM)] * len(outs)
            if isinstance(outs, (list, tuple))
            else pl.BlockSpec(memory_space=pltpu.VMEM)
        ),
        scratch_shapes=scratch,
        compiler_params=pltpu.CompilerParams(vmem_limit_bytes=VMEM_LIMIT),
    )(*args)


def fine_coefs(co):
    extent_y, extent_z = co["kyl"].shape[1], co["kyl"].shape[2]
    ys = jnp.arange(extent_y, dtype=jnp.int32)[None, :, None]
    zs = jnp.arange(extent_z, dtype=jnp.int32)[None, None, :]
    return {
        "kyl": jnp.where(ys == 0, 0.0, co["kyl"]),
        "kyh": jnp.where(ys == extent_y - 1, 0.0, co["kyh"]),
        "kzl": jnp.where(zs == 0, 0.0, co["kzl"]),
        "kzh": jnp.where(zs == extent_z - 1, 0.0, co["kzh"]),
    }


def fine_smooth(resid_ext, co, fc):
    length, extent_y, extent_z = resid_ext.shape
    out = jax.ShapeDtypeStruct((length - 2 * (SWEEPS - 1), extent_y, extent_z), jnp.float32)
    padded = lambda planes: pltpu.VMEM((planes, extent_y + 2 * PAD, extent_z), jnp.float32)
    return _vmem_call(
        _fine_first_kernel, out, [padded(length), padded(length - 2)],
        resid_ext, co["kxo"][1:-1], fc["kyl"], fc["kyh"], fc["kzl"], fc["kzh"], co["w"],
    )


def fine_second(fine_ext, rhs_ext, co, fc):
    planes, extent_y, extent_z = fine_ext.shape
    length = planes - 2
    block = length - 2 * (SWEEPS - 1)
    outs = [jax.ShapeDtypeStruct((block, extent_y, extent_z), jnp.float32)] * 2
    padded = lambda n: pltpu.VMEM((n, extent_y + 2 * PAD, extent_z), jnp.float32)
    return _vmem_call(
        _fine_second_kernel, outs,
        [padded(planes), pltpu.VMEM((length, extent_y, extent_z), jnp.float32),
         padded(length), padded(length - 2)],
        fine_ext, rhs_ext, co["kxo"], fc["kyl"], fc["kyh"], fc["kzl"], fc["kzh"], co["w"], co["diag"],
    )


def per_device(right_side, density):
    me = lax.axis_index("gx")

    (dl, rl), (dr, rr) = exchange(
        [density[-3:], right_side[-2:]], [density[:3], right_side[:2]], 1
    )
    rho0_ext = jnp.concatenate([dl, density, dr])
    rhs_ext = jnp.concatenate([rl, right_side, rr])
    co0 = make_coefs(rho0_ext, 1.0)

    rho1 = coarsen(density)
    rho2 = coarsen(rho1)
    rho3 = coarsen(rho2)

    def restrict(resid):
        r1 = coarsen(resid)
        r2 = coarsen(r1)
        return r1, r2, coarsen(r2)

    def gather_coarse(r1, r2, r3, with_rho):
        to_right = [r1[-2:], r2, r3]
        to_left = [r1[:2], r2, r3]
        if with_rho:
            to_right += [rho1[-3:], rho2, rho3]
            to_left += [rho1[:3], rho2, rho3]
        got_l, got_r = exchange(to_right, to_left, 1, True)
        r1e = jnp.concatenate([got_l[0], r1, got_r[0]])
        r2e = jnp.concatenate([got_l[1], r2, got_r[1]])
        win3 = [jnp.concatenate([got_l[2], r3, got_r[2]])]
        extra = {}
        if with_rho:
            extra["rho1e"] = jnp.concatenate([got_l[3], rho1, got_r[3]])
            rho2_l, rho2_r = got_l[4], got_r[4]
            win3.append(jnp.concatenate([got_l[5], rho3, got_r[5]]))
        to_right = list(win3)
        to_left = list(win3)
        if with_rho:
            to_right.append(rho2_r[-1:])
            to_left.append(rho2_l[:1])
        got_l, got_r = exchange(to_right, to_left, 3, True)
        win9 = [jnp.concatenate([got_l[k], win3[k], got_r[k]]) for k in range(len(win3))]
        if with_rho:
            extra["rho2e"] = jnp.concatenate([got_l[-1], rho2_l, rho2, rho2_r, got_r[-1]])
        got_l, got_r = exchange(win9, win9, 9, True)
        win27 = [jnp.concatenate([got_l[k], win9[k], got_r[k]]) for k in range(len(win9))]
        win27 = [part * inside(1, 13, 27) for part in win27]
        r1e = r1e * inside(4, 2, r1e.shape[0])
        r2e = r2e * inside(2, 2, r2e.shape[0])
        if with_rho:
            extra["rho1e"] = extra["rho1e"] * inside(4, 3, extra["rho1e"].shape[0])
            extra["rho2e"] = extra["rho2e"] * inside(2, 3, extra["rho2e"].shape[0])
        return r1e, r2e, win27, extra

    r1, r2, r3 = restrict(right_side)
    r1e, r2e, win, extra = gather_coarse(r1, r2, r3, True)
    r3w, rho3w = win
    co1 = make_coefs(extra["rho1e"], 0.25)
    co2 = make_coefs(extra["rho2e"], 0.25**2)
    center = 13
    co3 = make_coefs(rho3w[center - 3:center + 4], 0.25**3)
    pair_start = 1 - me % 2

    def to_top(window):
        return coarsen(lax.dynamic_slice_in_dim(window, pair_start, 2 * center))

    co4 = make_coefs(to_top(rho3w), 0.25**4)

    def coarse_part(r1e, r2e, r3w):
        top = smooth(to_top(r3w)[1:-1], co4, TOP_SWEEPS)
        summed = grow_sides(top) + smooth(r3w[center - 2:center + 3], co3, SWEEPS)
        summed = refine(summed) + smooth(r2e, co2, SWEEPS)
        summed = refine(summed) + smooth(r1e, co1, SWEEPS)
        return refine(summed)

    fc0 = fine_coefs(co0)
    fine_0 = fine_smooth(rhs_ext, co0, fc0)
    coarse_0 = coarse_part(r1e, r2e, r3w)

    (fl,), (fr,) = exchange([fine_0[-3:]], [fine_0[:3]], 1)
    fine_ext = jnp.concatenate([fl, fine_0, fr])
    fine_1, resid_block = fine_second(fine_ext, rhs_ext, co0, fc0)
    r1, r2, r3 = restrict(resid_block)
    r1e, r2e, win, _ = gather_coarse(r1, r2, r3, False)
    coarse_1 = coarse_part(r1e, r2e, win[0])

    pressure = (fine_0 + fine_1) + coarse_0
    return (pressure, coarse_1)


def solution(mesh):
    return jax.shard_map(
        per_device,
        mesh=mesh,
        in_specs=(P("gx", None, None), P("gx", None, None)),
        out_specs=(P("gx", None, None), P("gx", None, None)),
        check_vma=False,
    )
```

profile of v0, /device:TPU:117, one launch (start us, length us, event | category | flops | bytes accessed | tf_op | source)
XLA Modules:
  0.0 309.1 jit_solution(1516611019938211836)
XLA Ops:
  0.6 1.4 fusion.596
  3.8 2.6 collective-permute-start.1
  7.5 5.1 %collective-permute-start = (f32[5,256,256]{2,1,0:T(8,128)}, f32[5,256,256]{2,1,0:T(8,128)}, u32[]{:S(2)}, u32[]{:S(2)}) collective-permute-start(f32[5,256,256]{2,1,0:T(8,128)} %pad_maximum_fusion.12), channel_id=1, source_target_pairs={{0,1},{1,2},{2,3},{3,4},{4,5},{5,6},{6,7},{7,8},{8,9},{9,10},{10,1... | collective-permute-start | bytes 3932168 | tf_op jit(solution)/shard_map/ppermute | solution.py:25
  24.1 3.9 %collective-permute-start.4 = (f32[100352]{0:T(1024)}, f32[100352]{0:T(1024)}, u32[]{:S(2)}, u32[]{:S(2)}) collective-permute-start(f32[100352]{0:T(1024)} %get-tuple-element.95), channel_id=1, source_target_pairs={{0,1},{1,2},{2,3},{3,4},{4,5},{5,6},{6,7},{7,8},{8,9},{9,10},{10,1... | collective-permute-start | bytes 1204232 | tf_op jit(solution)/shard_map/ppermute | solution.py:25
  30.3 3.4 %collective-permute-done.5 = f32[100352]{0:T(1024)S(1)} collective-permute-done((f32[100352]{0:T(1024)}, f32[100352]{0:T(1024)S(1)}, u32[]{:S(2)}, u32[]{:S(2)}) %collective-permute-start.5) | collective-permute-done | bytes 401440 | tf_op jit(solution)/shard_map/ppermute | solution.py:25
  35.1 1.3 fusion.34
  39.9 1.7 collective-permute-start.7
  41.6 1.2 fusion.598
  45.1 1.6 slice.1920
  55.1 14.7 %collective-permute-start.8 = (f32[18,32,32]{2,1,0:T(8,128)}, f32[18,32,32]{2,1,0:T(8,128)S(1)}, u32[]{:S(2)}, u32[]{:S(2)}) collective-permute-start(f32[18,32,32]{2,1,0:T(8,128)} %constant_dynamic-update-slice_fusion.2), channel_id=1, source_target_pairs={{0,9},{1,10},{2,11},{3,12},{4,13},{5,14},{6,15},{7,16},{8,17},{9,1... | collective-permute-start | bytes 221192 | tf_op jit(solution)/shard_map/ppermute | solution.py:25
  71.4 2.4 collective-permute-done.8
  75.4 1.2 slice.1750
  76.6 1.2 slice.1749
  79.2 1.4 copy-done.3
  80.5 1.8 slice.1753.kxo
  83.2 1.2 slice.1748
  85.5 1.8 pad_maximum_fusion.11.resid.rhs
  87.3 7.1 %broadcast_divide_fusion = (f32[12,256,256]{2,1,0:T(8,128)}, f32[12,256,256]{2,1,0:T(8,128)}) fusion(f32[12,258,1]{2,1,0:T(8,128)S(1)} %get-tuple-element.32, f32[12,1,256]{2,1,0:T(1,128)S(1)} %get-tuple-element.30, f32[12,256,256]{2,1,0:T(8,128)S(1)} %slice.1754, f32[12,1,256]{2,1,0:T(1,128)S(1)} %get-tuple-element.31, ...), kind=kLoop, calls=%fused_computation.41 | loop fusion | flops 31457280 | bytes 15777984 | tf_op jit(solution)/shard_map/div | solution.py:119
  94.4 9.2 %broadcast_select_fusion = (f32[12,256,256]{2,1,0:T(8,128)}, f32[12,256,256]{2,1,0:T(8,128)}, f32[12,256,256]{2,1,0:T(8,128)}, f32[12,256,256]{2,1,0:T(8,128)}) fusion(pred[256]{0:T(512)(128)(4,1)S(1)} %get-tuple-element.112, f32[12,258,1]{2,1,0:T(8,128)S(1)} %get-tuple-element.32, f32[12,1,256]{2,1,0:T(1,128)S(1)} %get-tuple-element.30, ...), kind=kLoop, calls=%fused_computation.42 | loop fusion | flops 23592960 | bytes 15778496 | tf_op jit(solution)/shard_map/jit(_where)/select_n | solution.py:288
  103.6 35.1 %shard_map.41 = f32[8,256,256]{2,1,0:T(8,128)} custom-call(f32[12,256,256]{2,1,0:T(8,128)} %pad_maximum_fusion.11.resid.rhs, f32[11,256,256]{2,1,0:T(8,128)} %slice.1753.kxo, f32[12,256,256]{2,1,0:T(8,128)} %get-tuple-element.36.kyl, f32[12,256,256]{2,1,0:T(8,128)} %get-tuple-element.37.kyh, f32[12,256,256]{2,1,0:T(8,128)} %get-tuple-element.35.kzl, ...), custom_call_target="tpu_custom_call" | custom-call | tf_op jit(solution)/shard_map/pallas_call | solution.py:266
  138.8 1.6 fusion.594
  140.4 1.9 collective-permute-start.3
  142.3 5.8 %collective-permute-start.2 = (f32[3,256,256]{2,1,0:T(8,128)S(1)}, f32[3,256,256]{2,1,0:T(8,128)S(1)}, u32[]{:S(2)}, u32[]{:S(2)}) collective-permute-start(f32[3,256,256]{2,1,0:T(8,128)S(1)} %get-tuple-element.38), channel_id=1, source_target_pairs={{0,1},{1,2},{2,3},{3,4},{4,5},{5,6},{6,7},{7,8},{8,9},{9,10},{10,1... | collective-permute-start | bytes 2359304 | tf_op jit(solution)/shard_map/ppermute | solution.py:25
  151.8 4.1 %collective-permute-done.3 = f32[3,256,256]{2,1,0:T(8,128)S(1)} collective-permute-done((f32[3,256,256]{2,1,0:T(8,128)S(1)}, f32[3,256,256]{2,1,0:T(8,128)S(1)}, u32[]{:S(2)}, u32[]{:S(2)}) %collective-permute-start.3) | collective-permute-done | bytes 786464 | tf_op jit(solution)/shard_map/ppermute | solution.py:25
  155.8 1.2 collective-permute-done.2
  157.0 2.1 pad_maximum_fusion.1.fine_ext
  159.1 58.1 %shard_map.42 = (f32[8,256,256]{2,1,0:T(8,128)}, f32[8,256,256]{2,1,0:T(8,128)}) custom-call(f32[14,256,256]{2,1,0:T(8,128)} %pad_maximum_fusion.1.fine_ext, f32[12,256,256]{2,1,0:T(8,128)} %pad_maximum_fusion.11.resid.rhs, f32[13,256,256]{2,1,0:T(8,128)} %copy-done.3, f32[12,256,256]{2,1,0:T(8,128)} %get-tuple-element.36.kyl, ...), custom_call_target="tpu_custom_call" | custom-call | tf_op jit(solution)/shard_map/pallas_call | solution.py:266
  217.2 1.9 bitcast_reduce_fusion
  221.6 4.7 %collective-permute-start.10 = (f32[41984]{0:T(1024)S(1)}, f32[41984]{0:T(1024)S(1)}, u32[]{:S(2)}, u32[]{:S(2)}) collective-permute-start(f32[41984]{0:T(1024)S(1)} %get-tuple-element.87), channel_id=1, source_target_pairs={{0,1},{1,2},{2,3},{3,4},{4,5},{5,6},{6,7},{7,8},{8,9},{9,10},{10,1... | collective-permute-start | bytes 503816 | tf_op jit(solution)/shard_map/ppermute | solution.py:25
  226.3 1.7 slice_dynamic-update-slice_fusion
  228.0 1.8 collective-permute-done.11
  232.7 2.3 fusion.576
  238.8 15.7 %collective-permute-start.14 = (f32[9,32,32]{2,1,0:T(8,128)S(1)}, f32[9,32,32]{2,1,0:T(8,128)S(1)}, u32[]{:S(2)}, u32[]{:S(2)}) collective-permute-start(f32[9,32,32]{2,1,0:T(8,128)S(1)} %constant_dynamic-update-slice_fusion.27), channel_id=1, source_target_pairs={{0,9},{1,10},{2,11},{3,12},{4,13},{5,14},{6,15},{7,16},{8,17},{9,1... | collective-permute-start | bytes 110600 | tf_op jit(solution)/shard_map/ppermute | solution.py:25
  254.8 1.8 collective-permute-done.14
  256.6 7.2 %collective-permute-done.15 = f32[9,32,32]{2,1,0:T(8,128)S(1)} collective-permute-done((f32[9,32,32]{2,1,0:T(8,128)S(1)}, f32[9,32,32]{2,1,0:T(8,128)S(1)}, u32[]{:S(2)}, u32[]{:S(2)}) %collective-permute-start.15) | collective-permute-done | bytes 36896 | tf_op jit(solution)/shard_map/ppermute | solution.py:25
  270.5 1.5 slice.1842
  272.0 1.6 divide_select_fusion.3
  273.7 1.8 constant_dynamic-slice_fusion
  275.5 1.8 reduce_sum.119
  277.2 1.4 fusion.530
  278.9 1.9 fusion.196
  280.7 2.6 slice_multiply_fusion.14
  283.4 1.8 constant_dynamic-slice_fusion.1
  285.2 1.8 reduce_sum.115
  287.0 1.5 fusion.533
  288.8 1.3 fusion.236
  305.9 1.7 bitcast_add_fusion
  307.6 1.5 broadcast_in_dim.85
  (447 shorter events, 73.2 us)
Async XLA Ops:
  3.8 71.6 %collective-permute-start.1 = (f32[5,256,256]{2,1,0:T(8,128)}, f32[5,256,256]{2,1,0:T(8,128)}, u32[]{:S(2)}, u32[]{:S(2)}) collective-permute-start(f32[5,256,256]{2,1,0:T(8,128)} %pad_maximum_fusion.13), channel_id=1, source_target_pairs={{1,0},{2,1},{3,2},{4,3},{5,4},{6,5},{7,6},{8,7},{9,8},{10,9},{11,1... | collective-permute-start | bytes 3932168 | tf_op jit(solution)/shard_map/ppermute | solution.py:25
  7.5 69.0 %collective-permute-start = (f32[5,256,256]{2,1,0:T(8,128)}, f32[5,256,256]{2,1,0:T(8,128)}, u32[]{:S(2)}, u32[]{:S(2)}) collective-permute-start(f32[5,256,256]{2,1,0:T(8,128)} %pad_maximum_fusion.12), channel_id=1, source_target_pairs={{0,1},{1,2},{2,3},{3,4},{4,5},{5,6},{6,7},{7,8},{8,9},{9,10},{10,1... | collective-permute-start | bytes 3932168 | tf_op jit(solution)/shard_map/ppermute | solution.py:25
  19.5 33.7 %copy-start.72 = (f32[32,32]{1,0:T(8,128)}, f32[32,32]{1,0:T(8,128)S(1)}, u32[]{:S(2)}) copy-start(f32[32,32]{1,0:T(8,128)S(1)} %convolution_multiply_fusion.8) | copy-start | bytes 12292
  24.1 9.6 %collective-permute-start.5 = (f32[100352]{0:T(1024)}, f32[100352]{0:T(1024)S(1)}, u32[]{:S(2)}, u32[]{:S(2)}) collective-permute-start(f32[100352]{0:T(1024)} %get-tuple-element.96), channel_id=1, source_target_pairs={{0,127},{1,0},{2,1},{3,2},{4,3},{5,4},{6,5},{7,6},{8,7},{9,8},{10,... | collective-permute-start | bytes 1204232 | tf_op jit(solution)/shard_map/ppermute | solution.py:25
  24.1 9.6 %collective-permute-start.4 = (f32[100352]{0:T(1024)}, f32[100352]{0:T(1024)}, u32[]{:S(2)}, u32[]{:S(2)}) collective-permute-start(f32[100352]{0:T(1024)} %get-tuple-element.95), channel_id=1, source_target_pairs={{0,1},{1,2},{2,3},{3,4},{4,5},{5,6},{6,7},{7,8},{8,9},{9,10},{10,1... | collective-permute-start | bytes 1204232 | tf_op jit(solution)/shard_map/ppermute | solution.py:25
  37.4 16.4 %copy-start.74 = (f32[1,32,32]{2,1,0:T(8,128)}, f32[1,32,32]{2,1,0:T(8,128)S(1)}, u32[]{:S(2)}) copy-start(f32[1,32,32]{2,1,0:T(8,128)S(1)} %reshape.556) | copy-start | bytes 12292
  38.2 14.4 %copy-start.76 = (f32[1,32,32]{2,1,0:T(8,128)}, f32[1,32,32]{2,1,0:T(8,128)S(1)}, u32[]{:S(2)}) copy-start(f32[1,32,32]{2,1,0:T(8,128)S(1)} %reshape.555) | copy-start | bytes 12292
  38.3 12.2 %copy-start.78 = (f32[1,32,32]{2,1,0:T(8,128)}, f32[1,32,32]{2,1,0:T(8,128)S(1)}, u32[]{:S(2)}) copy-start(f32[1,32,32]{2,1,0:T(8,128)S(1)} %reshape.553) | copy-start | bytes 12292
  39.9 6.8 %collective-permute-start.6 = (f32[10240]{0:T(1024)}, f32[10240]{0:T(1024)S(1)}, u32[]{:S(2)}, u32[]{:S(2)}) collective-permute-start(f32[10240]{0:T(1024)} %get-tuple-element.94), channel_id=1, source_target_pairs={{0,3},{1,4},{2,5},{3,6},{4,7},{5,8},{6,9},{7,10},{8,11},{9,12},{10... | collective-permute-start | bytes 122888 | tf_op jit(solution)/shard_map/ppermute | solution.py:25
  39.9 6.9 %collective-permute-start.7 = (f32[10240]{0:T(1024)}, f32[10240]{0:T(1024)S(1)}, u32[]{:S(2)}, u32[]{:S(2)}) collective-permute-start(f32[10240]{0:T(1024)} %get-tuple-element.93), channel_id=1, source_target_pairs={{0,125},{1,126},{2,127},{3,0},{4,1},{5,2},{6,3},{7,4},{8,5},{9,6},... | collective-permute-start | bytes 122888 | tf_op jit(solution)/shard_map/ppermute | solution.py:25
  47.0 29.5 %copy-start.9 = (f32[8,64,64]{2,1,0:T(8,128)}, f32[8,64,64]{2,1,0:T(8,128)S(1)}, u32[]{:S(2)}) copy-start(f32[8,64,64]{2,1,0:T(8,128)S(1)} %broadcast_multiply_fusion.3) | copy-start | bytes 393220
  51.3 26.8 %copy-start.68 = (f32[3,32,32]{2,1,0:T(8,128)}, f32[3,32,32]{2,1,0:T(8,128)S(1)}, u32[]{:S(2)}) copy-start(f32[3,32,32]{2,1,0:T(8,128)S(1)} %reshape.559) | copy-start | bytes 36868
  54.5 23.6 %copy-start.70 = (f32[3,32,32]{2,1,0:T(8,128)}, f32[3,32,32]{2,1,0:T(8,128)S(1)}, u32[]{:S(2)}) copy-start(f32[3,32,32]{2,1,0:T(8,128)S(1)} %reshape.561) | copy-start | bytes 36868
  55.1 18.6 %collective-permute-start.8 = (f32[18,32,32]{2,1,0:T(8,128)}, f32[18,32,32]{2,1,0:T(8,128)S(1)}, u32[]{:S(2)}, u32[]{:S(2)}) collective-permute-start(f32[18,32,32]{2,1,0:T(8,128)} %constant_dynamic-update-slice_fusion.2), channel_id=1, source_target_pairs={{0,9},{1,10},{2,11},{3,12},{4,13},{5,14},{6,15},{7,16},{8,17},{9,1... | collective-permute-start | bytes 221192 | tf_op jit(solution)/shard_map/ppermute | solution.py:25
  71.4 154.9 %collective-permute-start.9 = (f32[18,32,32]{2,1,0:T(8,128)}, f32[18,32,32]{2,1,0:T(8,128)}, u32[]{:S(2)}, u32[]{:S(2)}) collective-permute-start(f32[18,32,32]{2,1,0:T(8,128)} %constant_dynamic-update-slice_fusion.2), channel_id=1, source_target_pairs={{0,119},{1,120},{2,121},{3,122},{4,123},{5,124},{6,125},{7,126},{8... | collective-permute-start | bytes 221192 | tf_op jit(solution)/shard_map/ppermute | solution.py:25
  138.7 11.8 %copy-start.69 = (f32[3,32,32]{2,1,0:T(8,128)S(1)}, f32[3,32,32]{2,1,0:T(8,128)}, u32[]{:S(2)}) copy-start(f32[3,32,32]{2,1,0:T(8,128)} %copy-done.68) | copy-start | bytes 36868
  138.8 12.4 %copy-start.71 = (f32[3,32,32]{2,1,0:T(8,128)S(1)}, f32[3,32,32]{2,1,0:T(8,128)}, u32[]{:S(2)}) copy-start(f32[3,32,32]{2,1,0:T(8,128)} %copy-done.70) | copy-start | bytes 36868
  138.8 18.2 %copy-start = (f32[8,256,256]{2,1,0:T(8,128)S(1)}, f32[8,256,256]{2,1,0:T(8,128)}, u32[]{:S(2)}) copy-start(f32[8,256,256]{2,1,0:T(8,128)} %shard_map.41) | copy-start | bytes 6291460
  140.4 15.4 %collective-permute-start.3 = (f32[3,256,256]{2,1,0:T(8,128)S(1)}, f32[3,256,256]{2,1,0:T(8,128)S(1)}, u32[]{:S(2)}, u32[]{:S(2)}) collective-permute-start(f32[3,256,256]{2,1,0:T(8,128)S(1)} %get-tuple-element.39), channel_id=1, source_target_pairs={{1,0},{2,1},{3,2},{4,3},{5,4},{6,5},{7,6},{8,7},{9,8},{10,9},{11,1... | collective-permute-start | bytes 2359304 | tf_op jit(solution)/shard_map/ppermute | solution.py:25
  142.3 14.7 %collective-permute-start.2 = (f32[3,256,256]{2,1,0:T(8,128)S(1)}, f32[3,256,256]{2,1,0:T(8,128)S(1)}, u32[]{:S(2)}, u32[]{:S(2)}) collective-permute-start(f32[3,256,256]{2,1,0:T(8,128)S(1)} %get-tuple-element.38), channel_id=1, source_target_pairs={{0,1},{1,2},{2,3},{3,4},{4,5},{5,6},{6,7},{7,8},{8,9},{9,10},{10,1... | collective-permute-start | bytes 2359304 | tf_op jit(solution)/shard_map/ppermute | solution.py:25
  219.2 12.8 %copy-start.10 = (f32[8,64,64]{2,1,0:T(8,128)S(1)}, f32[8,64,64]{2,1,0:T(8,128)}, u32[]{:S(2)}) copy-start(f32[8,64,64]{2,1,0:T(8,128)} %copy-done.9) | copy-start | bytes 393220
  219.2 12.8 %copy-start.22 = (f32[6,64,64]{2,1,0:T(8,128)S(1)}, f32[6,64,64]{2,1,0:T(8,128)}, u32[]{:S(2)}) copy-start(f32[6,64,64]{2,1,0:T(8,128)} %copy-done.21) | copy-start | bytes 294916
  219.2 12.8 %copy-start.51 = (f32[6,66,1]{2,1,0:T(8,128)S(1)}, f32[6,66,1]{2,1,0:T(8,128)}, u32[]{:S(2)}) copy-start(f32[6,66,1]{2,1,0:T(8,128)} %get-tuple-element.72) | copy-start | bytes 4756
  219.2 12.8 %copy-start.52 = (f32[6,66,1]{2,1,0:T(8,128)S(1)}, f32[6,66,1]{2,1,0:T(8,128)}, u32[]{:S(2)}) copy-start(f32[6,66,1]{2,1,0:T(8,128)} %get-tuple-element.73) | copy-start | bytes 4756
  219.2 12.8 %copy-start.92 = (f32[6,1,64]{2,1,0:T(1,128)S(1)}, f32[6,1,64]{2,1,0:T(1,128)}, u32[]{:S(2)}) copy-start(f32[6,1,64]{2,1,0:T(1,128)} %copy-done.91) | copy-start | bytes 4612
  219.2 12.8 %copy-start.94 = (f32[6,1,64]{2,1,0:T(1,128)S(1)}, f32[6,1,64]{2,1,0:T(1,128)}, u32[]{:S(2)}) copy-start(f32[6,1,64]{2,1,0:T(1,128)} %copy-done.93) | copy-start | bytes 4612
  219.2 12.8 %copy-start.98 = (f32[6]{0:T(128)S(1)}, f32[6]{0:T(128)}, u32[]{:S(2)}) copy-start(f32[6]{0:T(128)} %and_convert_fusion.2) | copy-start | bytes 76
  219.9 12.6 %copy-start.61 = (f32[2,64,64]{2,1,0:T(8,128)S(1)}, f32[2,64,64]{2,1,0:T(8,128)}, u32[]{:S(2)}) copy-start(f32[2,64,64]{2,1,0:T(8,128)} %copy-done.60) | copy-start | bytes 98308
  219.9 12.6 %copy-start.80 = (f32[2,64,64]{2,1,0:T(8,128)S(1)}, f32[2,64,64]{2,1,0:T(8,128)}, u32[]{:S(2)}) copy-start(f32[2,64,64]{2,1,0:T(8,128)} %reshape.572) | copy-start | bytes 98308
  219.9 12.6 %copy-start.81 = (f32[2,64,64]{2,1,0:T(8,128)S(1)}, f32[2,64,64]{2,1,0:T(8,128)}, u32[]{:S(2)}) copy-start(f32[2,64,64]{2,1,0:T(8,128)} %reshape.571) | copy-start | bytes 98308
  221.5 8.2 %collective-permute-start.11 = (f32[41984]{0:T(1024)S(1)}, f32[41984]{0:T(1024)S(1)}, u32[]{:S(2)}, u32[]{:S(2)}) collective-permute-start(f32[41984]{0:T(1024)S(1)} %get-tuple-element.88), channel_id=1, source_target_pairs={{0,127},{1,0},{2,1},{3,2},{4,3},{5,4},{6,5},{7,6},{8,7},{9,8},{10,... | collective-permute-start | bytes 503816 | tf_op jit(solution)/shard_map/ppermute | solution.py:25
  221.6 8.2 %collective-permute-start.10 = (f32[41984]{0:T(1024)S(1)}, f32[41984]{0:T(1024)S(1)}, u32[]{:S(2)}, u32[]{:S(2)}) collective-permute-start(f32[41984]{0:T(1024)S(1)} %get-tuple-element.87), channel_id=1, source_target_pairs={{0,1},{1,2},{2,3},{3,4},{4,5},{5,6},{6,7},{7,8},{8,9},{9,10},{10,1... | collective-permute-start | bytes 503816 | tf_op jit(solution)/shard_map/ppermute | solution.py:25
  229.9 8.7 %collective-permute-start.12 = (f32[3,32,32]{2,1,0:T(8,128)S(1)}, f32[3,32,32]{2,1,0:T(8,128)S(1)}, u32[]{:S(2)}, u32[]{:S(2)}) collective-permute-start(f32[3,32,32]{2,1,0:T(8,128)S(1)} %pad_maximum_fusion.53), channel_id=1, source_target_pairs={{0,3},{1,4},{2,5},{3,6},{4,7},{5,8},{6,9},{7,10},{8,11},{9,12},{10... | collective-permute-start | bytes 36872 | tf_op jit(solution)/shard_map/ppermute | solution.py:25
  231.0 7.8 %collective-permute-start.13 = (f32[3,32,32]{2,1,0:T(8,128)S(1)}, f32[3,32,32]{2,1,0:T(8,128)S(1)}, u32[]{:S(2)}, u32[]{:S(2)}) collective-permute-start(f32[3,32,32]{2,1,0:T(8,128)S(1)} %pad_maximum_fusion.53), channel_id=1, source_target_pairs={{0,125},{1,126},{2,127},{3,0},{4,1},{5,2},{6,3},{7,4},{8,5},{9,6},... | collective-permute-start | bytes 36872 | tf_op jit(solution)/shard_map/ppermute | solution.py:25
  232.4 22.1 %copy-start.19 = (f32[6,64,64]{2,1,0:T(8,128)}, f32[6,64,64]{2,1,0:T(8,128)S(1)}, u32[]{:S(2)}) copy-start(f32[6,64,64]{2,1,0:T(8,128)S(1)} %get-tuple-element.21) | copy-start | bytes 294916
  232.4 22.1 %copy-start.38 = (f32[6,64,64]{2,1,0:T(8,128)}, f32[6,64,64]{2,1,0:T(8,128)S(1)}, u32[]{:S(2)}) copy-start(f32[6,64,64]{2,1,0:T(8,128)S(1)} %get-tuple-element.22) | copy-start | bytes 294916
  232.4 22.0 %copy-start.40 = (f32[6,64,64]{2,1,0:T(8,128)}, f32[6,64,64]{2,1,0:T(8,128)S(1)}, u32[]{:S(2)}) copy-start(f32[6,64,64]{2,1,0:T(8,128)S(1)} %get-tuple-element.23) | copy-start | bytes 294916
  232.4 22.0 %copy-start.54 = (f32[6,64,64]{2,1,0:T(8,128)}, f32[6,64,64]{2,1,0:T(8,128)S(1)}, u32[]{:S(2)}) copy-start(f32[6,64,64]{2,1,0:T(8,128)S(1)} %get-tuple-element.20) | copy-start | bytes 294916
  237.2 17.5 %copy-start.35 = (f32[6,128,128]{2,1,0:T(8,128)}, f32[6,128,128]{2,1,0:T(8,128)S(1)}, u32[]{:S(2)}) copy-start(f32[6,128,128]{2,1,0:T(8,128)S(1)} %fusion.50) | copy-start | bytes 1179652
  237.6 27.3 %copy-start.33 = (f32[6,128,128]{2,1,0:T(8,128)}, f32[6,128,128]{2,1,0:T(8,128)S(1)}, u32[]{:S(2)}) copy-start(f32[6,128,128]{2,1,0:T(8,128)S(1)} %fusion.61) | copy-start | bytes 1179652
  237.7 26.2 %copy-start.57 = (f32[27,32,32]{2,1,0:T(8,128)S(1)}, f32[27,32,32]{2,1,0:T(8,128)}, u32[]{:S(2)}) copy-start(f32[27,32,32]{2,1,0:T(8,128)} %get-tuple-element.61) | copy-start | bytes 331780
  237.7 26.2 %copy-start.59 = (f32[27,32,32]{2,1,0:T(8,128)S(1)}, f32[27,32,32]{2,1,0:T(8,128)}, u32[]{:S(2)}) copy-start(f32[27,32,32]{2,1,0:T(8,128)} %get-tuple-element.60) | copy-start | bytes 331780
  237.7 26.2 %copy-start.99 = (f32[27]{0:T(128)S(1)}, f32[27]{0:T(128)}, u32[]{:S(2)}) copy-start(f32[27]{0:T(128)} %and_convert_fusion.4) | copy-start | bytes 328
  238.7 26.3 %copy-start.64 = (f32[4,64,64]{2,1,0:T(8,128)}, f32[4,64,64]{2,1,0:T(8,128)S(1)}, u32[]{:S(2)}) copy-start(f32[4,64,64]{2,1,0:T(8,128)S(1)} %fusion.154) | copy-start | bytes 196612
  238.8 17.8 %collective-permute-start.14 = (f32[9,32,32]{2,1,0:T(8,128)S(1)}, f32[9,32,32]{2,1,0:T(8,128)S(1)}, u32[]{:S(2)}, u32[]{:S(2)}) collective-permute-start(f32[9,32,32]{2,1,0:T(8,128)S(1)} %constant_dynamic-update-slice_fusion.27), channel_id=1, source_target_pairs={{0,9},{1,10},{2,11},{3,12},{4,13},{5,14},{6,15},{7,16},{8,17},{9,1... | collective-permute-start | bytes 110600 | tf_op jit(solution)/shard_map/ppermute | solution.py:25
  254.6 11.9 %copy-start.62 = (f32[4,64,64]{2,1,0:T(8,128)}, f32[4,64,64]{2,1,0:T(8,128)S(1)}, u32[]{:S(2)}) copy-start(f32[4,64,64]{2,1,0:T(8,128)S(1)} %fusion.165) | copy-start | bytes 196612
  254.6 12.9 %copy-start.90 = (s32[32]{0:T(128)S(1)}, s32[32]{0:T(128)}, u32[]{:S(2)}) copy-start(s32[32]{0:T(128)} %and_select_fusion) | copy-start | bytes 388
  254.7 9.1 %collective-permute-start.15 = (f32[9,32,32]{2,1,0:T(8,128)S(1)}, f32[9,32,32]{2,1,0:T(8,128)S(1)}, u32[]{:S(2)}, u32[]{:S(2)}) collective-permute-start(f32[9,32,32]{2,1,0:T(8,128)S(1)} %constant_dynamic-update-slice_fusion.27), channel_id=1, source_target_pairs={{0,119},{1,120},{2,121},{3,122},{4,123},{5,124},{6,125},{7,126},{8... | collective-permute-start | bytes 110600 | tf_op jit(solution)/shard_map/ppermute | solution.py:25
  (73 other events, 384.4 us)
where the time goes:
time: 311 us; the launch traced here: 309 us
  Pallas kernels  93.2 us (30%)
  other arithmetic  59.1 us (19%)
  starting transfers between devices  57.9 us (19%)
  local copies, waits for them, and re-layouts  54.9 us (18%)
  waiting for transfers between devices  21.8 us (7%)
  matrix products  19.3 us (6%)
    pallas_call x2, Pallas kernels, _vmem_call(): pl.pallas_call(kernel, out_shape=outs, in_specs=[pl.BlockSpec(memory_spac...  93.2 us
    ppermute x16, starting transfers between devices, recv(): return lax.ppermute(value, 'gx', pairs)  57.9 us
    ppermute x16, waiting for transfers between devices, recv(): return lax.ppermute(value, 'gx', pairs)  21.8 us
    unnamed x239, local copies, waits for them, and re-layouts  21.3 us
    select_n x1, other arithmetic, fine_coefs(): jnp.where(zs == extent_z - 1, 0.0, co['kzh'])  9.2 us
    mul x8, other arithmetic, smooth(): update = co['w'] * resid  7.6 us
    dot_general x12, matrix products, shrink_sides(): jnp.einsum('xyz,zw->xyw', field, pair_matrix(extent_z), precision=EXACT)  7.46 us
    reduce_sum x7, other arithmetic, coarsen(): planes = field.reshape(extent_x // 2, 2, extent_y, extent_z).sum(axis=1)  7.36 us
  transfers between devices with their start and end apart: 16, of which 7 were waited for; matrix products, arithmetic and copies ran while one was open for 25% of the time, Pallas kernels for 30%

commit v1 on v0

--- a/solution.py
+++ b/solution.py
@@ -147,7 +147,7 @@
     return update
 
 
-ROWS = 16
+ROWS = 64
 PAD = 8
 VMEM_LIMIT = 64 * 1024 * 1024
 
@@ -165,22 +165,19 @@
 
 
 def _plane_loop(first, last, extent_y, body):
-    chunks = extent_y // ROWS
-
     def step(i, carry):
-        q = first + i // chunks
-        y0 = pl.multiple_of((i % chunks) * ROWS, ROWS)
-        body(q, y0)
+        for y0 in range(0, extent_y, ROWS):
+            body(first + i, y0)
         return carry
 
-    lax.fori_loop(0, (last - first) * chunks, step, 0)
+    lax.fori_loop(0, last - first, step, 0)
 
 
 def _neighbour_sum(src, at, y0, kxo_lo, kxo_hi, kyl, kyh, kzl, kzh):
     extent_z = src.shape[2]
     center = src[at, pl.ds(PAD + y0, ROWS), :]
-    below = pltpu.roll(src[at, pl.ds(y0, ROWS + PAD), :], 1, 0)[PAD:PAD + ROWS]
-    above = pltpu.roll(src[at, pl.ds(PAD + y0, ROWS + PAD), :], ROWS + PAD - 1, 0)[:ROWS]
+    below = src[at, pl.ds(PAD + y0 - 1, ROWS), :]
+    above = src[at, pl.ds(PAD + y0 + 1, ROWS), :]
     left = pltpu.roll(center, 1, 1)
     right = pltpu.roll(center, extent_z - 1, 1)
     off = (

time: 311 us -> 250 us (0.80)
  Pallas kernels: 93.2 us -> 32.9 us
    pallas_call x2, Pallas kernels: 93.2 us -> 32.9 us  [_vmem_call(): pl.pallas_call(kernel, out_shape=outs, in_specs=[pl.BlockSpec(memory_spac...]
  transfers between devices with their start and end apart: 16 -> 16, of which waited for: 7 -> 7; matrix products, arithmetic and copies ran while one was open for 25% -> 32% of each run, Pallas kernels for 30% -> 13%
where the time goes in v1:
time: 250 us; the launch traced here: 249 us
  other arithmetic  59.1 us (24%)
  starting transfers between devices  57.9 us (23%)
  local copies, waits for them, and re-layouts  54.9 us (22%)
  Pallas kernels  32.9 us (13%)
  waiting for transfers between devices  21.8 us (9%)
  matrix products  19.3 us (8%)
  between operations  2.87 us (1%)
    ppermute x16, starting transfers between devices, recv(): return lax.ppermute(value, 'gx', pairs)  57.9 us
    pallas_call x2, Pallas kernels, _vmem_call(): pl.pallas_call(kernel, out_shape=outs, in_specs=[pl.BlockSpec(memory_spac...  32.9 us
    ppermute x16, waiting for transfers between devices, recv(): return lax.ppermute(value, 'gx', pairs)  21.8 us
    unnamed x239, local copies, waits for them, and re-layouts  21.3 us
    select_n x1, other arithmetic, fine_coefs(): jnp.where(zs == extent_z - 1, 0.0, co['kzh'])  9.2 us
    mul x8, other arithmetic, smooth(): update = co['w'] * resid  7.6 us
    dot_general x12, matrix products, shrink_sides(): jnp.einsum('xyz,zw->xyw', field, pair_matrix(extent_z), precision=EXACT)  7.46 us
    reduce_sum x7, other arithmetic, coarsen(): planes = field.reshape(extent_x // 2, 2, extent_y, extent_z).sum(axis=1)  7.36 us
  transfers between devices with their start and end apart: 16, of which 7 were waited for; matrix products, arithmetic and copies ran while one was open for 32% of the time, Pallas kernels for 13%

profile of v1, /device:TPU:117, one launch (start us, length us, event | category | flops | bytes accessed | tf_op | source)
XLA Modules:
  0.0 248.7 jit_solution(1880370729570266620)
XLA Ops:
  0.6 1.4 fusion.596
  3.8 2.6 %collective-permute-start.1 = (f32[5,256,256]{2,1,0:T(8,128)}, f32[5,256,256]{2,1,0:T(8,128)}, u32[]{:S(2)}, u32[]{:S(2)}) collective-permute-start(f32[5,256,256]{2,1,0:T(8,128)} %pad_maximum_fusion.13), channel_id=1, source_target_pairs={{1,0},{2,1},{3,2},{4,3},{5,4},{6,5},{7,6},{8,7},{9,8},{10,9},{11,1... | collective-permute-start | bytes 3932168 | tf_op jit(solution)/shard_map/ppermute | solution.py:25
  7.5 5.1 %collective-permute-start = (f32[5,256,256]{2,1,0:T(8,128)}, f32[5,256,256]{2,1,0:T(8,128)}, u32[]{:S(2)}, u32[]{:S(2)}) collective-permute-start(f32[5,256,256]{2,1,0:T(8,128)} %pad_maximum_fusion.12), channel_id=1, source_target_pairs={{0,1},{1,2},{2,3},{3,4},{4,5},{5,6},{6,7},{7,8},{8,9},{9,10},{10,1... | collective-permute-start | bytes 3932168 | tf_op jit(solution)/shard_map/ppermute | solution.py:25
  24.1 3.9 %collective-permute-start.4 = (f32[100352]{0:T(1024)}, f32[100352]{0:T(1024)}, u32[]{:S(2)}, u32[]{:S(2)}) collective-permute-start(f32[100352]{0:T(1024)} %get-tuple-element.95), channel_id=1, source_target_pairs={{0,1},{1,2},{2,3},{3,4},{4,5},{5,6},{6,7},{7,8},{8,9},{9,10},{10,1... | collective-permute-start | bytes 1204232 | tf_op jit(solution)/shard_map/ppermute | solution.py:25
  30.3 3.4 %collective-permute-done.5 = f32[100352]{0:T(1024)S(1)} collective-permute-done((f32[100352]{0:T(1024)}, f32[100352]{0:T(1024)S(1)}, u32[]{:S(2)}, u32[]{:S(2)}) %collective-permute-start.5) | collective-permute-done | bytes 401440 | tf_op jit(solution)/shard_map/ppermute | solution.py:25
  35.1 1.3 fusion.34
  39.9 1.7 collective-permute-start.7
  41.6 1.2 fusion.598
  45.1 1.6 slice.1920
  55.1 14.7 %collective-permute-start.8 = (f32[18,32,32]{2,1,0:T(8,128)}, f32[18,32,32]{2,1,0:T(8,128)S(1)}, u32[]{:S(2)}, u32[]{:S(2)}) collective-permute-start(f32[18,32,32]{2,1,0:T(8,128)} %constant_dynamic-update-slice_fusion.2), channel_id=1, source_target_pairs={{0,9},{1,10},{2,11},{3,12},{4,13},{5,14},{6,15},{7,16},{8,17},{9,1... | collective-permute-start | bytes 221192 | tf_op jit(solution)/shard_map/ppermute | solution.py:25
  71.4 2.4 collective-permute-done.8
  75.4 1.2 slice.1750
  76.6 1.2 slice.1749
  79.2 1.4 copy-done.3
  80.5 1.8 slice.1753.kxo
  83.2 1.2 slice.1748
  85.5 1.8 pad_maximum_fusion.11.resid.rhs
  87.3 7.1 %broadcast_divide_fusion = (f32[12,256,256]{2,1,0:T(8,128)}, f32[12,256,256]{2,1,0:T(8,128)}) fusion(f32[12,258,1]{2,1,0:T(8,128)S(1)} %get-tuple-element.32, f32[12,1,256]{2,1,0:T(1,128)S(1)} %get-tuple-element.30, f32[12,256,256]{2,1,0:T(8,128)S(1)} %slice.1754, f32[12,1,256]{2,1,0:T(1,128)S(1)} %get-tuple-element.31, ...), kind=kLoop, calls=%fused_computation.41 | loop fusion | flops 31457280 | bytes 15777984 | tf_op jit(solution)/shard_map/div | solution.py:119
  94.4 9.2 %broadcast_select_fusion = (f32[12,256,256]{2,1,0:T(8,128)}, f32[12,256,256]{2,1,0:T(8,128)}, f32[12,256,256]{2,1,0:T(8,128)}, f32[12,256,256]{2,1,0:T(8,128)}) fusion(pred[256]{0:T(512)(128)(4,1)S(1)} %get-tuple-element.112, f32[12,258,1]{2,1,0:T(8,128)S(1)} %get-tuple-element.32, f32[12,1,256]{2,1,0:T(1,128)S(1)} %get-tuple-element.30, ...), kind=kLoop, calls=%fused_computation.42 | loop fusion | flops 23592960 | bytes 15778496 | tf_op jit(solution)/shard_map/jit(_where)/select_n | solution.py:285
  103.6 13.4 %shard_map.41 = f32[8,256,256]{2,1,0:T(8,128)} custom-call(f32[12,256,256]{2,1,0:T(8,128)} %pad_maximum_fusion.11.resid.rhs, f32[11,256,256]{2,1,0:T(8,128)} %slice.1753.kxo, f32[12,256,256]{2,1,0:T(8,128)} %get-tuple-element.36.kyl, f32[12,256,256]{2,1,0:T(8,128)} %get-tuple-element.37.kyh, f32[12,256,256]{2,1,0:T(8,128)} %get-tuple-element.35.kzl, ...), custom_call_target="tpu_custom_call" | custom-call | tf_op jit(solution)/shard_map/pallas_call | solution.py:263
  117.1 1.6 fusion.594
  118.7 1.9 collective-permute-start.3
  120.6 5.8 %collective-permute-start.2 = (f32[3,256,256]{2,1,0:T(8,128)S(1)}, f32[3,256,256]{2,1,0:T(8,128)S(1)}, u32[]{:S(2)}, u32[]{:S(2)}) collective-permute-start(f32[3,256,256]{2,1,0:T(8,128)S(1)} %get-tuple-element.38), channel_id=1, source_target_pairs={{0,1},{1,2},{2,3},{3,4},{4,5},{5,6},{6,7},{7,8},{8,9},{9,10},{10,1... | collective-permute-start | bytes 2359304 | tf_op jit(solution)/shard_map/ppermute | solution.py:25
  130.1 4.1 %collective-permute-done.3 = f32[3,256,256]{2,1,0:T(8,128)S(1)} collective-permute-done((f32[3,256,256]{2,1,0:T(8,128)S(1)}, f32[3,256,256]{2,1,0:T(8,128)S(1)}, u32[]{:S(2)}, u32[]{:S(2)}) %collective-permute-start.3) | collective-permute-done | bytes 786464 | tf_op jit(solution)/shard_map/ppermute | solution.py:25
  134.1 1.2 collective-permute-done.2
  135.3 2.1 pad_maximum_fusion.1.fine_ext
  137.4 19.4 %shard_map.42 = (f32[8,256,256]{2,1,0:T(8,128)}, f32[8,256,256]{2,1,0:T(8,128)}) custom-call(f32[14,256,256]{2,1,0:T(8,128)} %pad_maximum_fusion.1.fine_ext, f32[12,256,256]{2,1,0:T(8,128)} %pad_maximum_fusion.11.resid.rhs, f32[13,256,256]{2,1,0:T(8,128)} %copy-done.3, f32[12,256,256]{2,1,0:T(8,128)} %get-tuple-element.36.kyl, ...), custom_call_target="tpu_custom_call" | custom-call | tf_op jit(solution)/shard_map/pallas_call | solution.py:263
  156.9 1.9 bitcast_reduce_fusion
  161.2 4.7 %collective-permute-start.10 = (f32[41984]{0:T(1024)S(1)}, f32[41984]{0:T(1024)S(1)}, u32[]{:S(2)}, u32[]{:S(2)}) collective-permute-start(f32[41984]{0:T(1024)S(1)} %get-tuple-element.87), channel_id=1, source_target_pairs={{0,1},{1,2},{2,3},{3,4},{4,5},{5,6},{6,7},{7,8},{8,9},{9,10},{10,1... | collective-permute-start | bytes 503816 | tf_op jit(solution)/shard_map/ppermute | solution.py:25
  165.9 1.7 slice_dynamic-update-slice_fusion
  167.6 1.8 collective-permute-done.11
  172.3 2.3 fusion.576
  178.4 15.7 %collective-permute-start.14 = (f32[9,32,32]{2,1,0:T(8,128)S(1)}, f32[9,32,32]{2,1,0:T(8,128)S(1)}, u32[]{:S(2)}, u32[]{:S(2)}) collective-permute-start(f32[9,32,32]{2,1,0:T(8,128)S(1)} %constant_dynamic-update-slice_fusion.27), channel_id=1, source_target_pairs={{0,9},{1,10},{2,11},{3,12},{4,13},{5,14},{6,15},{7,16},{8,17},{9,1... | collective-permute-start | bytes 110600 | tf_op jit(solution)/shard_map/ppermute | solution.py:25
  194.4 1.8 collective-permute-done.14
  196.3 7.2 %collective-permute-done.15 = f32[9,32,32]{2,1,0:T(8,128)S(1)} collective-permute-done((f32[9,32,32]{2,1,0:T(8,128)S(1)}, f32[9,32,32]{2,1,0:T(8,128)S(1)}, u32[]{:S(2)}, u32[]{:S(2)}) %collective-permute-start.15) | collective-permute-done | bytes 36896 | tf_op jit(solution)/shard_map/ppermute | solution.py:25
  210.1 1.5 slice.1842
  211.7 1.6 divide_select_fusion.3
  213.3 1.8 constant_dynamic-slice_fusion
  215.1 1.8 reduce_sum.119
  216.8 1.4 fusion.530
  218.5 1.9 fusion.196
  220.4 2.6 %slice_multiply_fusion.14 = (f32[11,16,16]{1,2,0:T(8,128)}, f32[11,16,16]{1,2,0:T(8,128)S(1)}, f32[11,16,16]{1,2,0:T(8,128)}, f32[11,16,16]{1,2,0:T(8,128)}) fusion(f32[13,16,16]{1,2,0:T(8,128)S(1)} %fusion.17, f32[11,1,16]{1,2,0:T(8,128)} %get-tuple-element.77, f32[11,16,16]{1,2,0:T(8,128)} %slice.1777, f32[11,1,16]{1,2,0:T(8,128)} %copy-done.53, ...), kind=kLoop, calls=%fused_computation.356 | loop fusion | flops 160512 | bytes 102784 | tf_op jit(solution)/shard_map/mul | solution.py:137
  223.0 1.8 constant_dynamic-slice_fusion.1
  224.8 1.8 reduce_sum.115
  226.6 1.5 fusion.533
  228.5 1.3 fusion.236
  245.6 1.7 bitcast_add_fusion
  247.2 1.5 broadcast_in_dim.85
  (447 shorter events, 73.2 us)
Async XLA Ops:
  3.8 71.6 %collective-permute-start.1 = (f32[5,256,256]{2,1,0:T(8,128)}, f32[5,256,256]{2,1,0:T(8,128)}, u32[]{:S(2)}, u32[]{:S(2)}) collective-permute-start(f32[5,256,256]{2,1,0:T(8,128)} %pad_maximum_fusion.13), channel_id=1, source_target_pairs={{1,0},{2,1},{3,2},{4,3},{5,4},{6,5},{7,6},{8,7},{9,8},{10,9},{11,1... | collective-permute-start | bytes 3932168 | tf_op jit(solution)/shard_map/ppermute | solution.py:25
  7.5 69.0 %collective-permute-start = (f32[5,256,256]{2,1,0:T(8,128)}, f32[5,256,256]{2,1,0:T(8,128)}, u32[]{:S(2)}, u32[]{:S(2)}) collective-permute-start(f32[5,256,256]{2,1,0:T(8,128)} %pad_maximum_fusion.12), channel_id=1, source_target_pairs={{0,1},{1,2},{2,3},{3,4},{4,5},{5,6},{6,7},{7,8},{8,9},{9,10},{10,1... | collective-permute-start | bytes 3932168 | tf_op jit(solution)/shard_map/ppermute | solution.py:25
  19.5 33.7 %copy-start.72 = (f32[32,32]{1,0:T(8,128)}, f32[32,32]{1,0:T(8,128)S(1)}, u32[]{:S(2)}) copy-start(f32[32,32]{1,0:T(8,128)S(1)} %convolution_multiply_fusion.8) | copy-start | bytes 12292
  24.1 9.6 %collective-permute-start.5 = (f32[100352]{0:T(1024)}, f32[100352]{0:T(1024)S(1)}, u32[]{:S(2)}, u32[]{:S(2)}) collective-permute-start(f32[100352]{0:T(1024)} %get-tuple-element.96), channel_id=1, source_target_pairs={{0,127},{1,0},{2,1},{3,2},{4,3},{5,4},{6,5},{7,6},{8,7},{9,8},{10,... | collective-permute-start | bytes 1204232 | tf_op jit(solution)/shard_map/ppermute | solution.py:25
  24.1 9.6 %collective-permute-start.4 = (f32[100352]{0:T(1024)}, f32[100352]{0:T(1024)}, u32[]{:S(2)}, u32[]{:S(2)}) collective-permute-start(f32[100352]{0:T(1024)} %get-tuple-element.95), channel_id=1, source_target_pairs={{0,1},{1,2},{2,3},{3,4},{4,5},{5,6},{6,7},{7,8},{8,9},{9,10},{10,1... | collective-permute-start | bytes 1204232 | tf_op jit(solution)/shard_map/ppermute | solution.py:25
  37.4 16.4 %copy-start.74 = (f32[1,32,32]{2,1,0:T(8,128)}, f32[1,32,32]{2,1,0:T(8,128)S(1)}, u32[]{:S(2)}) copy-start(f32[1,32,32]{2,1,0:T(8,128)S(1)} %reshape.556) | copy-start | bytes 12292
  38.2 14.4 %copy-start.76 = (f32[1,32,32]{2,1,0:T(8,128)}, f32[1,32,32]{2,1,0:T(8,128)S(1)}, u32[]{:S(2)}) copy-start(f32[1,32,32]{2,1,0:T(8,128)S(1)} %reshape.555) | copy-start | bytes 12292
  38.3 12.2 %copy-start.78 = (f32[1,32,32]{2,1,0:T(8,128)}, f32[1,32,32]{2,1,0:T(8,128)S(1)}, u32[]{:S(2)}) copy-start(f32[1,32,32]{2,1,0:T(8,128)S(1)} %reshape.553) | copy-start | bytes 12292
  39.9 6.8 %collective-permute-start.6 = (f32[10240]{0:T(1024)}, f32[10240]{0:T(1024)S(1)}, u32[]{:S(2)}, u32[]{:S(2)}) collective-permute-start(f32[10240]{0:T(1024)} %get-tuple-element.94), channel_id=1, source_target_pairs={{0,3},{1,4},{2,5},{3,6},{4,7},{5,8},{6,9},{7,10},{8,11},{9,12},{10... | collective-permute-start | bytes 122888 | tf_op jit(solution)/shard_map/ppermute | solution.py:25
  39.9 6.9 %collective-permute-start.7 = (f32[10240]{0:T(1024)}, f32[10240]{0:T(1024)S(1)}, u32[]{:S(2)}, u32[]{:S(2)}) collective-permute-start(f32[10240]{0:T(1024)} %get-tuple-element.93), channel_id=1, source_target_pairs={{0,125},{1,126},{2,127},{3,0},{4,1},{5,2},{6,3},{7,4},{8,5},{9,6},... | collective-permute-start | bytes 122888 | tf_op jit(solution)/shard_map/ppermute | solution.py:25
  47.0 29.5 %copy-start.9 = (f32[8,64,64]{2,1,0:T(8,128)}, f32[8,64,64]{2,1,0:T(8,128)S(1)}, u32[]{:S(2)}) copy-start(f32[8,64,64]{2,1,0:T(8,128)S(1)} %broadcast_multiply_fusion.3) | copy-start | bytes 393220
  51.3 26.8 %copy-start.68 = (f32[3,32,32]{2,1,0:T(8,128)}, f32[3,32,32]{2,1,0:T(8,128)S(1)}, u32[]{:S(2)}) copy-start(f32[3,32,32]{2,1,0:T(8,128)S(1)} %reshape.559) | copy-start | bytes 36868
  54.5 23.6 %copy-start.70 = (f32[3,32,32]{2,1,0:T(8,128)}, f32[3,32,32]{2,1,0:T(8,128)S(1)}, u32[]{:S(2)}) copy-start(f32[3,32,32]{2,1,0:T(8,128)S(1)} %reshape.561) | copy-start | bytes 36868
  55.1 18.6 %collective-permute-start.8 = (f32[18,32,32]{2,1,0:T(8,128)}, f32[18,32,32]{2,1,0:T(8,128)S(1)}, u32[]{:S(2)}, u32[]{:S(2)}) collective-permute-start(f32[18,32,32]{2,1,0:T(8,128)} %constant_dynamic-update-slice_fusion.2), channel_id=1, source_target_pairs={{0,9},{1,10},{2,11},{3,12},{4,13},{5,14},{6,15},{7,16},{8,17},{9,1... | collective-permute-start | bytes 221192 | tf_op jit(solution)/shard_map/ppermute | solution.py:25
  71.4 94.5 %collective-permute-start.9 = (f32[18,32,32]{2,1,0:T(8,128)}, f32[18,32,32]{2,1,0:T(8,128)}, u32[]{:S(2)}, u32[]{:S(2)}) collective-permute-start(f32[18,32,32]{2,1,0:T(8,128)} %constant_dynamic-update-slice_fusion.2), channel_id=1, source_target_pairs={{0,119},{1,120},{2,121},{3,122},{4,123},{5,124},{6,125},{7,126},{8... | collective-permute-start | bytes 221192 | tf_op jit(solution)/shard_map/ppermute | solution.py:25
  117.1 11.8 %copy-start.69 = (f32[3,32,32]{2,1,0:T(8,128)S(1)}, f32[3,32,32]{2,1,0:T(8,128)}, u32[]{:S(2)}) copy-start(f32[3,32,32]{2,1,0:T(8,128)} %copy-done.68) | copy-start | bytes 36868
  117.1 12.4 %copy-start.71 = (f32[3,32,32]{2,1,0:T(8,128)S(1)}, f32[3,32,32]{2,1,0:T(8,128)}, u32[]{:S(2)}) copy-start(f32[3,32,32]{2,1,0:T(8,128)} %copy-done.70) | copy-start | bytes 36868
  117.1 18.2 %copy-start = (f32[8,256,256]{2,1,0:T(8,128)S(1)}, f32[8,256,256]{2,1,0:T(8,128)}, u32[]{:S(2)}) copy-start(f32[8,256,256]{2,1,0:T(8,128)} %shard_map.41) | copy-start | bytes 6291460
  118.7 15.4 %collective-permute-start.3 = (f32[3,256,256]{2,1,0:T(8,128)S(1)}, f32[3,256,256]{2,1,0:T(8,128)S(1)}, u32[]{:S(2)}, u32[]{:S(2)}) collective-permute-start(f32[3,256,256]{2,1,0:T(8,128)S(1)} %get-tuple-element.39), channel_id=1, source_target_pairs={{1,0},{2,1},{3,2},{4,3},{5,4},{6,5},{7,6},{8,7},{9,8},{10,9},{11,1... | collective-permute-start | bytes 2359304 | tf_op jit(solution)/shard_map/ppermute | solution.py:25
  120.6 14.7 %collective-permute-start.2 = (f32[3,256,256]{2,1,0:T(8,128)S(1)}, f32[3,256,256]{2,1,0:T(8,128)S(1)}, u32[]{:S(2)}, u32[]{:S(2)}) collective-permute-start(f32[3,256,256]{2,1,0:T(8,128)S(1)} %get-tuple-element.38), channel_id=1, source_target_pairs={{0,1},{1,2},{2,3},{3,4},{4,5},{5,6},{6,7},{7,8},{8,9},{9,10},{10,1... | collective-permute-start | bytes 2359304 | tf_op jit(solution)/shard_map/ppermute | solution.py:25
  158.8 12.8 %copy-start.10 = (f32[8,64,64]{2,1,0:T(8,128)S(1)}, f32[8,64,64]{2,1,0:T(8,128)}, u32[]{:S(2)}) copy-start(f32[8,64,64]{2,1,0:T(8,128)} %copy-done.9) | copy-start | bytes 393220
  158.8 12.8 %copy-start.22 = (f32[6,64,64]{2,1,0:T(8,128)S(1)}, f32[6,64,64]{2,1,0:T(8,128)}, u32[]{:S(2)}) copy-start(f32[6,64,64]{2,1,0:T(8,128)} %copy-done.21) | copy-start | bytes 294916
  158.8 12.7 %copy-start.51 = (f32[6,66,1]{2,1,0:T(8,128)S(1)}, f32[6,66,1]{2,1,0:T(8,128)}, u32[]{:S(2)}) copy-start(f32[6,66,1]{2,1,0:T(8,128)} %get-tuple-element.72) | copy-start | bytes 4756
  158.8 12.7 %copy-start.52 = (f32[6,66,1]{2,1,0:T(8,128)S(1)}, f32[6,66,1]{2,1,0:T(8,128)}, u32[]{:S(2)}) copy-start(f32[6,66,1]{2,1,0:T(8,128)} %get-tuple-element.73) | copy-start | bytes 4756
  158.8 12.7 %copy-start.92 = (f32[6,1,64]{2,1,0:T(1,128)S(1)}, f32[6,1,64]{2,1,0:T(1,128)}, u32[]{:S(2)}) copy-start(f32[6,1,64]{2,1,0:T(1,128)} %copy-done.91) | copy-start | bytes 4612
  158.8 12.7 %copy-start.94 = (f32[6,1,64]{2,1,0:T(1,128)S(1)}, f32[6,1,64]{2,1,0:T(1,128)}, u32[]{:S(2)}) copy-start(f32[6,1,64]{2,1,0:T(1,128)} %copy-done.93) | copy-start | bytes 4612
  158.8 12.7 %copy-start.98 = (f32[6]{0:T(128)S(1)}, f32[6]{0:T(128)}, u32[]{:S(2)}) copy-start(f32[6]{0:T(128)} %and_convert_fusion.2) | copy-start | bytes 76
  159.5 12.5 %copy-start.61 = (f32[2,64,64]{2,1,0:T(8,128)S(1)}, f32[2,64,64]{2,1,0:T(8,128)}, u32[]{:S(2)}) copy-start(f32[2,64,64]{2,1,0:T(8,128)} %copy-done.60) | copy-start | bytes 98308
  159.5 12.5 %copy-start.80 = (f32[2,64,64]{2,1,0:T(8,128)S(1)}, f32[2,64,64]{2,1,0:T(8,128)}, u32[]{:S(2)}) copy-start(f32[2,64,64]{2,1,0:T(8,128)} %reshape.572) | copy-start | bytes 98308
  159.5 12.5 %copy-start.81 = (f32[2,64,64]{2,1,0:T(8,128)S(1)}, f32[2,64,64]{2,1,0:T(8,128)}, u32[]{:S(2)}) copy-start(f32[2,64,64]{2,1,0:T(8,128)} %reshape.571) | copy-start | bytes 98308
  161.2 8.2 %collective-permute-start.11 = (f32[41984]{0:T(1024)S(1)}, f32[41984]{0:T(1024)S(1)}, u32[]{:S(2)}, u32[]{:S(2)}) collective-permute-start(f32[41984]{0:T(1024)S(1)} %get-tuple-element.88), channel_id=1, source_target_pairs={{0,127},{1,0},{2,1},{3,2},{4,3},{5,4},{6,5},{7,6},{8,7},{9,8},{10,... | collective-permute-start | bytes 503816 | tf_op jit(solution)/shard_map/ppermute | solution.py:25
  161.2 8.2 %collective-permute-start.10 = (f32[41984]{0:T(1024)S(1)}, f32[41984]{0:T(1024)S(1)}, u32[]{:S(2)}, u32[]{:S(2)}) collective-permute-start(f32[41984]{0:T(1024)S(1)} %get-tuple-element.87), channel_id=1, source_target_pairs={{0,1},{1,2},{2,3},{3,4},{4,5},{5,6},{6,7},{7,8},{8,9},{9,10},{10,1... | collective-permute-start | bytes 503816 | tf_op jit(solution)/shard_map/ppermute | solution.py:25
  169.6 8.7 %collective-permute-start.12 = (f32[3,32,32]{2,1,0:T(8,128)S(1)}, f32[3,32,32]{2,1,0:T(8,128)S(1)}, u32[]{:S(2)}, u32[]{:S(2)}) collective-permute-start(f32[3,32,32]{2,1,0:T(8,128)S(1)} %pad_maximum_fusion.53), channel_id=1, source_target_pairs={{0,3},{1,4},{2,5},{3,6},{4,7},{5,8},{6,9},{7,10},{8,11},{9,12},{10... | collective-permute-start | bytes 36872 | tf_op jit(solution)/shard_map/ppermute | solution.py:25
  170.6 7.8 %collective-permute-start.13 = (f32[3,32,32]{2,1,0:T(8,128)S(1)}, f32[3,32,32]{2,1,0:T(8,128)S(1)}, u32[]{:S(2)}, u32[]{:S(2)}) collective-permute-start(f32[3,32,32]{2,1,0:T(8,128)S(1)} %pad_maximum_fusion.53), channel_id=1, source_target_pairs={{0,125},{1,126},{2,127},{3,0},{4,1},{5,2},{6,3},{7,4},{8,5},{9,6},... | collective-permute-start | bytes 36872 | tf_op jit(solution)/shard_map/ppermute | solution.py:25
  172.0 22.1 %copy-start.19 = (f32[6,64,64]{2,1,0:T(8,128)}, f32[6,64,64]{2,1,0:T(8,128)S(1)}, u32[]{:S(2)}) copy-start(f32[6,64,64]{2,1,0:T(8,128)S(1)} %get-tuple-element.21) | copy-start | bytes 294916
  172.0 22.1 %copy-start.38 = (f32[6,64,64]{2,1,0:T(8,128)}, f32[6,64,64]{2,1,0:T(8,128)S(1)}, u32[]{:S(2)}) copy-start(f32[6,64,64]{2,1,0:T(8,128)S(1)} %get-tuple-element.22) | copy-start | bytes 294916
  172.0 22.0 %copy-start.40 = (f32[6,64,64]{2,1,0:T(8,128)}, f32[6,64,64]{2,1,0:T(8,128)S(1)}, u32[]{:S(2)}) copy-start(f32[6,64,64]{2,1,0:T(8,128)S(1)} %get-tuple-element.23) | copy-start | bytes 294916
  172.1 22.0 %copy-start.54 = (f32[6,64,64]{2,1,0:T(8,128)}, f32[6,64,64]{2,1,0:T(8,128)S(1)}, u32[]{:S(2)}) copy-start(f32[6,64,64]{2,1,0:T(8,128)S(1)} %get-tuple-element.20) | copy-start | bytes 294916
  176.8 17.5 %copy-start.35 = (f32[6,128,128]{2,1,0:T(8,128)}, f32[6,128,128]{2,1,0:T(8,128)S(1)}, u32[]{:S(2)}) copy-start(f32[6,128,128]{2,1,0:T(8,128)S(1)} %fusion.50) | copy-start | bytes 1179652
  177.3 27.3 %copy-start.33 = (f32[6,128,128]{2,1,0:T(8,128)}, f32[6,128,128]{2,1,0:T(8,128)S(1)}, u32[]{:S(2)}) copy-start(f32[6,128,128]{2,1,0:T(8,128)S(1)} %fusion.61) | copy-start | bytes 1179652
  177.3 26.2 %copy-start.57 = (f32[27,32,32]{2,1,0:T(8,128)S(1)}, f32[27,32,32]{2,1,0:T(8,128)}, u32[]{:S(2)}) copy-start(f32[27,32,32]{2,1,0:T(8,128)} %get-tuple-element.61) | copy-start | bytes 331780
  177.3 26.2 %copy-start.59 = (f32[27,32,32]{2,1,0:T(8,128)S(1)}, f32[27,32,32]{2,1,0:T(8,128)}, u32[]{:S(2)}) copy-start(f32[27,32,32]{2,1,0:T(8,128)} %get-tuple-element.60) | copy-start | bytes 331780
  177.3 26.2 %copy-start.99 = (f32[27]{0:T(128)S(1)}, f32[27]{0:T(128)}, u32[]{:S(2)}) copy-start(f32[27]{0:T(128)} %and_convert_fusion.4) | copy-start | bytes 328
  178.3 26.3 %copy-start.64 = (f32[4,64,64]{2,1,0:T(8,128)}, f32[4,64,64]{2,1,0:T(8,128)S(1)}, u32[]{:S(2)}) copy-start(f32[4,64,64]{2,1,0:T(8,128)S(1)} %fusion.154) | copy-start | bytes 196612
  178.4 17.8 %collective-permute-start.14 = (f32[9,32,32]{2,1,0:T(8,128)S(1)}, f32[9,32,32]{2,1,0:T(8,128)S(1)}, u32[]{:S(2)}, u32[]{:S(2)}) collective-permute-start(f32[9,32,32]{2,1,0:T(8,128)S(1)} %constant_dynamic-update-slice_fusion.27), channel_id=1, source_target_pairs={{0,9},{1,10},{2,11},{3,12},{4,13},{5,14},{6,15},{7,16},{8,17},{9,1... | collective-permute-start | bytes 110600 | tf_op jit(solution)/shard_map/ppermute | solution.py:25
  194.3 11.9 %copy-start.62 = (f32[4,64,64]{2,1,0:T(8,128)}, f32[4,64,64]{2,1,0:T(8,128)S(1)}, u32[]{:S(2)}) copy-start(f32[4,64,64]{2,1,0:T(8,128)S(1)} %fusion.165) | copy-start | bytes 196612
  194.3 12.9 %copy-start.90 = (s32[32]{0:T(128)S(1)}, s32[32]{0:T(128)}, u32[]{:S(2)}) copy-start(s32[32]{0:T(128)} %and_select_fusion) | copy-start | bytes 388
  194.3 9.1 %collective-permute-start.15 = (f32[9,32,32]{2,1,0:T(8,128)S(1)}, f32[9,32,32]{2,1,0:T(8,128)S(1)}, u32[]{:S(2)}, u32[]{:S(2)}) collective-permute-start(f32[9,32,32]{2,1,0:T(8,128)S(1)} %constant_dynamic-update-slice_fusion.27), channel_id=1, source_target_pairs={{0,119},{1,120},{2,121},{3,122},{4,123},{5,124},{6,125},{7,126},{8... | collective-permute-start | bytes 110600 | tf_op jit(solution)/shard_map/ppermute | solution.py:25
  (73 other events, 384.4 us)

commit v2 on v1

--- a/solution.py
+++ b/solution.py
@@ -93,7 +93,7 @@
     return spread.reshape(2 * extent_x, 2 * extent_y, 2 * extent_z)
 
 
-def make_coefs(rho_ext, inv_spacing):
+def make_coefs(rho_ext, inv_spacing, zero_sides=False):
     two_s = 2.0 * inv_spacing
     center = rho_ext[1:-1]
     safe = jnp.where(center > 0, center, 1.0)
@@ -108,14 +108,25 @@
     ]
     faces = [two_s / (safe + jnp.where(nb > 0, nb, safe)) for nb in near]
     diag = faces[0] + faces[1] + faces[2] + faces[3] + faces[4] + faces[5]
+    sides = faces[2:]
+    if zero_sides:
+        extent_y, extent_z = center.shape[1], center.shape[2]
+        ys = jnp.arange(extent_y, dtype=jnp.int32)[None, :, None]
+        zs = jnp.arange(extent_z, dtype=jnp.int32)[None, None, :]
+        sides = [
+            jnp.where(ys == 0, 0.0, sides[0]),
+            jnp.where(ys == extent_y - 1, 0.0, sides[1]),
+            jnp.where(zs == 0, 0.0, sides[2]),
+            jnp.where(zs == extent_z - 1, 0.0, sides[3]),
+        ]
     lo, hi = rho_ext[:-1], rho_ext[1:]
     kxo = jnp.where((lo > 0) & (hi > 0), two_s / (lo + hi), 0.0)
     return {
         "kxo": kxo,
-        "kyl": faces[2],
-        "kyh": faces[3],
-        "kzl": faces[4],
-        "kzh": faces[5],
+        "kyl": sides[0],
+        "kyh": sides[1],
+        "kzl": sides[2],
+        "kzh": sides[3],
         "w": OMEGA / diag,
         "diag": diag,
     }
@@ -274,29 +285,17 @@
     )(*args)
 
 
-def fine_coefs(co):
-    extent_y, extent_z = co["kyl"].shape[1], co["kyl"].shape[2]
-    ys = jnp.arange(extent_y, dtype=jnp.int32)[None, :, None]
-    zs = jnp.arange(extent_z, dtype=jnp.int32)[None, None, :]
-    return {
-        "kyl": jnp.where(ys == 0, 0.0, co["kyl"]),
-        "kyh": jnp.where(ys == extent_y - 1, 0.0, co["kyh"]),
-        "kzl": jnp.where(zs == 0, 0.0, co["kzl"]),
-        "kzh": jnp.where(zs == extent_z - 1, 0.0, co["kzh"]),
-    }
-
-
-def fine_smooth(resid_ext, co, fc):
+def fine_smooth(resid_ext, co):
     length, extent_y, extent_z = resid_ext.shape
     out = jax.ShapeDtypeStruct((length - 2 * (SWEEPS - 1), extent_y, extent_z), jnp.float32)
     padded = lambda planes: pltpu.VMEM((planes, extent_y + 2 * PAD, extent_z), jnp.float32)
     return _vmem_call(
         _fine_first_kernel, out, [padded(length), padded(length - 2)],
-        resid_ext, co["kxo"][1:-1], fc["kyl"], fc["kyh"], fc["kzl"], fc["kzh"], co["w"],
-    )
-
-
-def fine_second(fine_ext, rhs_ext, co, fc):
+        resid_ext, co["kxo"][1:-1], co["kyl"], co["kyh"], co["kzl"], co["kzh"], co["w"],
+    )
+
+
+def fine_second(fine_ext, rhs_ext, co):
     planes, extent_y, extent_z = fine_ext.shape
     length = planes - 2
     block = length - 2 * (SWEEPS - 1)
@@ -306,7 +305,7 @@
         _fine_second_kernel, outs,
         [padded(planes), pltpu.VMEM((length, extent_y, extent_z), jnp.float32),
          padded(length), padded(length - 2)],
-        fine_ext, rhs_ext, co["kxo"], fc["kyl"], fc["kyh"], fc["kzl"], fc["kzh"], co["w"], co["diag"],
+        fine_ext, rhs_ext, co["kxo"], co["kyl"], co["kyh"], co["kzl"], co["kzh"], co["w"], co["diag"],
     )
 
 
@@ -318,7 +317,13 @@
     )
     rho0_ext = jnp.concatenate([dl, density, dr])
     rhs_ext = jnp.concatenate([rl, right_side, rr])
-    co0 = make_coefs(rho0_ext, 1.0)
+    co0 = make_coefs(rho0_ext, 1.0, zero_sides=True)
+
+    fine_0 = fine_smooth(rhs_ext, co0)
+
+    (fl,), (fr,) = exchange([fine_0[-3:]], [fine_0[:3]], 1)
+    fine_ext = jnp.concatenate([fl, fine_0, fr])
+    fine_1, resid_block = fine_second(fine_ext, rhs_ext, co0)
 
     rho1 = coarsen(density)
     rho2 = coarsen(rho1)
@@ -329,45 +334,38 @@
         r2 = coarsen(r1)
         return r1, r2, coarsen(r2)
 
-    def gather_coarse(r1, r2, r3, with_rho):
-        to_right = [r1[-2:], r2, r3]
-        to_left = [r1[:2], r2, r3]
-        if with_rho:
-            to_right += [rho1[-3:], rho2, rho3]
-            to_left += [rho1[:3], rho2, rho3]
-        got_l, got_r = exchange(to_right, to_left, 1, True)
-        r1e = jnp.concatenate([got_l[0], r1, got_r[0]])
-        r2e = jnp.concatenate([got_l[1], r2, got_r[1]])
-        win3 = [jnp.concatenate([got_l[2], r3, got_r[2]])]
-        extra = {}
-        if with_rho:
-            extra["rho1e"] = jnp.concatenate([got_l[3], rho1, got_r[3]])
-            rho2_l, rho2_r = got_l[4], got_r[4]
-            win3.append(jnp.concatenate([got_l[5], rho3, got_r[5]]))
-        to_right = list(win3)
-        to_left = list(win3)
-        if with_rho:
-            to_right.append(rho2_r[-1:])
-            to_left.append(rho2_l[:1])
-        got_l, got_r = exchange(to_right, to_left, 3, True)
-        win9 = [jnp.concatenate([got_l[k], win3[k], got_r[k]]) for k in range(len(win3))]
-        if with_rho:
-            extra["rho2e"] = jnp.concatenate([got_l[-1], rho2_l, rho2, rho2_r, got_r[-1]])
-        got_l, got_r = exchange(win9, win9, 9, True)
-        win27 = [jnp.concatenate([got_l[k], win9[k], got_r[k]]) for k in range(len(win9))]
-        win27 = [part * inside(1, 13, 27) for part in win27]
-        r1e = r1e * inside(4, 2, r1e.shape[0])
-        r2e = r2e * inside(2, 2, r2e.shape[0])
-        if with_rho:
-            extra["rho1e"] = extra["rho1e"] * inside(4, 3, extra["rho1e"].shape[0])
-            extra["rho2e"] = extra["rho2e"] * inside(2, 3, extra["rho2e"].shape[0])
-        return r1e, r2e, win27, extra
-
-    r1, r2, r3 = restrict(right_side)
-    r1e, r2e, win, extra = gather_coarse(r1, r2, r3, True)
-    r3w, rho3w = win
-    co1 = make_coefs(extra["rho1e"], 0.25)
-    co2 = make_coefs(extra["rho2e"], 0.25**2)
+    cycles = [restrict(right_side), restrict(resid_block)]
+    to_right, to_left = [], []
+    for r1, r2, _ in cycles:
+        to_right += [r1[-2:], r2]
+        to_left += [r1[:2], r2]
+    to_right += [rho1[-3:], rho2]
+    to_left += [rho1[:3], rho2]
+    level3 = jnp.concatenate([r3 for _, _, r3 in cycles] + [rho3])
+    to_right.append(level3)
+    to_left.append(level3)
+    got_l, got_r = exchange(to_right, to_left, 1, True)
+    parts = []
+    for k, (r1, r2, _) in enumerate(cycles):
+        r1e = jnp.concatenate([got_l[2 * k], r1, got_r[2 * k]])
+        r2e = jnp.concatenate([got_l[2 * k + 1], r2, got_r[2 * k + 1]])
+        parts.append((r1e * inside(4, 2, r1e.shape[0]), r2e * inside(2, 2, r2e.shape[0])))
+    at = 2 * len(cycles)
+    rho1e = jnp.concatenate([got_l[at], rho1, got_r[at]])
+    rho2_l, rho2_r = got_l[at + 1], got_r[at + 1]
+    win3 = jnp.concatenate([got_l[-1], level3, got_r[-1]])
+    got_l, got_r = exchange([win3, rho2_r[-1:]], [win3, rho2_l[:1]], 3, True)
+    win9 = jnp.concatenate([got_l[0], win3, got_r[0]])
+    rho2e = jnp.concatenate([got_l[1], rho2_l, rho2, rho2_r, got_r[1]])
+    (got_l,), (got_r,) = exchange([win9], [win9], 9, True)
+    win27 = jnp.concatenate([got_l, win9, got_r])
+    per = len(cycles) + 1
+    win27 = win27.reshape(27, per, win27.shape[1], win27.shape[2]) * inside(1, 13, 27)[:, None]
+    windows = [win27[:, k] for k in range(per)]
+    rho3w = windows[-1]
+
+    co1 = make_coefs(rho1e * inside(4, 3, rho1e.shape[0]), 0.25)
+    co2 = make_coefs(rho2e * inside(2, 3, rho2e.shape[0]), 0.25**2)
     center = 13
     co3 = make_coefs(rho3w[center - 3:center + 4], 0.25**3)
     pair_start = 1 - me % 2
@@ -384,17 +382,8 @@
         summed = refine(summed) + smooth(r1e, co1, SWEEPS)
         return refine(summed)
 
-    fc0 = fine_coefs(co0)
-    fine_0 = fine_smooth(rhs_ext, co0, fc0)
-    coarse_0 = coarse_part(r1e, r2e, r3w)
-
-    (fl,), (fr,) = exchange([fine_0[-3:]], [fine_0[:3]], 1)
-    fine_ext = jnp.concatenate([fl, fine_0, fr])
-    fine_1, resid_block = fine_second(fine_ext, rhs_ext, co0, fc0)
-    r1, r2, r3 = restrict(resid_block)
-    r1e, r2e, win, _ = gather_coarse(r1, r2, r3, False)
-    coarse_1 = coarse_part(r1e, r2e, win[0])
-
+    coarse_0 = coarse_part(parts[0][0], parts[0][1], windows[0])
+    coarse_1 = coarse_part(parts[1][0], parts[1][1], windows[1])
     pressure = (fine_0 + fine_1) + coarse_0
     return (pressure, coarse_1)
 

time: 250 us -> 222 us (0.89)
  the two profiles are of different devices: /device:TPU:117 before, /device:TPU:48 now
where the time goes in v2:
time: 222 us; the launch traced here: 220 us
  other arithmetic  51.7 us (23%)
  local copies, waits for them, and re-layouts  46.7 us (21%)
  starting transfers between devices  35.9 us (16%)
  Pallas kernels  32.9 us (15%)
  matrix products  27.6 us (12%)
  waiting for transfers between devices  22.3 us (10%)
  between operations  3.02 us (1%)
    ppermute x10, starting transfers between devices, recv(): return lax.ppermute(value, 'gx', pairs)  35.9 us
    pallas_call x2, Pallas kernels, _vmem_call(): pl.pallas_call(kernel, out_shape=outs, in_specs=[pl.BlockSpec(memory_spac...  32.9 us
    ppermute x10, waiting for transfers between devices, recv(): return lax.ppermute(value, 'gx', pairs)  22.3 us
    unnamed x245, local copies, waits for them, and re-layouts  12.7 us
    select_n x1, other arithmetic, make_coefs(): jnp.where(zs == extent_z - 1, 0.0, sides[3])  9.23 us
    dot_general x12, matrix products, shrink_sides(): jnp.einsum('xyz,zw->xyw', field, pair_matrix(extent_z), precision=EXACT)  8.77 us
    reduce_sum x7, other arithmetic, coarsen(): planes = field.reshape(extent_x // 2, 2, extent_y, extent_z).sum(axis=1)  7.52 us
    div x1, other arithmetic, make_coefs(): OMEGA / diag  7.08 us
  transfers between devices with their start and end apart: 10, of which 6 were waited for; matrix products, arithmetic and copies ran while one was open for 14% of the time, Pallas kernels for 0%

profile of v2, /device:TPU:48, one launch (start us, length us, event | category | flops | bytes accessed | tf_op | source)
XLA Modules:
  0.0 220.2 jit_solution(4916652410476957000)
XLA Ops:
  0.6 1.6 fusion.599
  2.8 1.2 pad_maximum_fusion.12
  3.9 2.0 collective-permute-start
  6.0 1.2 pad_maximum_fusion.13
  7.1 3.6 %collective-permute-start.1 = (f32[5,256,256]{2,1,0:T(8,128)}, f32[5,256,256]{2,1,0:T(8,128)}, u32[]{:S(2)}, u32[]{:S(2)}) collective-permute-start(f32[5,256,256]{2,1,0:T(8,128)} %pad_maximum_fusion.13), channel_id=1, source_target_pairs={{1,0},{2,1},{3,2},{4,3},{5,4},{6,5},{7,6},{8,7},{9,8},{10,9},{11,1... | collective-permute-start | bytes 3932168 | tf_op jit(solution)/shard_map/ppermute | solution.py:25
  13.9 1.1 bitcast_reduce_fusion.3
  18.6 4.7 %collective-permute-done = f32[5,256,256]{2,1,0:T(8,128)} collective-permute-done((f32[5,256,256]{2,1,0:T(8,128)}, f32[5,256,256]{2,1,0:T(8,128)}, u32[]{:S(2)}, u32[]{:S(2)}) %collective-permute-start) | collective-permute-done | bytes 1310752 | tf_op jit(solution)/shard_map/ppermute | solution.py:25
  23.3 1.2 slice.1729
  24.5 1.7 collective-permute-done.1
  26.2 1.2 slice.1730
  30.6 1.8 slice.1733.kxo
  32.4 7.1 %broadcast_divide_fusion = (f32[12,256,256]{2,1,0:T(8,128)}, f32[12,256,256]{2,1,0:T(8,128)}) fusion(f32[12,258,1]{2,1,0:T(8,128)S(1)} %get-tuple-element.32, f32[12,1,256]{2,1,0:T(1,128)S(1)} %get-tuple-element.30, f32[12,256,256]{2,1,0:T(8,128)S(1)} %slice.1734, f32[12,1,256]{2,1,0:T(1,128)S(1)} %get-tuple-element.31, ...), kind=kLoop, calls=%fused_computation.41 | loop fusion | flops 31457280 | bytes 15777984 | tf_op jit(solution)/shard_map/div | solution.py:130
  39.5 9.2 %broadcast_select_fusion = (f32[12,256,256]{2,1,0:T(8,128)}, f32[12,256,256]{2,1,0:T(8,128)}, f32[12,256,256]{2,1,0:T(8,128)}, f32[12,256,256]{2,1,0:T(8,128)}) fusion(pred[256]{0:T(512)(128)(4,1)S(1)} %get-tuple-element.104, f32[12,258,1]{2,1,0:T(8,128)S(1)} %get-tuple-element.32, f32[12,1,256]{2,1,0:T(1,128)S(1)} %get-tuple-element.30, ...), kind=kLoop, calls=%fused_computation.42 | loop fusion | flops 23592960 | bytes 15778496 | tf_op jit(solution)/shard_map/jit(_where)/select_n | solution.py:120
  48.7 1.1 slice.1727
  49.8 1.1 slice.1728
  50.9 2.0 pad_maximum_fusion.11.resid.rhs
  52.8 13.4 %shard_map.41 = f32[8,256,256]{2,1,0:T(8,128)} custom-call(f32[12,256,256]{2,1,0:T(8,128)} %pad_maximum_fusion.11.resid.rhs, f32[11,256,256]{2,1,0:T(8,128)} %slice.1733.kxo, f32[12,256,256]{2,1,0:T(8,128)} %get-tuple-element.36.kyl, f32[12,256,256]{2,1,0:T(8,128)} %get-tuple-element.37.kyh, f32[12,256,256]{2,1,0:T(8,128)} %get-tuple-element.35.kzl, ...), custom_call_target="tpu_custom_call" | custom-call | tf_op jit(solution)/shard_map/pallas_call | solution.py:274
  66.3 1.6 fusion.598
  67.9 4.1 %collective-permute-start.2 = (f32[3,256,256]{2,1,0:T(8,128)S(1)}, f32[3,256,256]{2,1,0:T(8,128)S(1)}, u32[]{:S(2)}, u32[]{:S(2)}) collective-permute-start(f32[3,256,256]{2,1,0:T(8,128)S(1)} %get-tuple-element.38), channel_id=1, source_target_pairs={{0,1},{1,2},{2,3},{3,4},{4,5},{5,6},{6,7},{7,8},{8,9},{9,10},{10,1... | collective-permute-start | bytes 2359304 | tf_op jit(solution)/shard_map/ppermute | solution.py:25
  72.0 2.1 collective-permute-start.3
  77.4 4.0 %collective-permute-done.2 = f32[3,256,256]{2,1,0:T(8,128)S(1)} collective-permute-done((f32[3,256,256]{2,1,0:T(8,128)S(1)}, f32[3,256,256]{2,1,0:T(8,128)S(1)}, u32[]{:S(2)}, u32[]{:S(2)}) %collective-permute-start.2) | collective-permute-done | bytes 786464 | tf_op jit(solution)/shard_map/ppermute | solution.py:25
  81.4 2.0 collective-permute-done.3
  83.4 2.1 pad_maximum_fusion.1.fine_ext
  85.6 19.4 %shard_map.42 = (f32[8,256,256]{2,1,0:T(8,128)}, f32[8,256,256]{2,1,0:T(8,128)}) custom-call(f32[14,256,256]{2,1,0:T(8,128)} %pad_maximum_fusion.1.fine_ext, f32[12,256,256]{2,1,0:T(8,128)} %pad_maximum_fusion.11.resid.rhs, f32[13,256,256]{2,1,0:T(8,128)} %copy-done.3, f32[12,256,256]{2,1,0:T(8,128)} %get-tuple-element.36.kyl, ...), custom_call_target="tpu_custom_call" | custom-call | tf_op jit(solution)/shard_map/pallas_call | solution.py:274
  105.0 2.0 bitcast_reduce_fusion.1
  109.6 2.0 collective-permute-start.4
  116.2 3.0 %collective-permute-done.4 = f32[142336]{0:T(1024)S(1)} collective-permute-done((f32[142336]{0:T(1024)S(1)}, f32[142336]{0:T(1024)S(1)}, u32[]{:S(2)}, u32[]{:S(2)}) %collective-permute-start.4) | collective-permute-done | bytes 569376 | tf_op jit(solution)/shard_map/ppermute | solution.py:25
  130.2 5.3 %collective-permute-start.6 = (f32[13312]{0:T(1024)}, f32[13312]{0:T(1024)}, u32[]{:S(2)}, u32[]{:S(2)}) collective-permute-start(f32[13312]{0:T(1024)} %get-tuple-element.85), channel_id=1, source_target_pairs={{0,3},{1,4},{2,5},{3,6},{4,7},{5,8},{6,9},{7,10},{8,11},{9,12},{10... | collective-permute-start | bytes 159752 | tf_op jit(solution)/shard_map/ppermute | solution.py:25
  135.5 11.7 %collective-permute-start.7 = (f32[13312]{0:T(1024)}, f32[13312]{0:T(1024)}, u32[]{:S(2)}, u32[]{:S(2)}) collective-permute-start(f32[13312]{0:T(1024)} %get-tuple-element.84), channel_id=1, source_target_pairs={{0,125},{1,126},{2,127},{3,0},{4,1},{5,2},{6,3},{7,4},{8,5},{9,6},... | collective-permute-start | bytes 159752 | tf_op jit(solution)/shard_map/ppermute | solution.py:25
  147.2 1.1 fusion.594
  158.5 4.8 %collective-permute-start.9 = (f32[27,32,32]{2,1,0:T(8,128)}, f32[27,32,32]{2,1,0:T(8,128)}, u32[]{:S(2)}, u32[]{:S(2)}) collective-permute-start(f32[27,32,32]{2,1,0:T(8,128)} %constant_dynamic-update-slice_fusion.7), channel_id=1, source_target_pairs={{0,119},{1,120},{2,121},{3,122},{4,123},{5,124},{6,125},{7,126},{8... | collective-permute-start | bytes 331784 | tf_op jit(solution)/shard_map/ppermute | solution.py:25
  165.7 1.1 fusion.590
  167.4 6.8 %collective-permute-done.8 = f32[27,32,32]{2,1,0:T(8,128)} collective-permute-done((f32[27,32,32]{2,1,0:T(8,128)}, f32[27,32,32]{2,1,0:T(8,128)}, u32[]{:S(2)}, u32[]{:S(2)}) %collective-permute-start.8) | collective-permute-done | bytes 110624 | tf_op jit(solution)/shard_map/ppermute | solution.py:25
  179.3 1.7 reduce_sum.117
  181.0 1.5 fusion.539
  187.1 1.7 reduce_sum.119
  189.0 1.7 fusion.534
  190.8 1.2 fusion.199
  192.1 1.9 slice_multiply_fusion.14
  198.4 1.3 fusion.284
  200.6 1.6 convolution_bitcast_fusion
  203.2 1.8 reduce_sum.118
  205.0 1.6 fusion.537
  207.5 1.1 fusion.241
  212.5 1.2 fusion.25
  214.2 1.3 fusion.267
  217.0 1.7 bitcast_add_fusion
  218.7 1.5 broadcast_in_dim.85
  (431 shorter events, 66.3 us)
Async XLA Ops:
  3.9 19.4 %collective-permute-start = (f32[5,256,256]{2,1,0:T(8,128)}, f32[5,256,256]{2,1,0:T(8,128)}, u32[]{:S(2)}, u32[]{:S(2)}) collective-permute-start(f32[5,256,256]{2,1,0:T(8,128)} %pad_maximum_fusion.12), channel_id=1, source_target_pairs={{0,1},{1,2},{2,3},{3,4},{4,5},{5,6},{6,7},{7,8},{8,9},{9,10},{10,1... | collective-permute-start | bytes 3932168 | tf_op jit(solution)/shard_map/ppermute | solution.py:25
  7.1 19.1 %collective-permute-start.1 = (f32[5,256,256]{2,1,0:T(8,128)}, f32[5,256,256]{2,1,0:T(8,128)}, u32[]{:S(2)}, u32[]{:S(2)}) collective-permute-start(f32[5,256,256]{2,1,0:T(8,128)} %pad_maximum_fusion.13), channel_id=1, source_target_pairs={{1,0},{2,1},{3,2},{4,3},{5,4},{6,5},{7,6},{8,7},{9,8},{10,9},{11,1... | collective-permute-start | bytes 3932168 | tf_op jit(solution)/shard_map/ppermute | solution.py:25
  12.2 12.3 %copy-start.29 = (f32[128,4,128]{2,0,1:T(8,128)}, f32[128,4,128]{2,0,1:T(8,128)S(1)}, u32[]{:S(2)}) copy-start(f32[128,4,128]{2,0,1:T(8,128)S(1)} %get-tuple-element.95) | copy-start | bytes 786436
  13.3 14.1 %copy-start.58 = (f32[2,64,64]{2,1,0:T(8,128)}, f32[2,64,64]{2,1,0:T(8,128)S(1)}, u32[]{:S(2)}) copy-start(f32[2,64,64]{2,1,0:T(8,128)S(1)} %get-tuple-element.103) | copy-start | bytes 98308
  15.5 12.2 %copy-start.45 = (f32[64,2,64]{2,0,1:T(8,128)}, f32[64,2,64]{2,0,1:T(8,128)S(1)}, u32[]{:S(2)}) copy-start(f32[64,2,64]{2,0,1:T(8,128)S(1)} %copy.81) | copy-start | bytes 98308
  16.9 10.8 %copy-start.103 = (s32[64]{0:T(128)}, s32[64]{0:T(128)S(1)}, u32[]{:S(2)}) copy-start(s32[64]{0:T(128)S(1)} %and_select_fusion.1) | copy-start | bytes 772
  39.5 11.4 %copy-start.5 = (f32[8,256,256]{2,1,0:T(8,128)S(1)}, f32[8,256,256]{2,1,0:T(8,128)}, u32[]{:S(2)}) copy-start(f32[8,256,256]{2,1,0:T(8,128)} %param.2) | copy-start | bytes 6291460
  66.3 9.3 %copy-start.97 = (f32[64,64]{1,0:T(8,128)S(1)}, f32[64,64]{1,0:T(8,128)}, u32[]{:S(2)}) copy-start(f32[64,64]{1,0:T(8,128)} %get-tuple-element.102) | copy-start | bytes 49156
  66.3 10.4 %copy-start.17 = (f32[128,4,128]{2,0,1:T(8,128)S(1)}, f32[128,4,128]{2,0,1:T(8,128)}, u32[]{:S(2)}) copy-start(f32[128,4,128]{2,0,1:T(8,128)} %get-tuple-element.99) | copy-start | bytes 786436
  66.3 17.2 %copy-start = (f32[8,256,256]{2,1,0:T(8,128)S(1)}, f32[8,256,256]{2,1,0:T(8,128)}, u32[]{:S(2)}) copy-start(f32[8,256,256]{2,1,0:T(8,128)} %shard_map.41) | copy-start | bytes 6291460
  67.9 13.5 %collective-permute-start.2 = (f32[3,256,256]{2,1,0:T(8,128)S(1)}, f32[3,256,256]{2,1,0:T(8,128)S(1)}, u32[]{:S(2)}, u32[]{:S(2)}) collective-permute-start(f32[3,256,256]{2,1,0:T(8,128)S(1)} %get-tuple-element.38), channel_id=1, source_target_pairs={{0,1},{1,2},{2,3},{3,4},{4,5},{5,6},{6,7},{7,8},{8,9},{9,10},{10,1... | collective-permute-start | bytes 2359304 | tf_op jit(solution)/shard_map/ppermute | solution.py:25
  72.0 11.4 %collective-permute-start.3 = (f32[3,256,256]{2,1,0:T(8,128)S(1)}, f32[3,256,256]{2,1,0:T(8,128)S(1)}, u32[]{:S(2)}, u32[]{:S(2)}) collective-permute-start(f32[3,256,256]{2,1,0:T(8,128)S(1)} %get-tuple-element.39), channel_id=1, source_target_pairs={{1,0},{2,1},{3,2},{4,3},{5,4},{6,5},{7,6},{8,7},{9,8},{10,9},{11,1... | collective-permute-start | bytes 2359304 | tf_op jit(solution)/shard_map/ppermute | solution.py:25
  107.1 12.2 %copy-start.18 = (f32[128,4,128]{2,0,1:T(8,128)S(1)}, f32[128,4,128]{2,0,1:T(8,128)}, u32[]{:S(2)}) copy-start(f32[128,4,128]{2,0,1:T(8,128)} %get-tuple-element.99) | copy-start | bytes 786436
  109.6 9.6 %collective-permute-start.4 = (f32[142336]{0:T(1024)S(1)}, f32[142336]{0:T(1024)S(1)}, u32[]{:S(2)}, u32[]{:S(2)}) collective-permute-start(f32[142336]{0:T(1024)S(1)} %get-tuple-element.92), channel_id=1, source_target_pairs={{0,1},{1,2},{2,3},{3,4},{4,5},{5,6},{6,7},{7,8},{8,9},{9,10},{10,1... | collective-permute-start | bytes 1708040 | tf_op jit(solution)/shard_map/ppermute | solution.py:25
  111.6 7.7 %collective-permute-start.5 = (f32[142336]{0:T(1024)S(1)}, f32[142336]{0:T(1024)S(1)}, u32[]{:S(2)}, u32[]{:S(2)}) collective-permute-start(f32[142336]{0:T(1024)S(1)} %get-tuple-element.93), channel_id=1, source_target_pairs={{0,127},{1,0},{2,1},{3,2},{4,3},{5,4},{6,5},{7,6},{8,7},{9,8},{10,... | collective-permute-start | bytes 1708040 | tf_op jit(solution)/shard_map/ppermute | solution.py:25
  120.1 28.2 %copy-start.6 = (f32[8,128,128]{2,1,0:T(8,128)}, f32[8,128,128]{2,1,0:T(8,128)S(1)}, u32[]{:S(2)}) copy-start(f32[8,128,128]{2,1,0:T(8,128)S(1)} %get-tuple-element.62) | copy-start | bytes 1572868
  123.1 25.3 %copy-start.9 = (f32[8,128,128]{2,1,0:T(8,128)}, f32[8,128,128]{2,1,0:T(8,128)S(1)}, u32[]{:S(2)}) copy-start(f32[8,128,128]{2,1,0:T(8,128)S(1)} %get-tuple-element.9) | copy-start | bytes 1572868
  123.1 24.0 %copy-start.30 = (f32[128,4,128]{2,0,1:T(8,128)S(1)}, f32[128,4,128]{2,0,1:T(8,128)}, u32[]{:S(2)}) copy-start(f32[128,4,128]{2,0,1:T(8,128)} %copy-done.29) | copy-start | bytes 786436
  128.8 19.6 %copy-start.13 = (f32[8,128,128]{2,1,0:T(8,128)S(1)}, f32[8,128,128]{2,1,0:T(8,128)}, u32[]{:S(2)}) copy-start(f32[8,128,128]{2,1,0:T(8,128)} %copy-done.12) | copy-start | bytes 1572868
  130.2 22.1 %collective-permute-start.6 = (f32[13312]{0:T(1024)}, f32[13312]{0:T(1024)}, u32[]{:S(2)}, u32[]{:S(2)}) collective-permute-start(f32[13312]{0:T(1024)} %get-tuple-element.85), channel_id=1, source_target_pairs={{0,3},{1,4},{2,5},{3,6},{4,7},{5,8},{6,9},{7,10},{8,11},{9,12},{10... | collective-permute-start | bytes 159752 | tf_op jit(solution)/shard_map/ppermute | solution.py:25
  135.5 21.4 %collective-permute-start.7 = (f32[13312]{0:T(1024)}, f32[13312]{0:T(1024)}, u32[]{:S(2)}, u32[]{:S(2)}) collective-permute-start(f32[13312]{0:T(1024)} %get-tuple-element.84), channel_id=1, source_target_pairs={{0,125},{1,126},{2,127},{3,0},{4,1},{5,2},{6,3},{7,4},{8,5},{9,6},... | collective-permute-start | bytes 159752 | tf_op jit(solution)/shard_map/ppermute | solution.py:25
  148.4 15.7 %copy-start.46 = (f32[64,2,64]{2,0,1:T(8,128)S(1)}, f32[64,2,64]{2,0,1:T(8,128)}, u32[]{:S(2)}) copy-start(f32[64,2,64]{2,0,1:T(8,128)} %copy-done.45) | copy-start | bytes 98308
  149.1 16.4 %copy-start.31 = (f32[6,128,128]{2,1,0:T(8,128)}, f32[6,128,128]{2,1,0:T(8,128)S(1)}, u32[]{:S(2)}) copy-start(f32[6,128,128]{2,1,0:T(8,128)S(1)} %fusion.53) | copy-start | bytes 1179652
  149.1 15.9 %copy-start.102 = (f32[8]{0:T(128)S(1)}, f32[8]{0:T(128)}, u32[]{:S(2)}) copy-start(f32[8]{0:T(128)} %and_convert_fusion.3) | copy-start | bytes 100
  150.9 14.5 %copy-start.57 = (f32[2,64,64]{2,1,0:T(8,128)S(1)}, f32[2,64,64]{2,1,0:T(8,128)}, u32[]{:S(2)}) copy-start(f32[2,64,64]{2,1,0:T(8,128)} %copy-done.56) | copy-start | bytes 98308
  158.5 15.8 %collective-permute-start.8 = (f32[27,32,32]{2,1,0:T(8,128)}, f32[27,32,32]{2,1,0:T(8,128)}, u32[]{:S(2)}, u32[]{:S(2)}) collective-permute-start(f32[27,32,32]{2,1,0:T(8,128)} %constant_dynamic-update-slice_fusion.7), channel_id=1, source_target_pairs={{0,9},{1,10},{2,11},{3,12},{4,13},{5,14},{6,15},{7,16},{8,17},{9,1... | collective-permute-start | bytes 331784 | tf_op jit(solution)/shard_map/ppermute | solution.py:25
  158.5 17.0 %collective-permute-start.9 = (f32[27,32,32]{2,1,0:T(8,128)}, f32[27,32,32]{2,1,0:T(8,128)}, u32[]{:S(2)}, u32[]{:S(2)}) collective-permute-start(f32[27,32,32]{2,1,0:T(8,128)} %constant_dynamic-update-slice_fusion.7), channel_id=1, source_target_pairs={{0,119},{1,120},{2,121},{3,122},{4,123},{5,124},{6,125},{7,126},{8... | collective-permute-start | bytes 331784 | tf_op jit(solution)/shard_map/ppermute | solution.py:25
  167.0 9.5 %copy-start.48 = (f32[6,64,64]{2,1,0:T(8,128)}, f32[6,64,64]{2,1,0:T(8,128)S(1)}, u32[]{:S(2)}) copy-start(f32[6,64,64]{2,1,0:T(8,128)S(1)} %get-tuple-element.27) | copy-start | bytes 294916
  167.0 9.5 %copy-start.101 = (f32[27]{0:T(128)S(1)}, f32[27]{0:T(128)}, u32[]{:S(2)}) copy-start(f32[27]{0:T(128)} %and_convert_fusion.4) | copy-start | bytes 328
  167.2 9.5 %copy-start.70 = (f32[4,64,64]{2,1,0:T(8,128)}, f32[4,64,64]{2,1,0:T(8,128)S(1)}, u32[]{:S(2)}) copy-start(f32[4,64,64]{2,1,0:T(8,128)S(1)} %fusion.168) | copy-start | bytes 196612
  186.3 12.1 %slice-start.6 = ((f32[4,64,64]{2,1,0:T(8,128)}), f32[2,64,64]{2,1,0:T(8,128)S(1)}, s32[]{:S(2)}) async-start(f32[4,64,64]{2,1,0:T(8,128)} %copy-done.70), calls=%async_computation.6 | async-start | bytes 131072 | tf_op jit(solution)/shard_map/slice | solution.py:151
  188.9 9.5 %copy-start.71 = (f32[4,64,64]{2,1,0:T(8,128)S(1)}, f32[4,64,64]{2,1,0:T(8,128)}, u32[]{:S(2)}) copy-start(f32[4,64,64]{2,1,0:T(8,128)} %copy-done.70) | copy-start | bytes 196612
  188.9 10.8 %copy-start.93 = (s32[128]{0:T(128)S(1)}, s32[128]{0:T(128)}, u32[]{:S(2)}) copy-start(s32[128]{0:T(128)} %copy-done.91) | copy-start | bytes 1540
  188.9 11.1 %copy-start.7 = (f32[8,128,128]{2,1,0:T(8,128)S(1)}, f32[8,128,128]{2,1,0:T(8,128)}, u32[]{:S(2)}) copy-start(f32[8,128,128]{2,1,0:T(8,128)} %copy-done.6) | copy-start | bytes 1572868
  188.9 11.1 %copy-start.10 = (f32[8,128,128]{2,1,0:T(8,128)S(1)}, f32[8,128,128]{2,1,0:T(8,128)}, u32[]{:S(2)}) copy-start(f32[8,128,128]{2,1,0:T(8,128)} %copy-done.9) | copy-start | bytes 1572868
  188.9 11.1 %copy-start.14 = (f32[8,128,128]{2,1,0:T(8,128)S(1)}, f32[8,128,128]{2,1,0:T(8,128)}, u32[]{:S(2)}) copy-start(f32[8,128,128]{2,1,0:T(8,128)} %copy-done.12) | copy-start | bytes 1572868
  188.9 11.1 %copy-start.28 = (f32[8,128,128]{2,1,0:T(8,128)S(1)}, f32[8,128,128]{2,1,0:T(8,128)}, u32[]{:S(2)}) copy-start(f32[8,128,128]{2,1,0:T(8,128)} %copy-done.27) | copy-start | bytes 1572868
  188.9 11.1 %copy-start.34 = (f32[6,128,128]{2,1,0:T(8,128)S(1)}, f32[6,128,128]{2,1,0:T(8,128)}, u32[]{:S(2)}) copy-start(f32[6,128,128]{2,1,0:T(8,128)} %copy-done.33) | copy-start | bytes 1179652
  188.9 11.1 %slice-start.1 = ((f32[6,128,128]{2,1,0:T(8,128)}), f32[4,128,128]{2,1,0:T(8,128)S(1)}, s32[]{:S(2)}) async-start(f32[6,128,128]{2,1,0:T(8,128)} %copy-done.33), calls=%async_computation.1 | async-start | bytes 524288 | tf_op jit(solution)/shard_map/slice | solution.py:151
  188.9 11.1 %copy-start.87 = (s32[256]{0:T(256)S(1)}, s32[256]{0:T(256)}, u32[]{:S(2)}) copy-start(s32[256]{0:T(256)} %copy-done.85) | copy-start | bytes 3076
  202.2 11.9 %slice-start.5 = ((f32[4,64,64]{2,1,0:T(8,128)}), f32[2,64,64]{2,1,0:T(8,128)S(1)}, s32[]{:S(2)}) async-start(f32[4,64,64]{2,1,0:T(8,128)} %copy-done.68), calls=%async_computation.5 | async-start | bytes 131072 | tf_op jit(solution)/shard_map/slice | solution.py:151
  204.9 10.8 %copy-start.8 = (f32[8,128,128]{2,1,0:T(8,128)S(1)}, f32[8,128,128]{2,1,0:T(8,128)}, u32[]{:S(2)}) copy-start(f32[8,128,128]{2,1,0:T(8,128)} %copy-done.6) | copy-start | bytes 1572868
  205.0 10.8 %copy-start.11 = (f32[8,128,128]{2,1,0:T(8,128)S(1)}, f32[8,128,128]{2,1,0:T(8,128)}, u32[]{:S(2)}) copy-start(f32[8,128,128]{2,1,0:T(8,128)} %copy-done.9) | copy-start | bytes 1572868
  205.0 10.8 %copy-start.15 = (f32[8,128,128]{2,1,0:T(8,128)S(1)}, f32[8,128,128]{2,1,0:T(8,128)}, u32[]{:S(2)}) copy-start(f32[8,128,128]{2,1,0:T(8,128)} %copy-done.12) | copy-start | bytes 1572868
  205.0 10.8 %copy-start.26 = (f32[8,128,128]{2,1,0:T(8,128)S(1)}, f32[8,128,128]{2,1,0:T(8,128)}, u32[]{:S(2)}) copy-start(f32[8,128,128]{2,1,0:T(8,128)} %copy-done.25) | copy-start | bytes 1572868
  205.0 10.8 %copy-start.32 = (f32[6,128,128]{2,1,0:T(8,128)S(1)}, f32[6,128,128]{2,1,0:T(8,128)}, u32[]{:S(2)}) copy-start(f32[6,128,128]{2,1,0:T(8,128)} %copy-done.31) | copy-start | bytes 1179652
  205.0 10.8 %slice-start = ((f32[6,128,128]{2,1,0:T(8,128)}), f32[4,128,128]{2,1,0:T(8,128)S(1)}, s32[]{:S(2)}) async-start(f32[6,128,128]{2,1,0:T(8,128)} %copy-done.31), calls=%async_computation | async-start | bytes 524288 | tf_op jit(solution)/shard_map/slice | solution.py:151
  205.0 10.8 %copy-start.88 = (s32[256]{0:T(256)S(1)}, s32[256]{0:T(256)}, u32[]{:S(2)}) copy-start(s32[256]{0:T(256)} %copy-done.85) | copy-start | bytes 3076
  (79 other events, 365.0 us)

commit v3 on v2

--- a/solution.py
+++ b/solution.py
@@ -93,7 +93,7 @@
     return spread.reshape(2 * extent_x, 2 * extent_y, 2 * extent_z)
 
 
-def make_coefs(rho_ext, inv_spacing, zero_sides=False):
+def make_coefs(rho_ext, inv_spacing):
     two_s = 2.0 * inv_spacing
     center = rho_ext[1:-1]
     safe = jnp.where(center > 0, center, 1.0)
@@ -109,16 +109,6 @@
     faces = [two_s / (safe + jnp.where(nb > 0, nb, safe)) for nb in near]
     diag = faces[0] + faces[1] + faces[2] + faces[3] + faces[4] + faces[5]
     sides = faces[2:]
-    if zero_sides:
-        extent_y, extent_z = center.shape[1], center.shape[2]
-        ys = jnp.arange(extent_y, dtype=jnp.int32)[None, :, None]
-        zs = jnp.arange(extent_z, dtype=jnp.int32)[None, None, :]
-        sides = [
-            jnp.where(ys == 0, 0.0, sides[0]),
-            jnp.where(ys == extent_y - 1, 0.0, sides[1]),
-            jnp.where(zs == 0, 0.0, sides[2]),
-            jnp.where(zs == extent_z - 1, 0.0, sides[3]),
-        ]
     lo, hi = rho_ext[:-1], rho_ext[1:]
     kxo = jnp.where((lo > 0) & (hi > 0), two_s / (lo + hi), 0.0)
     return {
@@ -189,8 +179,9 @@
     center = src[at, pl.ds(PAD + y0, ROWS), :]
     below = src[at, pl.ds(PAD + y0 - 1, ROWS), :]
     above = src[at, pl.ds(PAD + y0 + 1, ROWS), :]
-    left = pltpu.roll(center, 1, 1)
-    right = pltpu.roll(center, extent_z - 1, 1)
+    lanes = lax.broadcasted_iota(jnp.int32, center.shape, 1)
+    left = jnp.where(lanes == 0, 0.0, pltpu.roll(center, 1, 1))
+    right = jnp.where(lanes == extent_z - 1, 0.0, pltpu.roll(center, extent_z - 1, 1))
     off = (
         kxo_lo * src[at - 1, pl.ds(PAD + y0, ROWS), :]
         + kxo_hi * src[at + 1, pl.ds(PAD + y0, ROWS), :]
@@ -317,7 +308,7 @@
     )
     rho0_ext = jnp.concatenate([dl, density, dr])
     rhs_ext = jnp.concatenate([rl, right_side, rr])
-    co0 = make_coefs(rho0_ext, 1.0, zero_sides=True)
+    co0 = make_coefs(rho0_ext, 1.0)
 
     fine_0 = fine_smooth(rhs_ext, co0)
 
@@ -382,10 +373,13 @@
         summed = refine(summed) + smooth(r1e, co1, SWEEPS)
         return refine(summed)
 
-    coarse_0 = coarse_part(parts[0][0], parts[0][1], windows[0])
-    coarse_1 = coarse_part(parts[1][0], parts[1][1], windows[1])
-    pressure = (fine_0 + fine_1) + coarse_0
-    return (pressure, coarse_1)
+    coarse = jax.vmap(coarse_part)(
+        jnp.stack([parts[0][0], parts[1][0]]),
+        jnp.stack([parts[0][1], parts[1][1]]),
+        jnp.stack(windows[:2]),
+    )
+    pressure = (fine_0 + fine_1) + coarse[0]
+    return (pressure, coarse[1])
 
 
 def solution(mesh):

time: 222 us -> 258 us (1.16)
  local copies, waits for them, and re-layouts: 46.7 us -> 108 us
  other arithmetic: 51.7 us -> 36.2 us
  matrix products: 27.6 us -> 17.8 us
    slice x0 -> x86, local copies, waits for them, and re-layouts: none -> 57 us  [the longest x13 9.28 us: smooth(): update = (1.0 - OMEGA) * inner + co['w'][lo:hi] * (resid[lo:hi] + off)]
    mul x0 -> x19, local copies, waits for them, and re-layouts: none -> 14.9 us  [the longest x3 2.57 us: smooth(): kxo[lo - 1:hi - 1] * update[:-2] + kxo[lo:hi] * update[2:]]
    select_n x1 -> x0, other arithmetic: 9.23 us -> none  [make_coefs(): jnp.where(zs == extent_z - 1, 0.0, sides[3])]
    mul x8 -> x4, other arithmetic: 6.12 us -> 0.2 us  [smooth(): update = co['w'] * resid]
    reduce_sum x7 -> x6, other arithmetic: 7.52 us -> 2.43 us  [coarsen(): planes = field.reshape(extent_x // 2, 2, extent_y, extent_z).sum(axis=1)]
    div x4 -> x5, other arithmetic: 1.67 us -> 6.19 us  [make_coefs(): faces = [two_s / (safe + jnp.where(nb > 0, nb, safe)) for nb in near]]
    dot_general x12 -> x11, matrix products: 8.77 us -> 4.44 us  [shrink_sides(): jnp.einsum('xyz,zw->xyw', field, pair_matrix(extent_z), precision=EXACT)]
    reshape x12 -> x8, local copies, waits for them, and re-layouts: 3.52 us -> 0.62 us  [split(): out.append(flat[at:at + size].reshape(shape))]
  transfers between devices with their start and end apart: 10 -> 10, of which waited for: 6 -> 7; matrix products, arithmetic and copies ran while one was open for 14% -> 12% of each run, Pallas kernels for 0% -> 0%
where the time goes in v3:
time: 258 us; the launch traced here: 255 us
  local copies, waits for them, and re-layouts  108 us (42%)
  other arithmetic  36.2 us (14%)
  starting transfers between devices  36 us (14%)
  Pallas kernels  32.5 us (13%)
  waiting for transfers between devices  21.6 us (8%)
  matrix products  17.8 us (7%)
  between operations  2.61 us (1%)
    ppermute x10, starting transfers between devices, recv(): return lax.ppermute(value, 'gx', pairs)  36 us
    pallas_call x2, Pallas kernels, _vmem_call(): pl.pallas_call(kernel, out_shape=outs, in_specs=[pl.BlockSpec(memory_spac...  32.5 us
    ppermute x10, waiting for transfers between devices, recv(): return lax.ppermute(value, 'gx', pairs)  21.6 us
    unnamed x155, local copies, waits for them, and re-layouts  10.5 us
    div x5, other arithmetic, make_coefs(): OMEGA / diag  9.49 us
    slice x13, local copies, waits for them, and re-layouts, smooth(): update = (1.0 - OMEGA) * inner + co['w'][lo:hi] * (resid[lo:hi] + off)  9.28 us
    slice x13, local copies, waits for them, and re-layouts, side_terms(): co['kzl'][lo:hi] * padded[:, 1:-1, :-2]  9.21 us
    slice x13, local copies, waits for them, and re-layouts, side_terms(): co['kzh'][lo:hi] * padded[:, 1:-1, 2:]  9.2 us
  transfers between devices with their start and end apart: 10, of which 7 were waited for; matrix products, arithmetic and copies ran while one was open for 12% of the time, Pallas kernels for 0%

profile of v3, /device:TPU:48, one launch (start us, length us, event | category | flops | bytes accessed | tf_op | source)
XLA Modules:
  0.0 255.0 jit_solution(12891181613073929958)
XLA Ops:
  0.6 1.6 fusion.395
  3.9 2.0 collective-permute-start
  7.1 3.6 %collective-permute-start.1 = (f32[5,256,256]{2,1,0:T(8,128)}, f32[5,256,256]{2,1,0:T(8,128)}, u32[]{:S(2)}, u32[]{:S(2)}) collective-permute-start(f32[5,256,256]{2,1,0:T(8,128)} %pad_maximum_fusion.14), channel_id=1, source_target_pairs={{1,0},{2,1},{3,2},{4,3},{5,4},{6,5},{7,6},{8,7},{9,8},{10,9},{11,1... | collective-permute-start | bytes 3932168 | tf_op jit(solution)/shard_map/ppermute | solution.py:25
  19.5 3.8 %collective-permute-done = f32[5,256,256]{2,1,0:T(8,128)} collective-permute-done((f32[5,256,256]{2,1,0:T(8,128)}, f32[5,256,256]{2,1,0:T(8,128)}, u32[]{:S(2)}, u32[]{:S(2)}) %collective-permute-start) | collective-permute-done | bytes 1310752 | tf_op jit(solution)/shard_map/ppermute | solution.py:25
  24.5 1.7 collective-permute-done.1
  28.8 7.6 %broadcast_divide_fusion = (f32[12,256,256]{2,1,0:T(8,128)}, f32[12,256,256]{2,1,0:T(8,128)}, f32[12,256,256]{2,1,0:T(8,128)}) fusion(f32[12,258,1]{2,1,0:T(8,128)S(1)} %get-tuple-element.33, f32[12,1,256]{2,1,0:T(1,128)S(1)} %get-tuple-element.31, f32[12,256,256]{2,1,0:T(8,128)S(1)} %slice.1290, f32[12,1,256]{2,1,0:T(1,128)S(1)} %get-tuple-element.32, ...), kind=kLoop, calls=%fused_computation.50 | loop fusion | flops 33030144 | bytes 22069440 | tf_op jit(solution)/shard_map/div | solution.py:120
  36.5 5.8 %fusion.13 = (f32[12,256,256]{2,1,0:T(8,128)}, f32[12,256,256]{2,1,0:T(8,128)}, f32[12,256,256]{2,1,0:T(8,128)}) fusion(f32[12,258,1]{2,1,0:T(8,128)S(1)} %get-tuple-element.33, f32[12,1,256]{2,1,0:T(1,128)S(1)} %get-tuple-element.31, f32[12,256,256]{2,1,0:T(8,128)S(1)} %slice.1290, f32[12,1,256]{2,1,0:T(1,128)S(1)} %get-tuple-element.32, ...), kind=kLoop, calls=%fused_computation.24 | loop fusion | flops 16515072 | bytes 12632256 | tf_op jit(solution)/shard_map/div | solution.py:109
  42.9 1.7 slice.1289.kxo
  44.7 1.9 slice.1283
  47.7 2.0 pad_maximum_fusion.11.resid.rhs
  49.7 13.3 %shard_map.41 = f32[8,256,256]{2,1,0:T(8,128)} custom-call(f32[12,256,256]{2,1,0:T(8,128)} %pad_maximum_fusion.11.resid.rhs, f32[11,256,256]{2,1,0:T(8,128)} %slice.1289.kxo, f32[12,256,256]{2,1,0:T(8,128)} %get-tuple-element.37.kyl, f32[12,256,256]{2,1,0:T(8,128)} %get-tuple-element.38.kyh, f32[12,256,256]{2,1,0:T(8,128)} %get-tuple-element.36.kzl, ...), custom_call_target="tpu_custom_call" | custom-call | tf_op jit(solution)/shard_map/pallas_call | solution.py:265
  63.0 1.6 fusion.394
  64.6 4.1 %collective-permute-start.2 = (f32[3,256,256]{2,1,0:T(8,128)S(1)}, f32[3,256,256]{2,1,0:T(8,128)S(1)}, u32[]{:S(2)}, u32[]{:S(2)}) collective-permute-start(f32[3,256,256]{2,1,0:T(8,128)S(1)} %get-tuple-element.41), channel_id=1, source_target_pairs={{0,1},{1,2},{2,3},{3,4},{4,5},{5,6},{6,7},{7,8},{8,9},{9,10},{10,1... | collective-permute-start | bytes 2359304 | tf_op jit(solution)/shard_map/ppermute | solution.py:25
  68.7 2.1 collective-permute-start.3
  72.9 5.2 %collective-permute-done.2 = f32[3,256,256]{2,1,0:T(8,128)S(1)} collective-permute-done((f32[3,256,256]{2,1,0:T(8,128)S(1)}, f32[3,256,256]{2,1,0:T(8,128)S(1)}, u32[]{:S(2)}, u32[]{:S(2)}) %collective-permute-start.2) | collective-permute-done | bytes 786464 | tf_op jit(solution)/shard_map/ppermute | solution.py:25
  78.1 2.0 collective-permute-done.3
  80.1 2.1 pad_maximum_fusion.1.fine_ext
  82.2 19.2 %shard_map.42 = (f32[8,256,256]{2,1,0:T(8,128)}, f32[8,256,256]{2,1,0:T(8,128)}) custom-call(f32[14,256,256]{2,1,0:T(8,128)} %pad_maximum_fusion.1.fine_ext, f32[12,256,256]{2,1,0:T(8,128)} %pad_maximum_fusion.11.resid.rhs, f32[13,256,256]{2,1,0:T(8,128)} %copy-done.3, f32[12,256,256]{2,1,0:T(8,128)} %get-tuple-element.37.kyl, ...), custom_call_target="tpu_custom_call" | custom-call | tf_op jit(solution)/shard_map/pallas_call | solution.py:265
  101.5 2.0 bitcast_reduce_fusion.1
  105.8 2.0 collective-permute-start.4
  111.6 3.8 %collective-permute-done.4 = f32[142336]{0:T(1024)S(1)} collective-permute-done((f32[142336]{0:T(1024)S(1)}, f32[142336]{0:T(1024)S(1)}, u32[]{:S(2)}, u32[]{:S(2)}) %collective-permute-start.4) | collective-permute-done | bytes 569376 | tf_op jit(solution)/shard_map/ppermute | solution.py:25
  124.0 5.4 %collective-permute-start.6 = (f32[13312]{0:T(1024)}, f32[13312]{0:T(1024)}, u32[]{:S(2)}, u32[]{:S(2)}) collective-permute-start(f32[13312]{0:T(1024)} %get-tuple-element.108), channel_id=1, source_target_pairs={{0,3},{1,4},{2,5},{3,6},{4,7},{5,8},{6,9},{7,10},{8,11},{9,12},{10... | collective-permute-start | bytes 159752 | tf_op jit(solution)/shard_map/ppermute | solution.py:25
  129.4 11.7 %collective-permute-start.7 = (f32[13312]{0:T(1024)}, f32[13312]{0:T(1024)}, u32[]{:S(2)}, u32[]{:S(2)}) collective-permute-start(f32[13312]{0:T(1024)} %get-tuple-element.107), channel_id=1, source_target_pairs={{0,125},{1,126},{2,127},{3,0},{4,1},{5,2},{6,3},{7,4},{8,5},{9,6},... | collective-permute-start | bytes 159752 | tf_op jit(solution)/shard_map/ppermute | solution.py:25
  141.6 1.5 collective-permute-done.6
  150.7 4.8 %collective-permute-start.9 = (f32[27,32,32]{2,1,0:T(8,128)}, f32[27,32,32]{2,1,0:T(8,128)}, u32[]{:S(2)}, u32[]{:S(2)}) collective-permute-start(f32[27,32,32]{2,1,0:T(8,128)} %constant_dynamic-update-slice_fusion.7), channel_id=1, source_target_pairs={{0,119},{1,120},{2,121},{3,122},{4,123},{5,124},{6,125},{7,126},{8... | collective-permute-start | bytes 331784 | tf_op jit(solution)/shard_map/ppermute | solution.py:25
  163.0 3.5 %collective-permute-done.8 = f32[27,32,32]{2,1,0:T(8,128)} collective-permute-done((f32[27,32,32]{2,1,0:T(8,128)}, f32[27,32,32]{2,1,0:T(8,128)}, u32[]{:S(2)}, u32[]{:S(2)}) %collective-permute-start.8) | collective-permute-done | bytes 110624 | tf_op jit(solution)/shard_map/ppermute | solution.py:25
  211.4 1.5 copy.255
  212.9 1.5 copy.256
  214.3 1.5 copy.252
  215.8 1.5 copy.257
  217.3 1.5 copy.258
  218.7 1.5 copy.253
  220.2 1.5 copy.254
  221.7 1.3 fusion.248
  223.7 1.4 copy.262
  225.1 1.4 copy.263
  226.5 1.4 copy.259
  227.9 1.4 copy.264
  229.3 1.4 copy.265
  230.7 1.4 copy.260
  232.1 1.4 copy.261
  236.9 1.4 copy.271
  238.2 1.4 copy.272
  239.6 1.4 copy.267
  240.9 1.4 copy.268
  246.4 1.8 fusion.149
  251.8 1.7 bitcast_add_fusion
  253.5 1.5 broadcast_in_dim.47
  (411 shorter events, 104.5 us)
Async XLA Ops:
  3.9 7.0 %copy-start.2 = (f32[8,256,256]{2,1,0:T(8,128)S(1)}, f32[8,256,256]{2,1,0:T(8,128)}, u32[]{:S(2)}) copy-start(f32[8,256,256]{2,1,0:T(8,128)} %param.3) | copy-start | bytes 6291460
  3.9 19.4 %collective-permute-start = (f32[5,256,256]{2,1,0:T(8,128)}, f32[5,256,256]{2,1,0:T(8,128)}, u32[]{:S(2)}, u32[]{:S(2)}) collective-permute-start(f32[5,256,256]{2,1,0:T(8,128)} %pad_maximum_fusion.13), channel_id=1, source_target_pairs={{0,1},{1,2},{2,3},{3,4},{4,5},{5,6},{6,7},{7,8},{8,9},{9,10},{10,1... | collective-permute-start | bytes 3932168 | tf_op jit(solution)/shard_map/ppermute | solution.py:25
  7.1 19.1 %collective-permute-start.1 = (f32[5,256,256]{2,1,0:T(8,128)}, f32[5,256,256]{2,1,0:T(8,128)}, u32[]{:S(2)}, u32[]{:S(2)}) collective-permute-start(f32[5,256,256]{2,1,0:T(8,128)} %pad_maximum_fusion.14), channel_id=1, source_target_pairs={{1,0},{2,1},{3,2},{4,3},{5,4},{6,5},{7,6},{8,7},{9,8},{10,9},{11,1... | collective-permute-start | bytes 3932168 | tf_op jit(solution)/shard_map/ppermute | solution.py:25
  11.1 6.3 %copy-start.54 = (s32[64]{0:T(128)}, s32[64]{0:T(128)S(1)}, u32[]{:S(2)}) copy-start(s32[64]{0:T(128)S(1)} %and_select_fusion.1) | copy-start | bytes 772
  13.4 14.0 %copy-start.23 = (f32[64,2,64]{2,0,1:T(8,128)}, f32[64,2,64]{2,0,1:T(8,128)S(1)}, u32[]{:S(2)}) copy-start(f32[64,2,64]{2,0,1:T(8,128)S(1)} %copy.223) | copy-start | bytes 98308
  14.5 13.2 %copy-start.13 = (f32[128,4,128]{2,0,1:T(8,128)}, f32[128,4,128]{2,0,1:T(8,128)S(1)}, u32[]{:S(2)}) copy-start(f32[128,4,128]{2,0,1:T(8,128)S(1)} %get-tuple-element.122) | copy-start | bytes 786436
  15.0 12.7 %copy-start.30 = (f32[64,2,64]{2,0,1:T(8,128)}, f32[64,2,64]{2,0,1:T(8,128)S(1)}, u32[]{:S(2)}) copy-start(f32[64,2,64]{2,0,1:T(8,128)S(1)} %get-tuple-element.130) | copy-start | bytes 98308
  63.0 7.9 %copy-start.32 = (f32[2,128,128]{2,1,0:T(8,128)S(1)}, f32[2,128,128]{2,1,0:T(8,128)}, u32[]{:S(2)}) copy-start(f32[2,128,128]{2,1,0:T(8,128)} %get-tuple-element.76) | copy-start | bytes 393220
  63.0 8.5 %copy-start.47 = (f32[8192]{0:T(1024)S(1)}, f32[8192]{0:T(1024)}, u32[]{:S(2)}) copy-start(f32[8192]{0:T(1024)} %reshape.709) | copy-start | bytes 98308
  63.0 9.2 %copy-start.8 = (f32[128,4,128]{2,0,1:T(8,128)S(1)}, f32[128,4,128]{2,0,1:T(8,128)}, u32[]{:S(2)}) copy-start(f32[128,4,128]{2,0,1:T(8,128)} %get-tuple-element.126) | copy-start | bytes 786436
  63.0 17.2 %copy-start = (f32[8,256,256]{2,1,0:T(8,128)S(1)}, f32[8,256,256]{2,1,0:T(8,128)}, u32[]{:S(2)}) copy-start(f32[8,256,256]{2,1,0:T(8,128)} %shard_map.41) | copy-start | bytes 6291460
  64.6 13.5 %collective-permute-start.2 = (f32[3,256,256]{2,1,0:T(8,128)S(1)}, f32[3,256,256]{2,1,0:T(8,128)S(1)}, u32[]{:S(2)}, u32[]{:S(2)}) collective-permute-start(f32[3,256,256]{2,1,0:T(8,128)S(1)} %get-tuple-element.41), channel_id=1, source_target_pairs={{0,1},{1,2},{2,3},{3,4},{4,5},{5,6},{6,7},{7,8},{8,9},{9,10},{10,1... | collective-permute-start | bytes 2359304 | tf_op jit(solution)/shard_map/ppermute | solution.py:25
  68.7 11.4 %collective-permute-start.3 = (f32[3,256,256]{2,1,0:T(8,128)S(1)}, f32[3,256,256]{2,1,0:T(8,128)S(1)}, u32[]{:S(2)}, u32[]{:S(2)}) collective-permute-start(f32[3,256,256]{2,1,0:T(8,128)S(1)} %get-tuple-element.42), channel_id=1, source_target_pairs={{1,0},{2,1},{3,2},{4,3},{5,4},{6,5},{7,6},{8,7},{9,8},{10,9},{11,1... | collective-permute-start | bytes 2359304 | tf_op jit(solution)/shard_map/ppermute | solution.py:25
  103.5 12.0 %copy-start.9 = (f32[128,4,128]{2,0,1:T(8,128)S(1)}, f32[128,4,128]{2,0,1:T(8,128)}, u32[]{:S(2)}) copy-start(f32[128,4,128]{2,0,1:T(8,128)} %get-tuple-element.126) | copy-start | bytes 786436
  105.8 9.6 %collective-permute-start.4 = (f32[142336]{0:T(1024)S(1)}, f32[142336]{0:T(1024)S(1)}, u32[]{:S(2)}, u32[]{:S(2)}) collective-permute-start(f32[142336]{0:T(1024)S(1)} %get-tuple-element.115), channel_id=1, source_target_pairs={{0,1},{1,2},{2,3},{3,4},{4,5},{5,6},{6,7},{7,8},{8,9},{9,10},{10,1... | collective-permute-start | bytes 1708040 | tf_op jit(solution)/shard_map/ppermute | solution.py:25
  107.8 7.7 %collective-permute-start.5 = (f32[142336]{0:T(1024)S(1)}, f32[142336]{0:T(1024)S(1)}, u32[]{:S(2)}, u32[]{:S(2)}) collective-permute-start(f32[142336]{0:T(1024)S(1)} %get-tuple-element.116), channel_id=1, source_target_pairs={{0,127},{1,0},{2,1},{3,2},{4,3},{5,4},{6,5},{7,6},{8,7},{9,8},{10,... | collective-permute-start | bytes 1708040 | tf_op jit(solution)/shard_map/ppermute | solution.py:25
  108.8 14.4 %copy-start.37 = (f32[1,32,32]{2,1,0:T(8,128)}, f32[1,32,32]{2,1,0:T(8,128)S(1)}, u32[]{:S(2)}) copy-start(f32[1,32,32]{2,1,0:T(8,128)S(1)} %copy.225) | copy-start | bytes 12292
  108.9 14.3 %copy-start.35 = (f32[1,32,32]{2,1,0:T(8,128)}, f32[1,32,32]{2,1,0:T(8,128)S(1)}, u32[]{:S(2)}) copy-start(f32[1,32,32]{2,1,0:T(8,128)S(1)} %copy.227) | copy-start | bytes 12292
  122.3 18.8 %copy-start.29 = (f32[142336]{0:T(1024)S(1)}, f32[142336]{0:T(1024)}, u32[]{:S(2)}) copy-start(f32[142336]{0:T(1024)} %copy-done.28) | copy-start | bytes 1708036
  122.3 19.1 %copy-start.31 = (f32[64,2,64]{2,0,1:T(8,128)S(1)}, f32[64,2,64]{2,0,1:T(8,128)}, u32[]{:S(2)}) copy-start(f32[64,2,64]{2,0,1:T(8,128)} %copy-done.30) | copy-start | bytes 98308
  122.3 19.1 %copy-start.62 = (f32[6]{0:T(128)S(1)}, f32[6]{0:T(128)}, u32[]{:S(2)}) copy-start(f32[6]{0:T(128)} %and_convert_fusion.2) | copy-start | bytes 76
  123.0 34.2 %copy-start.6 = (f32[2,6,128,128]{3,2,1,0:T(8,128)}, f32[2,6,128,128]{3,2,1,0:T(8,128)S(1)}, u32[]{:S(2)}) copy-start(f32[2,6,128,128]{3,2,1,0:T(8,128)S(1)} %fusion.28) | copy-start | bytes 2359300
  123.0 33.3 %copy-start.24 = (f32[64,2,64]{2,0,1:T(8,128)S(1)}, f32[64,2,64]{2,0,1:T(8,128)}, u32[]{:S(2)}) copy-start(f32[64,2,64]{2,0,1:T(8,128)} %copy-done.23) | copy-start | bytes 98308
  123.0 34.1 %copy-start.59 = (f32[8]{0:T(128)S(1)}, f32[8]{0:T(128)}, u32[]{:S(2)}) copy-start(f32[8]{0:T(128)} %get-tuple-element.132) | copy-start | bytes 100
  124.0 19.2 %collective-permute-start.6 = (f32[13312]{0:T(1024)}, f32[13312]{0:T(1024)}, u32[]{:S(2)}, u32[]{:S(2)}) collective-permute-start(f32[13312]{0:T(1024)} %get-tuple-element.108), channel_id=1, source_target_pairs={{0,3},{1,4},{2,5},{3,6},{4,7},{5,8},{6,9},{7,10},{8,11},{9,12},{10... | collective-permute-start | bytes 159752 | tf_op jit(solution)/shard_map/ppermute | solution.py:25
  129.4 19.8 %collective-permute-start.7 = (f32[13312]{0:T(1024)}, f32[13312]{0:T(1024)}, u32[]{:S(2)}, u32[]{:S(2)}) collective-permute-start(f32[13312]{0:T(1024)} %get-tuple-element.107), channel_id=1, source_target_pairs={{0,125},{1,126},{2,127},{3,0},{4,1},{5,2},{6,3},{7,4},{8,5},{9,6},... | collective-permute-start | bytes 159752 | tf_op jit(solution)/shard_map/ppermute | solution.py:25
  141.5 16.7 %copy-start.10 = (f32[1,6,64,64]{3,2,1,0:T(8,128)}, f32[1,6,64,64]{3,2,1,0:T(8,128)S(1)}, u32[]{:S(2)}) copy-start(f32[1,6,64,64]{3,2,1,0:T(8,128)S(1)} %get-tuple-element.120) | copy-start | bytes 294916
  150.7 15.8 %collective-permute-start.8 = (f32[27,32,32]{2,1,0:T(8,128)}, f32[27,32,32]{2,1,0:T(8,128)}, u32[]{:S(2)}, u32[]{:S(2)}) collective-permute-start(f32[27,32,32]{2,1,0:T(8,128)} %constant_dynamic-update-slice_fusion.7), channel_id=1, source_target_pairs={{0,9},{1,10},{2,11},{3,12},{4,13},{5,14},{6,15},{7,16},{8,17},{9,1... | collective-permute-start | bytes 331784 | tf_op jit(solution)/shard_map/ppermute | solution.py:25
  150.7 17.0 %collective-permute-start.9 = (f32[27,32,32]{2,1,0:T(8,128)}, f32[27,32,32]{2,1,0:T(8,128)}, u32[]{:S(2)}, u32[]{:S(2)}) collective-permute-start(f32[27,32,32]{2,1,0:T(8,128)} %constant_dynamic-update-slice_fusion.7), channel_id=1, source_target_pairs={{0,119},{1,120},{2,121},{3,122},{4,123},{5,124},{6,125},{7,126},{8... | collective-permute-start | bytes 331784 | tf_op jit(solution)/shard_map/ppermute | solution.py:25
  158.1 9.5 %copy-start.38 = (f32[1,32,32]{2,1,0:T(8,128)S(1)}, f32[1,32,32]{2,1,0:T(8,128)}, u32[]{:S(2)}) copy-start(f32[1,32,32]{2,1,0:T(8,128)} %copy-done.37) | copy-start | bytes 12292
  158.1 9.5 %copy-start.40 = (f32[1,32,32]{2,1,0:T(8,128)S(1)}, f32[1,32,32]{2,1,0:T(8,128)}, u32[]{:S(2)}) copy-start(f32[1,32,32]{2,1,0:T(8,128)} %copy.226) | copy-start | bytes 12292
  158.1 9.5 %copy-start.36 = (f32[1,32,32]{2,1,0:T(8,128)S(1)}, f32[1,32,32]{2,1,0:T(8,128)}, u32[]{:S(2)}) copy-start(f32[1,32,32]{2,1,0:T(8,128)} %copy-done.35) | copy-start | bytes 12292
  158.2 10.5 %copy-start.61 = (f32[27]{0:T(128)S(1)}, f32[27]{0:T(128)}, u32[]{:S(2)}) copy-start(f32[27]{0:T(128)} %and_convert_fusion.4) | copy-start | bytes 328
  158.5 10.4 %copy-start.16 = (f32[2,4,64,64]{3,2,1,0:T(8,128)}, f32[2,4,64,64]{3,2,1,0:T(8,128)S(1)}, u32[]{:S(2)}) copy-start(f32[2,4,64,64]{3,2,1,0:T(8,128)S(1)} %fusion.94) | copy-start | bytes 393220
  175.3 18.6 %slice-start.5 = ((f32[5,32,32]{2,1,0:T(8,128)}), f32[3,32,32]{2,1,0:T(8,128)S(1)}, s32[]{:S(2)}) async-start(f32[5,32,32]{2,1,0:T(8,128)} %copy-done.34), calls=%async_computation.5 | async-start | bytes 98304 | tf_op jit(solution)/shard_map/vmap()/slice | solution.py:129
  175.3 18.6 %copy-start.41 = (f32[3,32,32]{2,1,0:T(8,128)S(1)}, f32[3,32,32]{2,1,0:T(8,128)}, u32[]{:S(2)}) copy-start(f32[3,32,32]{2,1,0:T(8,128)} %slice.1396) | copy-start | bytes 36868
  175.3 18.6 %copy-start.42 = (f32[3,32,32]{2,1,0:T(8,128)S(1)}, f32[3,32,32]{2,1,0:T(8,128)}, u32[]{:S(2)}) copy-start(f32[3,32,32]{2,1,0:T(8,128)} %slice.1385) | copy-start | bytes 36868
  175.3 18.6 %copy-start.43 = (f32[3,32,32]{2,1,0:T(8,128)S(1)}, f32[3,32,32]{2,1,0:T(8,128)}, u32[]{:S(2)}) copy-start(f32[3,32,32]{2,1,0:T(8,128)} %slice.1397) | copy-start | bytes 36868
  176.5 19.6 %copy-start.60 = (s32[1,3]{1,0:T(1,128)S(1)}, s32[1,3]{1,0:T(1,128)}, u32[]{:S(2)}) copy-start(s32[1,3]{1,0:T(1,128)} %pad_bitcast_fusion) | copy-start | bytes 40
  198.2 12.4 %copy-start.11 = (f32[2,13,16,16]{3,2,1,0:T(8,128)}, f32[2,13,16,16]{3,2,1,0:T(8,128)S(1)}, u32[]{:S(2)}) copy-start(f32[2,13,16,16]{3,2,1,0:T(8,128)S(1)} %fusion.17) | copy-start | bytes 79876
  210.7 37.8 %copy-start.7 = (f32[2,6,128,128]{3,2,1,0:T(8,128)S(1)}, f32[2,6,128,128]{3,2,1,0:T(8,128)}, u32[]{:S(2)}) copy-start(f32[2,6,128,128]{3,2,1,0:T(8,128)} %copy-done.6) | copy-start | bytes 2359300
  210.8 37.8 %slice-start = ((f32[2,6,128,128]{3,2,1,0:T(8,128)}), f32[2,4,128,128]{3,2,1,0:T(8,128)S(1)}, s32[]{:S(2)}) async-start(f32[2,6,128,128]{3,2,1,0:T(8,128)} %copy-done.6), calls=%async_computation | async-start | bytes 1048576 | tf_op jit(solution)/shard_map/vmap()/slice | solution.py:141
  223.6 24.5 %copy-start.53 = (s32[128]{0:T(128)S(1)}, s32[128]{0:T(128)}, u32[]{:S(2)}) copy-start(s32[128]{0:T(128)} %copy-done.51) | copy-start | bytes 1540
  223.6 24.9 %copy-start.50 = (s32[256]{0:T(256)S(1)}, s32[256]{0:T(256)}, u32[]{:S(2)}) copy-start(s32[256]{0:T(256)} %copy-done.48) | copy-start | bytes 3076
  242.3 6.3 %copy-start.19 = (f32[4,128,128]{2,1,0:T(8,128)S(1)}, f32[4,128,128]{2,1,0:T(8,128)}, u32[]{:S(2)}) copy-start(f32[4,128,128]{2,1,0:T(8,128)} %slice.1486) | copy-start | bytes 786436
  242.3 6.3 %copy-start.20 = (f32[4,128,128]{2,1,0:T(8,128)S(1)}, f32[4,128,128]{2,1,0:T(8,128)}, u32[]{:S(2)}) copy-start(f32[4,128,128]{2,1,0:T(8,128)} %slice.1487) | copy-start | bytes 786436
  242.3 6.3 %copy-start.21 = (f32[4,128,128]{2,1,0:T(8,128)S(1)}, f32[4,128,128]{2,1,0:T(8,128)}, u32[]{:S(2)}) copy-start(f32[4,128,128]{2,1,0:T(8,128)} %get-tuple-element.52) | copy-start | bytes 786436
  242.3 6.3 %copy-start.22 = (f32[4,128,128]{2,1,0:T(8,128)S(1)}, f32[4,128,128]{2,1,0:T(8,128)}, u32[]{:S(2)}) copy-start(f32[4,128,128]{2,1,0:T(8,128)} %get-tuple-element.53) | copy-start | bytes 786436
  (31 other events, 101.2 us)

commit v4 on v3

--- a/solution.py
+++ b/solution.py
@@ -373,13 +373,10 @@
         summed = refine(summed) + smooth(r1e, co1, SWEEPS)
         return refine(summed)
 
-    coarse = jax.vmap(coarse_part)(
-        jnp.stack([parts[0][0], parts[1][0]]),
-        jnp.stack([parts[0][1], parts[1][1]]),
-        jnp.stack(windows[:2]),
-    )
-    pressure = (fine_0 + fine_1) + coarse[0]
-    return (pressure, coarse[1])
+    coarse_0 = coarse_part(parts[0][0], parts[0][1], windows[0])
+    coarse_1 = coarse_part(parts[1][0], parts[1][1], windows[1])
+    pressure = (fine_0 + fine_1) + coarse_0
+    return (pressure, coarse_1)
 
 
 def solution(mesh):

time: 258 us -> 217 us (0.84)
  local copies, waits for them, and re-layouts: 108 us -> 45.5 us
  other arithmetic: 36.2 us -> 47.5 us
  matrix products: 17.8 us -> 27.7 us
    slice x86 -> x0, local copies, waits for them, and re-layouts: 57 us -> none  [the longest x13 9.28 us: smooth(): update = (1.0 - OMEGA) * inner + co['w'][lo:hi] * (resid[lo:hi] + off)]
    mul x19 -> x0, local copies, waits for them, and re-layouts: 14.9 us -> none  [the longest x3 2.57 us: smooth(): kxo[lo - 1:hi - 1] * update[:-2] + kxo[lo:hi] * update[2:]]
    mul x4 -> x8, other arithmetic: 0.2 us -> 5.35 us  [smooth(): update = co['w'] * resid]
    reduce_sum x6 -> x7, other arithmetic: 2.43 us -> 7.51 us  [coarsen(): planes = field.reshape(extent_x // 2, 2, extent_y, extent_z).sum(axis=1)]
    dot_general x11 -> x12, matrix products: 4.44 us -> 8.78 us  [shrink_sides(): jnp.einsum('xyz,zw->xyw', field, pair_matrix(extent_z), precision=EXACT)]
    unnamed x155 -> x253, local copies, waits for them, and re-layouts: 10.5 us -> 14.8 us
    reshape x8 -> x12, local copies, waits for them, and re-layouts: 0.62 us -> 3.44 us  [split(): out.append(flat[at:at + size].reshape(shape))]
    dot_general x4 -> x8, matrix products: 3.49 us -> 5.99 us  [grow_sides(): jnp.einsum('xvz,yv->xyz', along_z, pair_matrix(2 * extent_y), precision=E...]
  transfers between devices with their start and end apart: 10 -> 10, of which waited for: 7 -> 6; matrix products, arithmetic and copies ran while one was open for 12% -> 13% of each run, Pallas kernels for 0% -> 0%
where the time goes in v4:
time: 217 us; the launch traced here: 215 us
  other arithmetic  47.5 us (22%)
  local copies, waits for them, and re-layouts  45.5 us (21%)
  starting transfers between devices  35.2 us (16%)
  Pallas kernels  32.5 us (15%)
  matrix products  27.7 us (13%)
  waiting for transfers between devices  24 us (11%)
  between operations  3.09 us (1%)
    ppermute x10, starting transfers between devices, recv(): return lax.ppermute(value, 'gx', pairs)  35.2 us
    pallas_call x2, Pallas kernels, _vmem_call(): pl.pallas_call(kernel, out_shape=outs, in_specs=[pl.BlockSpec(memory_spac...  32.5 us
    ppermute x10, waiting for transfers between devices, recv(): return lax.ppermute(value, 'gx', pairs)  24 us
    unnamed x253, local copies, waits for them, and re-layouts  14.8 us
    dot_general x12, matrix products, shrink_sides(): jnp.einsum('xyz,zw->xyw', field, pair_matrix(extent_z), precision=EXACT)  8.78 us
    div x1, other arithmetic, make_coefs(): OMEGA / diag  7.6 us
    reduce_sum x7, other arithmetic, coarsen(): planes = field.reshape(extent_x // 2, 2, extent_y, extent_z).sum(axis=1)  7.51 us
    div x5, other arithmetic, make_coefs(): faces = [two_s / (safe + jnp.where(nb > 0, nb, safe)) for nb in near]  7.42 us
  transfers between devices with their start and end apart: 10, of which 6 were waited for; matrix products, arithmetic and copies ran while one was open for 13% of the time, Pallas kernels for 0%

profile of v4, /device:TPU:48, one launch (start us, length us, event | category | flops | bytes accessed | tf_op | source)
XLA Modules:
  0.0 215.5 jit_solution(4161833914545267381)
XLA Ops:
  0.6 1.6 fusion.599
  2.8 1.2 pad_maximum_fusion.12
  3.9 2.0 collective-permute-start
  6.0 1.2 pad_maximum_fusion.13
  7.1 3.6 %collective-permute-start.1 = (f32[5,256,256]{2,1,0:T(8,128)}, f32[5,256,256]{2,1,0:T(8,128)}, u32[]{:S(2)}, u32[]{:S(2)}) collective-permute-start(f32[5,256,256]{2,1,0:T(8,128)} %pad_maximum_fusion.13), channel_id=1, source_target_pairs={{1,0},{2,1},{3,2},{4,3},{5,4},{6,5},{7,6},{8,7},{9,8},{10,9},{11,1... | collective-permute-start | bytes 3932168 | tf_op jit(solution)/shard_map/ppermute | solution.py:25
  11.8 1.1 bitcast_reduce_fusion.3
  19.2 4.1 %collective-permute-done = f32[5,256,256]{2,1,0:T(8,128)} collective-permute-done((f32[5,256,256]{2,1,0:T(8,128)}, f32[5,256,256]{2,1,0:T(8,128)}, u32[]{:S(2)}, u32[]{:S(2)}) %collective-permute-start) | collective-permute-done | bytes 1310752 | tf_op jit(solution)/shard_map/ppermute | solution.py:25
  23.3 1.2 slice.1729
  24.5 1.7 collective-permute-done.1
  26.2 1.2 slice.1730
  28.8 7.6 %broadcast_divide_fusion = (f32[12,256,256]{2,1,0:T(8,128)}, f32[12,256,256]{2,1,0:T(8,128)}, f32[12,256,256]{2,1,0:T(8,128)}) fusion(f32[12,258,1]{2,1,0:T(8,128)S(1)} %get-tuple-element.32, f32[12,1,256]{2,1,0:T(1,128)S(1)} %get-tuple-element.30, f32[12,256,256]{2,1,0:T(8,128)S(1)} %slice.1734, f32[12,1,256]{2,1,0:T(1,128)S(1)} %get-tuple-element.31, ...), kind=kLoop, calls=%fused_computation.41 | loop fusion | flops 33030144 | bytes 22069440 | tf_op jit(solution)/shard_map/div | solution.py:120
  36.4 5.7 %fusion.13 = (f32[12,256,256]{2,1,0:T(8,128)}, f32[12,256,256]{2,1,0:T(8,128)}, f32[12,256,256]{2,1,0:T(8,128)}) fusion(f32[12,258,1]{2,1,0:T(8,128)S(1)} %get-tuple-element.32, f32[12,1,256]{2,1,0:T(1,128)S(1)} %get-tuple-element.30, f32[12,256,256]{2,1,0:T(8,128)S(1)} %slice.1734, f32[12,1,256]{2,1,0:T(1,128)S(1)} %get-tuple-element.31, ...), kind=kLoop, calls=%fused_computation.24 | loop fusion | flops 16515072 | bytes 12632256 | tf_op jit(solution)/shard_map/div | solution.py:109
  42.9 1.8 slice.1733.kxo
  44.7 1.9 slice.1727
  46.5 1.1 slice.1728
  47.6 1.9 pad_maximum_fusion.11.resid.rhs
  49.6 13.3 %shard_map.41 = f32[8,256,256]{2,1,0:T(8,128)} custom-call(f32[12,256,256]{2,1,0:T(8,128)} %pad_maximum_fusion.11.resid.rhs, f32[11,256,256]{2,1,0:T(8,128)} %slice.1733.kxo, f32[12,256,256]{2,1,0:T(8,128)} %get-tuple-element.36.kyl, f32[12,256,256]{2,1,0:T(8,128)} %get-tuple-element.37.kyh, f32[12,256,256]{2,1,0:T(8,128)} %get-tuple-element.35.kzl, ...), custom_call_target="tpu_custom_call" | custom-call | tf_op jit(solution)/shard_map/pallas_call | solution.py:265
  62.9 1.6 fusion.598
  64.5 4.1 %collective-permute-start.2 = (f32[3,256,256]{2,1,0:T(8,128)S(1)}, f32[3,256,256]{2,1,0:T(8,128)S(1)}, u32[]{:S(2)}, u32[]{:S(2)}) collective-permute-start(f32[3,256,256]{2,1,0:T(8,128)S(1)} %get-tuple-element.38), channel_id=1, source_target_pairs={{0,1},{1,2},{2,3},{3,4},{4,5},{5,6},{6,7},{7,8},{8,9},{9,10},{10,1... | collective-permute-start | bytes 2359304 | tf_op jit(solution)/shard_map/ppermute | solution.py:25
  68.6 2.1 collective-permute-start.3
  74.1 3.9 %collective-permute-done.2 = f32[3,256,256]{2,1,0:T(8,128)S(1)} collective-permute-done((f32[3,256,256]{2,1,0:T(8,128)S(1)}, f32[3,256,256]{2,1,0:T(8,128)S(1)}, u32[]{:S(2)}, u32[]{:S(2)}) %collective-permute-start.2) | collective-permute-done | bytes 786464 | tf_op jit(solution)/shard_map/ppermute | solution.py:25
  78.0 2.0 collective-permute-done.3
  80.1 2.1 pad_maximum_fusion.1.fine_ext
  82.2 19.2 %shard_map.42 = (f32[8,256,256]{2,1,0:T(8,128)}, f32[8,256,256]{2,1,0:T(8,128)}) custom-call(f32[14,256,256]{2,1,0:T(8,128)} %pad_maximum_fusion.1.fine_ext, f32[12,256,256]{2,1,0:T(8,128)} %pad_maximum_fusion.11.resid.rhs, f32[13,256,256]{2,1,0:T(8,128)} %copy-done.3, f32[12,256,256]{2,1,0:T(8,128)} %get-tuple-element.36.kyl, ...), custom_call_target="tpu_custom_call" | custom-call | tf_op jit(solution)/shard_map/pallas_call | solution.py:265
  101.4 2.0 bitcast_reduce_fusion.1
  106.0 2.0 collective-permute-start.4
  110.3 5.3 %collective-permute-done.4 = f32[142336]{0:T(1024)S(1)} collective-permute-done((f32[142336]{0:T(1024)S(1)}, f32[142336]{0:T(1024)S(1)}, u32[]{:S(2)}, u32[]{:S(2)}) %collective-permute-start.4) | collective-permute-done | bytes 569376 | tf_op jit(solution)/shard_map/ppermute | solution.py:25
  126.7 4.6 %collective-permute-start.6 = (f32[13312]{0:T(1024)}, f32[13312]{0:T(1024)}, u32[]{:S(2)}, u32[]{:S(2)}) collective-permute-start(f32[13312]{0:T(1024)} %get-tuple-element.85), channel_id=1, source_target_pairs={{0,3},{1,4},{2,5},{3,6},{4,7},{5,8},{6,9},{7,10},{8,11},{9,12},{10... | collective-permute-start | bytes 159752 | tf_op jit(solution)/shard_map/ppermute | solution.py:25
  131.3 11.7 %collective-permute-start.7 = (f32[13312]{0:T(1024)}, f32[13312]{0:T(1024)}, u32[]{:S(2)}, u32[]{:S(2)}) collective-permute-start(f32[13312]{0:T(1024)} %get-tuple-element.84), channel_id=1, source_target_pairs={{0,125},{1,126},{2,127},{3,0},{4,1},{5,2},{6,3},{7,4},{8,5},{9,6},... | collective-permute-start | bytes 159752 | tf_op jit(solution)/shard_map/ppermute | solution.py:25
  153.7 4.8 %collective-permute-start.9 = (f32[27,32,32]{2,1,0:T(8,128)}, f32[27,32,32]{2,1,0:T(8,128)}, u32[]{:S(2)}, u32[]{:S(2)}) collective-permute-start(f32[27,32,32]{2,1,0:T(8,128)} %constant_dynamic-update-slice_fusion.7), channel_id=1, source_target_pairs={{0,119},{1,120},{2,121},{3,122},{4,123},{5,124},{6,125},{7,126},{8... | collective-permute-start | bytes 331784 | tf_op jit(solution)/shard_map/ppermute | solution.py:25
  160.7 1.3 fusion.590
  162.6 6.8 %collective-permute-done.8 = f32[27,32,32]{2,1,0:T(8,128)} collective-permute-done((f32[27,32,32]{2,1,0:T(8,128)}, f32[27,32,32]{2,1,0:T(8,128)}, u32[]{:S(2)}, u32[]{:S(2)}) %collective-permute-start.8) | collective-permute-done | bytes 110624 | tf_op jit(solution)/shard_map/ppermute | solution.py:25
  172.7 1.1 fusion.601
  174.5 1.8 reduce_sum.117
  176.3 1.5 fusion.539
  182.4 1.8 reduce_sum.119
  184.3 1.7 fusion.534
  186.1 1.2 fusion.199
  187.4 1.9 slice_multiply_fusion.14
  193.7 1.3 fusion.284
  195.9 1.6 convolution_bitcast_fusion
  198.5 1.7 reduce_sum.118
  200.3 1.6 fusion.537
  202.8 1.1 fusion.241
  207.8 1.2 fusion.25
  209.5 1.3 fusion.267
  212.3 1.7 bitcast_add_fusion
  214.0 1.5 broadcast_in_dim.38
  (440 shorter events, 63.0 us)
Async XLA Ops:
  3.9 19.4 %collective-permute-start = (f32[5,256,256]{2,1,0:T(8,128)}, f32[5,256,256]{2,1,0:T(8,128)}, u32[]{:S(2)}, u32[]{:S(2)}) collective-permute-start(f32[5,256,256]{2,1,0:T(8,128)} %pad_maximum_fusion.12), channel_id=1, source_target_pairs={{0,1},{1,2},{2,3},{3,4},{4,5},{5,6},{6,7},{7,8},{8,9},{9,10},{10,1... | collective-permute-start | bytes 3932168 | tf_op jit(solution)/shard_map/ppermute | solution.py:25
  7.1 19.1 %collective-permute-start.1 = (f32[5,256,256]{2,1,0:T(8,128)}, f32[5,256,256]{2,1,0:T(8,128)}, u32[]{:S(2)}, u32[]{:S(2)}) collective-permute-start(f32[5,256,256]{2,1,0:T(8,128)} %pad_maximum_fusion.13), channel_id=1, source_target_pairs={{1,0},{2,1},{3,2},{4,3},{5,4},{6,5},{7,6},{8,7},{9,8},{10,9},{11,1... | collective-permute-start | bytes 3932168 | tf_op jit(solution)/shard_map/ppermute | solution.py:25
  13.4 14.0 %copy-start.49 = (f32[64,2,64]{2,0,1:T(8,128)}, f32[64,2,64]{2,0,1:T(8,128)S(1)}, u32[]{:S(2)}) copy-start(f32[64,2,64]{2,0,1:T(8,128)S(1)} %copy.81) | copy-start | bytes 98308
  14.5 13.2 %copy-start.29 = (f32[128,4,128]{2,0,1:T(8,128)}, f32[128,4,128]{2,0,1:T(8,128)S(1)}, u32[]{:S(2)}) copy-start(f32[128,4,128]{2,0,1:T(8,128)S(1)} %get-tuple-element.95) | copy-start | bytes 786436
  15.6 12.1 %copy-start.63 = (f32[2,64,64]{2,1,0:T(8,128)}, f32[2,64,64]{2,1,0:T(8,128)S(1)}, u32[]{:S(2)}) copy-start(f32[2,64,64]{2,1,0:T(8,128)S(1)} %get-tuple-element.103) | copy-start | bytes 98308
  62.9 9.3 %copy-start.102 = (f32[64,64]{1,0:T(8,128)S(1)}, f32[64,64]{1,0:T(8,128)}, u32[]{:S(2)}) copy-start(f32[64,64]{1,0:T(8,128)} %get-tuple-element.102) | copy-start | bytes 49156
  62.9 10.4 %copy-start.17 = (f32[128,4,128]{2,0,1:T(8,128)S(1)}, f32[128,4,128]{2,0,1:T(8,128)}, u32[]{:S(2)}) copy-start(f32[128,4,128]{2,0,1:T(8,128)} %get-tuple-element.99) | copy-start | bytes 786436
  62.9 17.2 %copy-start = (f32[8,256,256]{2,1,0:T(8,128)S(1)}, f32[8,256,256]{2,1,0:T(8,128)}, u32[]{:S(2)}) copy-start(f32[8,256,256]{2,1,0:T(8,128)} %shard_map.41) | copy-start | bytes 6291460
  64.5 13.5 %collective-permute-start.2 = (f32[3,256,256]{2,1,0:T(8,128)S(1)}, f32[3,256,256]{2,1,0:T(8,128)S(1)}, u32[]{:S(2)}, u32[]{:S(2)}) collective-permute-start(f32[3,256,256]{2,1,0:T(8,128)S(1)} %get-tuple-element.38), channel_id=1, source_target_pairs={{0,1},{1,2},{2,3},{3,4},{4,5},{5,6},{6,7},{7,8},{8,9},{9,10},{10,1... | collective-permute-start | bytes 2359304 | tf_op jit(solution)/shard_map/ppermute | solution.py:25
  68.6 11.4 %collective-permute-start.3 = (f32[3,256,256]{2,1,0:T(8,128)S(1)}, f32[3,256,256]{2,1,0:T(8,128)S(1)}, u32[]{:S(2)}, u32[]{:S(2)}) collective-permute-start(f32[3,256,256]{2,1,0:T(8,128)S(1)} %get-tuple-element.39), channel_id=1, source_target_pairs={{1,0},{2,1},{3,2},{4,3},{5,4},{6,5},{7,6},{8,7},{9,8},{10,9},{11,1... | collective-permute-start | bytes 2359304 | tf_op jit(solution)/shard_map/ppermute | solution.py:25
  103.4 13.0 %copy-start.18 = (f32[128,4,128]{2,0,1:T(8,128)S(1)}, f32[128,4,128]{2,0,1:T(8,128)}, u32[]{:S(2)}) copy-start(f32[128,4,128]{2,0,1:T(8,128)} %get-tuple-element.99) | copy-start | bytes 786436
  106.0 9.6 %collective-permute-start.4 = (f32[142336]{0:T(1024)S(1)}, f32[142336]{0:T(1024)S(1)}, u32[]{:S(2)}, u32[]{:S(2)}) collective-permute-start(f32[142336]{0:T(1024)S(1)} %get-tuple-element.92), channel_id=1, source_target_pairs={{0,1},{1,2},{2,3},{3,4},{4,5},{5,6},{6,7},{7,8},{8,9},{9,10},{10,1... | collective-permute-start | bytes 1708040 | tf_op jit(solution)/shard_map/ppermute | solution.py:25
  107.9 8.5 %collective-permute-start.5 = (f32[142336]{0:T(1024)S(1)}, f32[142336]{0:T(1024)S(1)}, u32[]{:S(2)}, u32[]{:S(2)}) collective-permute-start(f32[142336]{0:T(1024)S(1)} %get-tuple-element.93), channel_id=1, source_target_pairs={{0,127},{1,0},{2,1},{3,2},{4,3},{5,4},{6,5},{7,6},{8,7},{9,8},{10,... | collective-permute-start | bytes 1708040 | tf_op jit(solution)/shard_map/ppermute | solution.py:25
  109.0 40.7 %copy-start.78 = (f32[1,32,32]{2,1,0:T(8,128)}, f32[1,32,32]{2,1,0:T(8,128)S(1)}, u32[]{:S(2)}) copy-start(f32[1,32,32]{2,1,0:T(8,128)S(1)} %copy.83) | copy-start | bytes 12292
  110.3 40.0 %copy-start.80 = (f32[1,32,32]{2,1,0:T(8,128)}, f32[1,32,32]{2,1,0:T(8,128)S(1)}, u32[]{:S(2)}) copy-start(f32[1,32,32]{2,1,0:T(8,128)S(1)} %copy.84) | copy-start | bytes 12292
  117.5 25.7 %copy-start.6 = (f32[8,128,128]{2,1,0:T(8,128)}, f32[8,128,128]{2,1,0:T(8,128)S(1)}, u32[]{:S(2)}) copy-start(f32[8,128,128]{2,1,0:T(8,128)S(1)} %get-tuple-element.62) | copy-start | bytes 1572868
  119.8 23.3 %copy-start.9 = (f32[8,128,128]{2,1,0:T(8,128)}, f32[8,128,128]{2,1,0:T(8,128)S(1)}, u32[]{:S(2)}) copy-start(f32[8,128,128]{2,1,0:T(8,128)S(1)} %get-tuple-element.9) | copy-start | bytes 1572868
  119.9 23.0 %copy-start.30 = (f32[128,4,128]{2,0,1:T(8,128)S(1)}, f32[128,4,128]{2,0,1:T(8,128)}, u32[]{:S(2)}) copy-start(f32[128,4,128]{2,0,1:T(8,128)} %copy-done.29) | copy-start | bytes 786436
  126.0 17.1 %copy-start.13 = (f32[8,128,128]{2,1,0:T(8,128)S(1)}, f32[8,128,128]{2,1,0:T(8,128)}, u32[]{:S(2)}) copy-start(f32[8,128,128]{2,1,0:T(8,128)} %copy-done.12) | copy-start | bytes 1572868
  126.7 20.8 %collective-permute-start.6 = (f32[13312]{0:T(1024)}, f32[13312]{0:T(1024)}, u32[]{:S(2)}, u32[]{:S(2)}) collective-permute-start(f32[13312]{0:T(1024)} %get-tuple-element.85), channel_id=1, source_target_pairs={{0,3},{1,4},{2,5},{3,6},{4,7},{5,8},{6,9},{7,10},{8,11},{9,12},{10... | collective-permute-start | bytes 159752 | tf_op jit(solution)/shard_map/ppermute | solution.py:25
  131.3 20.9 %collective-permute-start.7 = (f32[13312]{0:T(1024)}, f32[13312]{0:T(1024)}, u32[]{:S(2)}, u32[]{:S(2)}) collective-permute-start(f32[13312]{0:T(1024)} %get-tuple-element.84), channel_id=1, source_target_pairs={{0,125},{1,126},{2,127},{3,0},{4,1},{5,2},{6,3},{7,4},{8,5},{9,6},... | collective-permute-start | bytes 159752 | tf_op jit(solution)/shard_map/ppermute | solution.py:25
  143.2 16.1 %copy-start.50 = (f32[64,2,64]{2,0,1:T(8,128)S(1)}, f32[64,2,64]{2,0,1:T(8,128)}, u32[]{:S(2)}) copy-start(f32[64,2,64]{2,0,1:T(8,128)} %copy-done.49) | copy-start | bytes 98308
  144.3 16.3 %copy-start.31 = (f32[6,128,128]{2,1,0:T(8,128)}, f32[6,128,128]{2,1,0:T(8,128)S(1)}, u32[]{:S(2)}) copy-start(f32[6,128,128]{2,1,0:T(8,128)S(1)} %fusion.53) | copy-start | bytes 1179652
  146.1 14.6 %copy-start.105 = (f32[6]{0:T(128)S(1)}, f32[6]{0:T(128)}, u32[]{:S(2)}) copy-start(f32[6]{0:T(128)} %and_convert_fusion.2) | copy-start | bytes 76
  148.3 12.3 %copy-start.42 = (f32[9,32,32]{2,1,0:T(8,128)}, f32[9,32,32]{2,1,0:T(8,128)S(1)}, u32[]{:S(2)}) copy-start(f32[9,32,32]{2,1,0:T(8,128)S(1)} %reshape.493) | copy-start | bytes 110596
  153.7 15.8 %collective-permute-start.8 = (f32[27,32,32]{2,1,0:T(8,128)}, f32[27,32,32]{2,1,0:T(8,128)}, u32[]{:S(2)}, u32[]{:S(2)}) collective-permute-start(f32[27,32,32]{2,1,0:T(8,128)} %constant_dynamic-update-slice_fusion.7), channel_id=1, source_target_pairs={{0,9},{1,10},{2,11},{3,12},{4,13},{5,14},{6,15},{7,16},{8,17},{9,1... | collective-permute-start | bytes 331784 | tf_op jit(solution)/shard_map/ppermute | solution.py:25
  153.7 17.0 %collective-permute-start.9 = (f32[27,32,32]{2,1,0:T(8,128)}, f32[27,32,32]{2,1,0:T(8,128)}, u32[]{:S(2)}, u32[]{:S(2)}) collective-permute-start(f32[27,32,32]{2,1,0:T(8,128)} %constant_dynamic-update-slice_fusion.7), channel_id=1, source_target_pairs={{0,119},{1,120},{2,121},{3,122},{4,123},{5,124},{6,125},{7,126},{8... | collective-permute-start | bytes 331784 | tf_op jit(solution)/shard_map/ppermute | solution.py:25
  162.2 9.5 %copy-start.52 = (f32[6,64,64]{2,1,0:T(8,128)}, f32[6,64,64]{2,1,0:T(8,128)S(1)}, u32[]{:S(2)}) copy-start(f32[6,64,64]{2,1,0:T(8,128)S(1)} %get-tuple-element.27) | copy-start | bytes 294916
  162.3 9.5 %copy-start.106 = (f32[27]{0:T(128)S(1)}, f32[27]{0:T(128)}, u32[]{:S(2)}) copy-start(f32[27]{0:T(128)} %and_convert_fusion.4) | copy-start | bytes 328
  162.4 9.5 %copy-start.75 = (f32[4,64,64]{2,1,0:T(8,128)}, f32[4,64,64]{2,1,0:T(8,128)S(1)}, u32[]{:S(2)}) copy-start(f32[4,64,64]{2,1,0:T(8,128)S(1)} %fusion.168) | copy-start | bytes 196612
  181.5 12.2 %slice-start.8 = ((f32[4,64,64]{2,1,0:T(8,128)}), f32[2,64,64]{2,1,0:T(8,128)S(1)}, s32[]{:S(2)}) async-start(f32[4,64,64]{2,1,0:T(8,128)} %copy-done.75), calls=%async_computation.8 | async-start | bytes 131072 | tf_op jit(solution)/shard_map/slice | solution.py:141
  184.2 9.5 %copy-start.76 = (f32[4,64,64]{2,1,0:T(8,128)S(1)}, f32[4,64,64]{2,1,0:T(8,128)}, u32[]{:S(2)}) copy-start(f32[4,64,64]{2,1,0:T(8,128)} %copy-done.75) | copy-start | bytes 196612
  184.2 10.8 %copy-start.98 = (s32[128]{0:T(128)S(1)}, s32[128]{0:T(128)}, u32[]{:S(2)}) copy-start(s32[128]{0:T(128)} %copy-done.96) | copy-start | bytes 1540
  184.2 11.1 %copy-start.7 = (f32[8,128,128]{2,1,0:T(8,128)S(1)}, f32[8,128,128]{2,1,0:T(8,128)}, u32[]{:S(2)}) copy-start(f32[8,128,128]{2,1,0:T(8,128)} %copy-done.6) | copy-start | bytes 1572868
  184.2 11.1 %copy-start.10 = (f32[8,128,128]{2,1,0:T(8,128)S(1)}, f32[8,128,128]{2,1,0:T(8,128)}, u32[]{:S(2)}) copy-start(f32[8,128,128]{2,1,0:T(8,128)} %copy-done.9) | copy-start | bytes 1572868
  184.2 11.1 %copy-start.14 = (f32[8,128,128]{2,1,0:T(8,128)S(1)}, f32[8,128,128]{2,1,0:T(8,128)}, u32[]{:S(2)}) copy-start(f32[8,128,128]{2,1,0:T(8,128)} %copy-done.12) | copy-start | bytes 1572868
  184.2 11.1 %copy-start.28 = (f32[8,128,128]{2,1,0:T(8,128)S(1)}, f32[8,128,128]{2,1,0:T(8,128)}, u32[]{:S(2)}) copy-start(f32[8,128,128]{2,1,0:T(8,128)} %copy-done.27) | copy-start | bytes 1572868
  184.2 11.1 %copy-start.34 = (f32[6,128,128]{2,1,0:T(8,128)S(1)}, f32[6,128,128]{2,1,0:T(8,128)}, u32[]{:S(2)}) copy-start(f32[6,128,128]{2,1,0:T(8,128)} %copy-done.33) | copy-start | bytes 1179652
  184.2 11.1 %slice-start.1 = ((f32[6,128,128]{2,1,0:T(8,128)}), f32[4,128,128]{2,1,0:T(8,128)S(1)}, s32[]{:S(2)}) async-start(f32[6,128,128]{2,1,0:T(8,128)} %copy-done.33), calls=%async_computation.1 | async-start | bytes 524288 | tf_op jit(solution)/shard_map/slice | solution.py:141
  184.3 11.1 %copy-start.92 = (s32[256]{0:T(256)S(1)}, s32[256]{0:T(256)}, u32[]{:S(2)}) copy-start(s32[256]{0:T(256)} %copy-done.90) | copy-start | bytes 3076
  197.5 11.9 %slice-start.7 = ((f32[4,64,64]{2,1,0:T(8,128)}), f32[2,64,64]{2,1,0:T(8,128)S(1)}, s32[]{:S(2)}) async-start(f32[4,64,64]{2,1,0:T(8,128)} %copy-done.73), calls=%async_computation.7 | async-start | bytes 131072 | tf_op jit(solution)/shard_map/slice | solution.py:141
  200.2 10.8 %copy-start.8 = (f32[8,128,128]{2,1,0:T(8,128)S(1)}, f32[8,128,128]{2,1,0:T(8,128)}, u32[]{:S(2)}) copy-start(f32[8,128,128]{2,1,0:T(8,128)} %copy-done.6) | copy-start | bytes 1572868
  200.2 10.8 %copy-start.11 = (f32[8,128,128]{2,1,0:T(8,128)S(1)}, f32[8,128,128]{2,1,0:T(8,128)}, u32[]{:S(2)}) copy-start(f32[8,128,128]{2,1,0:T(8,128)} %copy-done.9) | copy-start | bytes 1572868
  200.2 10.8 %copy-start.15 = (f32[8,128,128]{2,1,0:T(8,128)S(1)}, f32[8,128,128]{2,1,0:T(8,128)}, u32[]{:S(2)}) copy-start(f32[8,128,128]{2,1,0:T(8,128)} %copy-done.12) | copy-start | bytes 1572868
  200.3 10.8 %copy-start.26 = (f32[8,128,128]{2,1,0:T(8,128)S(1)}, f32[8,128,128]{2,1,0:T(8,128)}, u32[]{:S(2)}) copy-start(f32[8,128,128]{2,1,0:T(8,128)} %copy-done.25) | copy-start | bytes 1572868
  200.3 10.8 %copy-start.32 = (f32[6,128,128]{2,1,0:T(8,128)S(1)}, f32[6,128,128]{2,1,0:T(8,128)}, u32[]{:S(2)}) copy-start(f32[6,128,128]{2,1,0:T(8,128)} %copy-done.31) | copy-start | bytes 1179652
  200.3 10.8 %slice-start = ((f32[6,128,128]{2,1,0:T(8,128)}), f32[4,128,128]{2,1,0:T(8,128)S(1)}, s32[]{:S(2)}) async-start(f32[6,128,128]{2,1,0:T(8,128)} %copy-done.31), calls=%async_computation | async-start | bytes 524288 | tf_op jit(solution)/shard_map/slice | solution.py:141
  200.3 10.8 %copy-start.93 = (s32[256]{0:T(256)S(1)}, s32[256]{0:T(256)}, u32[]{:S(2)}) copy-start(s32[256]{0:T(256)} %copy-done.90) | copy-start | bytes 3076
  (85 other events, 392.0 us)

commit v5 on v4

--- a/solution.py
+++ b/solution.py
@@ -225,20 +225,31 @@
         _plane_loop(sweep_no, length - sweep_no, extent_y, body)
 
 
-def _fine_first_kernel(resid, kxo, kyl, kyh, kzl, kzh, w, out, buf_a, buf_b):
-    _smooth_in_vmem(resid, kxo, kyl, kyh, kzl, kzh, w, out, (buf_a, buf_b), SWEEPS)
+def _fine_first_kernel(resid, kxo_full, kyl, kyh, kzl, kzh, w, out, low, high, buf_a, buf_b):
+    _smooth_in_vmem(resid, kxo_full.at[1:-1], kyl, kyh, kzl, kzh, w, out, (buf_a, buf_b), SWEEPS)
+    width, block, extent_y = low.shape[0], out.shape[0], out.shape[1]
+
+    def edges(q, y0):
+        rows = pl.ds(y0, ROWS)
+        low[q, rows, :] = out[q, rows, :]
+        high[q, rows, :] = out[block - width + q, rows, :]
+
+    _plane_loop(0, width, extent_y, edges)
 
 
 def _fine_second_kernel(
-    fine_ext, rhs, kxo_full, kyl, kyh, kzl, kzh, w, diag, out, resid_out, held, resid, buf_a, buf_b
+    fine_l, fine, fine_r, rhs, kxo_full, kyl, kyh, kzl, kzh, w, diag, out, resid_out, held, resid,
+    buf_a, buf_b,
 ):
-    planes, extent_y = fine_ext.shape[0], fine_ext.shape[1]
+    width, block, extent_y = fine_l.shape[0], fine.shape[0], fine.shape[1]
+    planes = held.shape[0]
     _zero_pads(held)
-
-    def copy_in(q, y0):
-        held[q, pl.ds(PAD + y0, ROWS), :] = fine_ext[q, pl.ds(y0, ROWS), :]
-
-    _plane_loop(0, planes, extent_y, copy_in)
+    for src, first in ((fine_l, 0), (fine, width), (fine_r, width + block)):
+
+        def copy_in(q, y0, src=src, first=first):
+            held[q, pl.ds(PAD + y0, ROWS), :] = src[q - first, pl.ds(y0, ROWS), :]
+
+        _plane_loop(first, first + src.shape[0], extent_y, copy_in)
 
     def residual(q, y0):
         rows = pl.ds(y0, ROWS)
@@ -276,18 +287,23 @@
     )(*args)
 
 
-def fine_smooth(resid_ext, co):
+def fine_smooth(resid_ext, co, width):
     length, extent_y, extent_z = resid_ext.shape
-    out = jax.ShapeDtypeStruct((length - 2 * (SWEEPS - 1), extent_y, extent_z), jnp.float32)
+    outs = [
+        jax.ShapeDtypeStruct((length - 2 * (SWEEPS - 1), extent_y, extent_z), jnp.float32),
+        jax.ShapeDtypeStruct((width, extent_y, extent_z), jnp.float32),
+        jax.ShapeDtypeStruct((width, extent_y, extent_z), jnp.float32),
+    ]
     padded = lambda planes: pltpu.VMEM((planes, extent_y + 2 * PAD, extent_z), jnp.float32)
     return _vmem_call(
-        _fine_first_kernel, out, [padded(length), padded(length - 2)],
-        resid_ext, co["kxo"][1:-1], co["kyl"], co["kyh"], co["kzl"], co["kzh"], co["w"],
-    )
-
-
-def fine_second(fine_ext, rhs_ext, co):
-    planes, extent_y, extent_z = fine_ext.shape
+        _fine_first_kernel, outs, [padded(length), padded(length - 2)],
+        resid_ext, co["kxo"], co["kyl"], co["kyh"], co["kzl"], co["kzh"], co["w"],
+    )
+
+
+def fine_second(fine_l, fine, fine_r, rhs_ext, co):
+    extent_y, extent_z = fine.shape[1], fine.shape[2]
+    planes = fine.shape[0] + 2 * fine_l.shape[0]
     length = planes - 2
     block = length - 2 * (SWEEPS - 1)
     outs = [jax.ShapeDtypeStruct((block, extent_y, extent_z), jnp.float32)] * 2
@@ -296,7 +312,7 @@
         _fine_second_kernel, outs,
         [padded(planes), pltpu.VMEM((length, extent_y, extent_z), jnp.float32),
          padded(length), padded(length - 2)],
-        fine_ext, rhs_ext, co["kxo"], co["kyl"], co["kyh"], co["kzl"], co["kzh"], co["w"], co["diag"],
+        fine_l, fine, fine_r, rhs_ext, co["kxo"], co["kyl"], co["kyh"], co["kzl"], co["kzh"], co["w"], co["diag"],
     )
 
 
@@ -310,11 +326,10 @@
     rhs_ext = jnp.concatenate([rl, right_side, rr])
     co0 = make_coefs(rho0_ext, 1.0)
 
-    fine_0 = fine_smooth(rhs_ext, co0)
-
-    (fl,), (fr,) = exchange([fine_0[-3:]], [fine_0[:3]], 1)
-    fine_ext = jnp.concatenate([fl, fine_0, fr])
-    fine_1, resid_block = fine_second(fine_ext, rhs_ext, co0)
+    fine_0, low, high = fine_smooth(rhs_ext, co0, 3)
+
+    (fl,), (fr,) = exchange([high], [low], 1)
+    fine_1, resid_block = fine_second(fl, fine_0, fr, rhs_ext, co0)
 
     rho1 = coarsen(density)
     rho2 = coarsen(rho1)

time: 217 us -> 214 us (0.986)
  waiting for transfers between devices: 24 us -> 20.6 us
  local copies, waits for them, and re-layouts: 45.5 us -> 43.1 us
    ppermute x10, waiting for transfers between devices: 24 us -> 20.6 us  [recv(): return lax.ppermute(value, 'gx', pairs)]
    slice x2 -> x0, local copies, waits for them, and re-layouts: 3.41 us -> none  [the longest x1 1.79 us: fine_smooth(): co['kxo'][1:-1]]
    unnamed x253 -> x239, local copies, waits for them, and re-layouts: 14.8 us -> 15.5 us
  transfers between devices with their start and end apart: 10 -> 10, of which waited for: 6 -> 6; matrix products, arithmetic and copies ran while one was open for 13% -> 15% of each run, Pallas kernels for 0% -> 0%
where the time goes in v5:
time: 214 us; the launch traced here: 212 us
  other arithmetic  47 us (22%)
  local copies, waits for them, and re-layouts  43.1 us (20%)
  starting transfers between devices  35.2 us (16%)
  Pallas kernels  33.2 us (16%)
  matrix products  29.5 us (14%)
  waiting for transfers between devices  20.6 us (10%)
  between operations  3.01 us (1%)
    ppermute x10, starting transfers between devices, recv(): return lax.ppermute(value, 'gx', pairs)  35.2 us
    pallas_call x2, Pallas kernels, _vmem_call(): pl.pallas_call(kernel, out_shape=outs, in_specs=[pl.BlockSpec(memory_spac...  33.2 us
    ppermute x10, waiting for transfers between devices, recv(): return lax.ppermute(value, 'gx', pairs)  20.6 us
    unnamed x239, local copies, waits for them, and re-layouts  15.5 us
    dot_general x12, matrix products, shrink_sides(): jnp.einsum('xyz,zw->xyw', field, pair_matrix(extent_z), precision=EXACT)  9.56 us
    div x1, other arithmetic, make_coefs(): OMEGA / diag  7.61 us
    reduce_sum x7, other arithmetic, coarsen(): planes = field.reshape(extent_x // 2, 2, extent_y, extent_z).sum(axis=1)  7.52 us
    div x5, other arithmetic, make_coefs(): faces = [two_s / (safe + jnp.where(nb > 0, nb, safe)) for nb in near]  7.4 us
  transfers between devices with their start and end apart: 10, of which 6 were waited for; matrix products, arithmetic and copies ran while one was open for 15% of the time, Pallas kernels for 0%

profile of v5, /device:TPU:48, one launch (start us, length us, event | category | flops | bytes accessed | tf_op | source)
XLA Modules:
  0.0 211.7 jit_solution(12329926767904502618)
XLA Ops:
  0.6 1.6 fusion.598
  2.8 1.2 pad_maximum_fusion.11
  3.9 2.0 collective-permute-start
  6.0 1.2 pad_maximum_fusion.12
  7.1 3.6 %collective-permute-start.1 = (f32[5,256,256]{2,1,0:T(8,128)}, f32[5,256,256]{2,1,0:T(8,128)}, u32[]{:S(2)}, u32[]{:S(2)}) collective-permute-start(f32[5,256,256]{2,1,0:T(8,128)} %pad_maximum_fusion.12), channel_id=1, source_target_pairs={{1,0},{2,1},{3,2},{4,3},{5,4},{6,5},{7,6},{8,7},{9,8},{10,9},{11,1... | collective-permute-start | bytes 3932168 | tf_op jit(solution)/shard_map/ppermute | solution.py:25
  11.8 1.1 bitcast_reduce_fusion.3
  19.2 4.1 %collective-permute-done = f32[5,256,256]{2,1,0:T(8,128)} collective-permute-done((f32[5,256,256]{2,1,0:T(8,128)}, f32[5,256,256]{2,1,0:T(8,128)}, u32[]{:S(2)}, u32[]{:S(2)}) %collective-permute-start) | collective-permute-done | bytes 1310752 | tf_op jit(solution)/shard_map/ppermute | solution.py:25
  23.3 1.2 slice.1717
  24.5 1.7 collective-permute-done.1
  26.2 1.2 slice.1718
  28.8 7.6 %broadcast_divide_fusion = (f32[12,256,256]{2,1,0:T(8,128)}, f32[12,256,256]{2,1,0:T(8,128)}, f32[12,256,256]{2,1,0:T(8,128)}) fusion(f32[12,258,1]{2,1,0:T(8,128)S(1)} %get-tuple-element.38, f32[12,1,256]{2,1,0:T(1,128)S(1)} %get-tuple-element.36, f32[12,256,256]{2,1,0:T(8,128)S(1)} %slice.1721, f32[12,1,256]{2,1,0:T(1,128)S(1)} %get-tuple-element.37, ...), kind=kLoop, calls=%fused_computation.40 | loop fusion | flops 33030144 | bytes 22069440 | tf_op jit(solution)/shard_map/div | solution.py:120
  36.4 5.7 %fusion.13 = (f32[12,256,256]{2,1,0:T(8,128)}, f32[12,256,256]{2,1,0:T(8,128)}, f32[12,256,256]{2,1,0:T(8,128)}) fusion(f32[12,258,1]{2,1,0:T(8,128)S(1)} %get-tuple-element.38, f32[12,1,256]{2,1,0:T(1,128)S(1)} %get-tuple-element.36, f32[12,256,256]{2,1,0:T(8,128)S(1)} %slice.1721, f32[12,1,256]{2,1,0:T(1,128)S(1)} %get-tuple-element.37, ...), kind=kLoop, calls=%fused_computation.23 | loop fusion | flops 16515072 | bytes 12632256 | tf_op jit(solution)/shard_map/div | solution.py:109
  42.2 2.5 %divide_select_fusion.kxo_full = f32[13,256,256]{2,1,0:T(8,128)} fusion(f32[14,256,256]{2,1,0:T(8,128)S(1)} %pad_maximum_fusion), kind=kLoop, calls=%fused_computation.14 | loop fusion | flops 5111808 | bytes 10223616 | tf_op jit(solution)/shard_map/jit(_where)/select_n | solution.py:113
  44.6 1.1 slice.1715
  45.7 1.1 slice.1716
  46.8 1.9 pad_maximum_fusion.10.resid.rhs
  48.7 14.0 %shard_map.41 = (f32[8,256,256]{2,1,0:T(8,128)}, f32[3,256,256]{2,1,0:T(8,128)}, f32[3,256,256]{2,1,0:T(8,128)}) custom-call(f32[12,256,256]{2,1,0:T(8,128)} %pad_maximum_fusion.10.resid.rhs, f32[13,256,256]{2,1,0:T(8,128)} %divide_select_fusion.kxo_full, f32[12,256,256]{2,1,0:T(8,128)} %get-tuple-element.42.kyl, f32[12,256,256]{2,1,0:T(8,128)} %get-tuple-element.43.kyh, ...), custom_call_target="tpu_custom_call" | custom-call | tf_op jit(solution)/shard_map/pallas_call | solution.py:276
  62.8 4.1 %collective-permute-start.2 = (f32[3,256,256]{2,1,0:T(8,128)}, f32[3,256,256]{2,1,0:T(8,128)}, u32[]{:S(2)}, u32[]{:S(2)}) collective-permute-start(f32[3,256,256]{2,1,0:T(8,128)} %get-tuple-element.8), channel_id=1, source_target_pairs={{0,1},{1,2},{2,3},{3,4},{4,5},{5,6},{6,7},{7,8},{8,9},{9,10},{10,1... | collective-permute-start | bytes 2359304 | tf_op jit(solution)/shard_map/ppermute | solution.py:25
  66.9 2.1 collective-permute-start.3
  69.0 1.4 constant_dynamic-update-slice_fusion.38
  70.4 1.5 fusion.21
  72.9 1.4 fusion.23
  74.4 1.8 fusion.608
  76.6 2.0 collective-permute-done.3.fine_r
  78.6 19.2 %shard_map.42 = (f32[8,256,256]{2,1,0:T(8,128)}, f32[8,256,256]{2,1,0:T(8,128)}) custom-call(f32[3,256,256]{2,1,0:T(8,128)} %collective-permute-done.2.fine_l, f32[8,256,256]{2,1,0:T(8,128)} %get-tuple-element.7.fine, f32[3,256,256]{2,1,0:T(8,128)} %collective-permute-done.3.fine_r, f32[12,256,256]{2,1,0:T(8,128)} %pad_maximum_fusion.10.resid.rhs, ...), custom_call_target="tpu_custom_call" | custom-call | tf_op jit(solution)/shard_map/pallas_call | solution.py:276
  97.9 2.0 bitcast_reduce_fusion.1
  102.4 2.0 collective-permute-start.4
  106.5 5.5 %collective-permute-done.4 = f32[142336]{0:T(1024)S(1)} collective-permute-done((f32[142336]{0:T(1024)S(1)}, f32[142336]{0:T(1024)S(1)}, u32[]{:S(2)}, u32[]{:S(2)}) %collective-permute-start.4) | collective-permute-done | bytes 569376 | tf_op jit(solution)/shard_map/ppermute | solution.py:25
  123.1 4.6 %collective-permute-start.6 = (f32[13312]{0:T(1024)}, f32[13312]{0:T(1024)}, u32[]{:S(2)}, u32[]{:S(2)}) collective-permute-start(f32[13312]{0:T(1024)} %get-tuple-element.89), channel_id=1, source_target_pairs={{0,3},{1,4},{2,5},{3,6},{4,7},{5,8},{6,9},{7,10},{8,11},{9,12},{10... | collective-permute-start | bytes 159752 | tf_op jit(solution)/shard_map/ppermute | solution.py:25
  127.7 11.7 %collective-permute-start.7 = (f32[13312]{0:T(1024)}, f32[13312]{0:T(1024)}, u32[]{:S(2)}, u32[]{:S(2)}) collective-permute-start(f32[13312]{0:T(1024)} %get-tuple-element.88), channel_id=1, source_target_pairs={{0,125},{1,126},{2,127},{3,0},{4,1},{5,2},{6,3},{7,4},{8,5},{9,6},... | collective-permute-start | bytes 159752 | tf_op jit(solution)/shard_map/ppermute | solution.py:25
  150.2 4.8 %collective-permute-start.9 = (f32[27,32,32]{2,1,0:T(8,128)}, f32[27,32,32]{2,1,0:T(8,128)}, u32[]{:S(2)}, u32[]{:S(2)}) collective-permute-start(f32[27,32,32]{2,1,0:T(8,128)} %constant_dynamic-update-slice_fusion.7), channel_id=1, source_target_pairs={{0,119},{1,120},{2,121},{3,122},{4,123},{5,124},{6,125},{7,126},{8... | collective-permute-start | bytes 331784 | tf_op jit(solution)/shard_map/ppermute | solution.py:25
  157.2 1.3 fusion.590
  159.1 6.8 %collective-permute-done.8 = f32[27,32,32]{2,1,0:T(8,128)} collective-permute-done((f32[27,32,32]{2,1,0:T(8,128)}, f32[27,32,32]{2,1,0:T(8,128)}, u32[]{:S(2)}, u32[]{:S(2)}) %collective-permute-start.8) | collective-permute-done | bytes 110624 | tf_op jit(solution)/shard_map/ppermute | solution.py:25
  171.0 1.7 reduce_sum.117
  172.7 1.5 fusion.539
  178.8 1.7 reduce_sum.119
  180.7 1.7 fusion.534
  182.6 1.2 fusion.199
  183.8 1.9 slice_multiply_fusion.14
  190.0 1.3 fusion.284
  192.2 1.6 convolution_bitcast_fusion
  194.7 1.8 reduce_sum.118
  196.6 1.6 fusion.537
  199.1 1.1 fusion.241
  204.1 1.2 fusion.25
  205.7 1.3 fusion.267
  208.6 1.7 bitcast_add_fusion
  210.2 1.5 broadcast_in_dim.38
  (423 shorter events, 61.1 us)
Async XLA Ops:
  3.9 19.4 %collective-permute-start = (f32[5,256,256]{2,1,0:T(8,128)}, f32[5,256,256]{2,1,0:T(8,128)}, u32[]{:S(2)}, u32[]{:S(2)}) collective-permute-start(f32[5,256,256]{2,1,0:T(8,128)} %pad_maximum_fusion.11), channel_id=1, source_target_pairs={{0,1},{1,2},{2,3},{3,4},{4,5},{5,6},{6,7},{7,8},{8,9},{9,10},{10,1... | collective-permute-start | bytes 3932168 | tf_op jit(solution)/shard_map/ppermute | solution.py:25
  7.1 19.1 %collective-permute-start.1 = (f32[5,256,256]{2,1,0:T(8,128)}, f32[5,256,256]{2,1,0:T(8,128)}, u32[]{:S(2)}, u32[]{:S(2)}) collective-permute-start(f32[5,256,256]{2,1,0:T(8,128)} %pad_maximum_fusion.12), channel_id=1, source_target_pairs={{1,0},{2,1},{3,2},{4,3},{5,4},{6,5},{7,6},{8,7},{9,8},{10,9},{11,1... | collective-permute-start | bytes 3932168 | tf_op jit(solution)/shard_map/ppermute | solution.py:25
  13.4 14.0 %copy-start.46 = (f32[64,2,64]{2,0,1:T(8,128)}, f32[64,2,64]{2,0,1:T(8,128)S(1)}, u32[]{:S(2)}) copy-start(f32[64,2,64]{2,0,1:T(8,128)S(1)} %copy.81) | copy-start | bytes 98308
  14.5 13.2 %copy-start.26 = (f32[128,4,128]{2,0,1:T(8,128)}, f32[128,4,128]{2,0,1:T(8,128)S(1)}, u32[]{:S(2)}) copy-start(f32[128,4,128]{2,0,1:T(8,128)S(1)} %get-tuple-element.99) | copy-start | bytes 786436
  15.6 12.1 %copy-start.60 = (f32[2,64,64]{2,1,0:T(8,128)}, f32[2,64,64]{2,1,0:T(8,128)S(1)}, u32[]{:S(2)}) copy-start(f32[2,64,64]{2,1,0:T(8,128)S(1)} %get-tuple-element.107) | copy-start | bytes 98308
  62.8 13.8 %collective-permute-start.2 = (f32[3,256,256]{2,1,0:T(8,128)}, f32[3,256,256]{2,1,0:T(8,128)}, u32[]{:S(2)}, u32[]{:S(2)}) collective-permute-start(f32[3,256,256]{2,1,0:T(8,128)} %get-tuple-element.8), channel_id=1, source_target_pairs={{0,1},{1,2},{2,3},{3,4},{4,5},{5,6},{6,7},{7,8},{8,9},{9,10},{10,1... | collective-permute-start | bytes 2359304 | tf_op jit(solution)/shard_map/ppermute | solution.py:25
  66.9 11.7 %collective-permute-start.3 = (f32[3,256,256]{2,1,0:T(8,128)}, f32[3,256,256]{2,1,0:T(8,128)}, u32[]{:S(2)}, u32[]{:S(2)}) collective-permute-start(f32[3,256,256]{2,1,0:T(8,128)} %get-tuple-element.9), channel_id=1, source_target_pairs={{1,0},{2,1},{3,2},{4,3},{5,4},{6,5},{7,6},{8,7},{9,8},{10,9},{11,1... | collective-permute-start | bytes 2359304 | tf_op jit(solution)/shard_map/ppermute | solution.py:25
  99.9 13.0 %copy-start.15 = (f32[128,4,128]{2,0,1:T(8,128)S(1)}, f32[128,4,128]{2,0,1:T(8,128)}, u32[]{:S(2)}) copy-start(f32[128,4,128]{2,0,1:T(8,128)} %get-tuple-element.103) | copy-start | bytes 786436
  102.4 9.6 %collective-permute-start.4 = (f32[142336]{0:T(1024)S(1)}, f32[142336]{0:T(1024)S(1)}, u32[]{:S(2)}, u32[]{:S(2)}) collective-permute-start(f32[142336]{0:T(1024)S(1)} %get-tuple-element.96), channel_id=1, source_target_pairs={{0,1},{1,2},{2,3},{3,4},{4,5},{5,6},{6,7},{7,8},{8,9},{9,10},{10,1... | collective-permute-start | bytes 1708040 | tf_op jit(solution)/shard_map/ppermute | solution.py:25
  104.4 8.5 %collective-permute-start.5 = (f32[142336]{0:T(1024)S(1)}, f32[142336]{0:T(1024)S(1)}, u32[]{:S(2)}, u32[]{:S(2)}) collective-permute-start(f32[142336]{0:T(1024)S(1)} %get-tuple-element.97), channel_id=1, source_target_pairs={{0,127},{1,0},{2,1},{3,2},{4,3},{5,4},{6,5},{7,6},{8,7},{9,8},{10,... | collective-permute-start | bytes 1708040 | tf_op jit(solution)/shard_map/ppermute | solution.py:25
  105.3 40.8 %copy-start.75 = (f32[1,32,32]{2,1,0:T(8,128)}, f32[1,32,32]{2,1,0:T(8,128)S(1)}, u32[]{:S(2)}) copy-start(f32[1,32,32]{2,1,0:T(8,128)S(1)} %copy.83) | copy-start | bytes 12292
  106.5 40.2 %copy-start.77 = (f32[1,32,32]{2,1,0:T(8,128)}, f32[1,32,32]{2,1,0:T(8,128)S(1)}, u32[]{:S(2)}) copy-start(f32[1,32,32]{2,1,0:T(8,128)S(1)} %copy.84) | copy-start | bytes 12292
  113.9 25.7 %copy-start.4 = (f32[8,128,128]{2,1,0:T(8,128)}, f32[8,128,128]{2,1,0:T(8,128)S(1)}, u32[]{:S(2)}) copy-start(f32[8,128,128]{2,1,0:T(8,128)S(1)} %get-tuple-element.66) | copy-start | bytes 1572868
  116.3 23.3 %copy-start.7 = (f32[8,128,128]{2,1,0:T(8,128)}, f32[8,128,128]{2,1,0:T(8,128)S(1)}, u32[]{:S(2)}) copy-start(f32[8,128,128]{2,1,0:T(8,128)S(1)} %get-tuple-element.15) | copy-start | bytes 1572868
  116.4 23.0 %copy-start.27 = (f32[128,4,128]{2,0,1:T(8,128)S(1)}, f32[128,4,128]{2,0,1:T(8,128)}, u32[]{:S(2)}) copy-start(f32[128,4,128]{2,0,1:T(8,128)} %copy-done.26) | copy-start | bytes 786436
  122.4 17.2 %copy-start.11 = (f32[8,128,128]{2,1,0:T(8,128)S(1)}, f32[8,128,128]{2,1,0:T(8,128)}, u32[]{:S(2)}) copy-start(f32[8,128,128]{2,1,0:T(8,128)} %copy-done.10) | copy-start | bytes 1572868
  123.1 20.8 %collective-permute-start.6 = (f32[13312]{0:T(1024)}, f32[13312]{0:T(1024)}, u32[]{:S(2)}, u32[]{:S(2)}) collective-permute-start(f32[13312]{0:T(1024)} %get-tuple-element.89), channel_id=1, source_target_pairs={{0,3},{1,4},{2,5},{3,6},{4,7},{5,8},{6,9},{7,10},{8,11},{9,12},{10... | collective-permute-start | bytes 159752 | tf_op jit(solution)/shard_map/ppermute | solution.py:25
  127.7 20.9 %collective-permute-start.7 = (f32[13312]{0:T(1024)}, f32[13312]{0:T(1024)}, u32[]{:S(2)}, u32[]{:S(2)}) collective-permute-start(f32[13312]{0:T(1024)} %get-tuple-element.88), channel_id=1, source_target_pairs={{0,125},{1,126},{2,127},{3,0},{4,1},{5,2},{6,3},{7,4},{8,5},{9,6},... | collective-permute-start | bytes 159752 | tf_op jit(solution)/shard_map/ppermute | solution.py:25
  139.6 16.1 %copy-start.47 = (f32[64,2,64]{2,0,1:T(8,128)S(1)}, f32[64,2,64]{2,0,1:T(8,128)}, u32[]{:S(2)}) copy-start(f32[64,2,64]{2,0,1:T(8,128)} %copy-done.46) | copy-start | bytes 98308
  140.8 16.4 %copy-start.28 = (f32[6,128,128]{2,1,0:T(8,128)}, f32[6,128,128]{2,1,0:T(8,128)S(1)}, u32[]{:S(2)}) copy-start(f32[6,128,128]{2,1,0:T(8,128)S(1)} %fusion.53) | copy-start | bytes 1179652
  142.5 14.7 %copy-start.100 = (f32[6]{0:T(128)S(1)}, f32[6]{0:T(128)}, u32[]{:S(2)}) copy-start(f32[6]{0:T(128)} %and_convert_fusion.2) | copy-start | bytes 76
  144.8 12.4 %copy-start.39 = (f32[9,32,32]{2,1,0:T(8,128)}, f32[9,32,32]{2,1,0:T(8,128)S(1)}, u32[]{:S(2)}) copy-start(f32[9,32,32]{2,1,0:T(8,128)S(1)} %reshape.493) | copy-start | bytes 110596
  150.2 15.8 %collective-permute-start.8 = (f32[27,32,32]{2,1,0:T(8,128)}, f32[27,32,32]{2,1,0:T(8,128)}, u32[]{:S(2)}, u32[]{:S(2)}) collective-permute-start(f32[27,32,32]{2,1,0:T(8,128)} %constant_dynamic-update-slice_fusion.7), channel_id=1, source_target_pairs={{0,9},{1,10},{2,11},{3,12},{4,13},{5,14},{6,15},{7,16},{8,17},{9,1... | collective-permute-start | bytes 331784 | tf_op jit(solution)/shard_map/ppermute | solution.py:25
  150.2 17.0 %collective-permute-start.9 = (f32[27,32,32]{2,1,0:T(8,128)}, f32[27,32,32]{2,1,0:T(8,128)}, u32[]{:S(2)}, u32[]{:S(2)}) collective-permute-start(f32[27,32,32]{2,1,0:T(8,128)} %constant_dynamic-update-slice_fusion.7), channel_id=1, source_target_pairs={{0,119},{1,120},{2,121},{3,122},{4,123},{5,124},{6,125},{7,126},{8... | collective-permute-start | bytes 331784 | tf_op jit(solution)/shard_map/ppermute | solution.py:25
  158.7 9.5 %copy-start.49 = (f32[6,64,64]{2,1,0:T(8,128)}, f32[6,64,64]{2,1,0:T(8,128)S(1)}, u32[]{:S(2)}) copy-start(f32[6,64,64]{2,1,0:T(8,128)S(1)} %get-tuple-element.33) | copy-start | bytes 294916
  158.7 9.5 %copy-start.101 = (f32[27]{0:T(128)S(1)}, f32[27]{0:T(128)}, u32[]{:S(2)}) copy-start(f32[27]{0:T(128)} %and_convert_fusion.4) | copy-start | bytes 328
  158.9 9.5 %copy-start.72 = (f32[4,64,64]{2,1,0:T(8,128)}, f32[4,64,64]{2,1,0:T(8,128)S(1)}, u32[]{:S(2)}) copy-start(f32[4,64,64]{2,1,0:T(8,128)S(1)} %fusion.168) | copy-start | bytes 196612
  178.0 12.0 %slice-start.8 = ((f32[4,64,64]{2,1,0:T(8,128)}), f32[2,64,64]{2,1,0:T(8,128)S(1)}, s32[]{:S(2)}) async-start(f32[4,64,64]{2,1,0:T(8,128)} %copy-done.72), calls=%async_computation.8 | async-start | bytes 131072 | tf_op jit(solution)/shard_map/slice | solution.py:141
  180.6 9.4 %copy-start.73 = (f32[4,64,64]{2,1,0:T(8,128)S(1)}, f32[4,64,64]{2,1,0:T(8,128)}, u32[]{:S(2)}) copy-start(f32[4,64,64]{2,1,0:T(8,128)} %copy-done.72) | copy-start | bytes 196612
  180.6 10.6 %copy-start.94 = (s32[128]{0:T(128)S(1)}, s32[128]{0:T(128)}, u32[]{:S(2)}) copy-start(s32[128]{0:T(128)} %copy-done.92) | copy-start | bytes 1540
  180.6 11.0 %copy-start.5 = (f32[8,128,128]{2,1,0:T(8,128)S(1)}, f32[8,128,128]{2,1,0:T(8,128)}, u32[]{:S(2)}) copy-start(f32[8,128,128]{2,1,0:T(8,128)} %copy-done.4) | copy-start | bytes 1572868
  180.6 11.0 %copy-start.8 = (f32[8,128,128]{2,1,0:T(8,128)S(1)}, f32[8,128,128]{2,1,0:T(8,128)}, u32[]{:S(2)}) copy-start(f32[8,128,128]{2,1,0:T(8,128)} %copy-done.7) | copy-start | bytes 1572868
  180.6 11.0 %copy-start.12 = (f32[8,128,128]{2,1,0:T(8,128)S(1)}, f32[8,128,128]{2,1,0:T(8,128)}, u32[]{:S(2)}) copy-start(f32[8,128,128]{2,1,0:T(8,128)} %copy-done.10) | copy-start | bytes 1572868
  180.6 11.0 %copy-start.25 = (f32[8,128,128]{2,1,0:T(8,128)S(1)}, f32[8,128,128]{2,1,0:T(8,128)}, u32[]{:S(2)}) copy-start(f32[8,128,128]{2,1,0:T(8,128)} %copy-done.24) | copy-start | bytes 1572868
  180.6 11.0 %copy-start.31 = (f32[6,128,128]{2,1,0:T(8,128)S(1)}, f32[6,128,128]{2,1,0:T(8,128)}, u32[]{:S(2)}) copy-start(f32[6,128,128]{2,1,0:T(8,128)} %copy-done.30) | copy-start | bytes 1179652
  180.7 11.0 %slice-start.1 = ((f32[6,128,128]{2,1,0:T(8,128)}), f32[4,128,128]{2,1,0:T(8,128)S(1)}, s32[]{:S(2)}) async-start(f32[6,128,128]{2,1,0:T(8,128)} %copy-done.30), calls=%async_computation.1 | async-start | bytes 524288 | tf_op jit(solution)/shard_map/slice | solution.py:141
  180.7 11.0 %copy-start.88 = (s32[256]{0:T(256)S(1)}, s32[256]{0:T(256)}, u32[]{:S(2)}) copy-start(s32[256]{0:T(256)} %copy-done.86) | copy-start | bytes 3076
  193.8 11.9 %slice-start.7 = ((f32[4,64,64]{2,1,0:T(8,128)}), f32[2,64,64]{2,1,0:T(8,128)S(1)}, s32[]{:S(2)}) async-start(f32[4,64,64]{2,1,0:T(8,128)} %copy-done.70), calls=%async_computation.7 | async-start | bytes 131072 | tf_op jit(solution)/shard_map/slice | solution.py:141
  194.7 9.3 %slice-start.9 = ((f32[3,32,32]{2,1,0:T(8,128)}), f32[1,32,32]{2,1,0:T(8,128)S(1)}, s32[]{:S(2)}) async-start(f32[3,32,32]{2,1,0:T(8,128)} %copy-done.81), calls=%async_computation.9 | async-start | bytes 32768 | tf_op jit(solution)/shard_map/slice | solution.py:141
  196.5 9.2 %copy-start.71 = (f32[4,64,64]{2,1,0:T(8,128)S(1)}, f32[4,64,64]{2,1,0:T(8,128)}, u32[]{:S(2)}) copy-start(f32[4,64,64]{2,1,0:T(8,128)} %copy-done.70) | copy-start | bytes 196612
  196.5 9.2 %copy-start.95 = (s32[128]{0:T(128)S(1)}, s32[128]{0:T(128)}, u32[]{:S(2)}) copy-start(s32[128]{0:T(128)} %copy-done.92) | copy-start | bytes 1540
  196.5 10.8 %copy-start.6 = (f32[8,128,128]{2,1,0:T(8,128)S(1)}, f32[8,128,128]{2,1,0:T(8,128)}, u32[]{:S(2)}) copy-start(f32[8,128,128]{2,1,0:T(8,128)} %copy-done.4) | copy-start | bytes 1572868
  196.5 10.8 %copy-start.9 = (f32[8,128,128]{2,1,0:T(8,128)S(1)}, f32[8,128,128]{2,1,0:T(8,128)}, u32[]{:S(2)}) copy-start(f32[8,128,128]{2,1,0:T(8,128)} %copy-done.7) | copy-start | bytes 1572868
  196.5 10.8 %copy-start.13 = (f32[8,128,128]{2,1,0:T(8,128)S(1)}, f32[8,128,128]{2,1,0:T(8,128)}, u32[]{:S(2)}) copy-start(f32[8,128,128]{2,1,0:T(8,128)} %copy-done.10) | copy-start | bytes 1572868
  196.6 10.8 %copy-start.23 = (f32[8,128,128]{2,1,0:T(8,128)S(1)}, f32[8,128,128]{2,1,0:T(8,128)}, u32[]{:S(2)}) copy-start(f32[8,128,128]{2,1,0:T(8,128)} %copy-done.22) | copy-start | bytes 1572868
  196.6 10.8 %copy-start.29 = (f32[6,128,128]{2,1,0:T(8,128)S(1)}, f32[6,128,128]{2,1,0:T(8,128)}, u32[]{:S(2)}) copy-start(f32[6,128,128]{2,1,0:T(8,128)} %copy-done.28) | copy-start | bytes 1179652
  196.6 10.8 %slice-start = ((f32[6,128,128]{2,1,0:T(8,128)}), f32[4,128,128]{2,1,0:T(8,128)S(1)}, s32[]{:S(2)}) async-start(f32[6,128,128]{2,1,0:T(8,128)} %copy-done.28), calls=%async_computation | async-start | bytes 524288 | tf_op jit(solution)/shard_map/slice | solution.py:141
  196.6 10.8 %copy-start.89 = (s32[256]{0:T(256)S(1)}, s32[256]{0:T(256)}, u32[]{:S(2)}) copy-start(s32[256]{0:T(256)} %copy-done.86) | copy-start | bytes 3076
  (78 other events, 334.0 us)

commit v6 on v5

--- a/solution.py
+++ b/solution.py
@@ -319,9 +319,8 @@
 def per_device(right_side, density):
     me = lax.axis_index("gx")
 
-    (dl, rl), (dr, rr) = exchange(
-        [density[-3:], right_side[-2:]], [density[:3], right_side[:2]], 1
-    )
+    dl, dr = recv(density[-3:], 1, False), recv(density[:3], -1, False)
+    rl, rr = recv(right_side[-2:], 1, False), recv(right_side[:2], -1, False)
     rho0_ext = jnp.concatenate([dl, density, dr])
     rhs_ext = jnp.concatenate([rl, right_side, rr])
     co0 = make_coefs(rho0_ext, 1.0)

time: 214 us -> 218 us (1.019)
  starting transfers between devices: 35.2 us -> 44.8 us
  waiting for transfers between devices: 20.6 us -> 14.8 us
  other arithmetic: 47 us -> 43.1 us
  local copies, waits for them, and re-layouts: 43.1 us -> 46.8 us
    ppermute x10 -> x12, starting transfers between devices: 35.2 us -> 44.8 us  [recv(): return lax.ppermute(value, 'gx', pairs)]
    ppermute x10 -> x12, waiting for transfers between devices: 20.6 us -> 14.8 us  [recv(): return lax.ppermute(value, 'gx', pairs)]
    concatenate x4 -> x0, other arithmetic: 4.55 us -> none  [the longest x1 1.95 us: per_device(): rhs_ext = jnp.concatenate([rl, right_side, rr])]
    unnamed x239 -> x243, local copies, waits for them, and re-layouts: 15.5 us -> 19.9 us
    slice x6 -> x2, local copies, waits for them, and re-layouts: 6.22 us -> 3.89 us  [the longest x1 2.84 us: per_device(): dl, dr = (recv(density[-3:], 1, False), recv(density[:3], -1, False))]
  transfers between devices with their start and end apart: 10 -> 12, of which waited for: 6 -> 4; matrix products, arithmetic and copies ran while one was open for 15% -> 18% of each run, Pallas kernels for 0% -> 0%
where the time goes in v6:
time: 218 us; the launch traced here: 216 us
  local copies, waits for them, and re-layouts  46.8 us (21%)
  starting transfers between devices  44.8 us (21%)
  other arithmetic  43.1 us (20%)
  Pallas kernels  33.4 us (15%)
  matrix products  30.1 us (14%)
  waiting for transfers between devices  14.8 us (7%)
  between operations  3.05 us (1%)
    ppermute x12, starting transfers between devices, recv(): return lax.ppermute(value, 'gx', pairs)  44.8 us
    pallas_call x2, Pallas kernels, _vmem_call(): pl.pallas_call(kernel, out_shape=outs, in_specs=[pl.BlockSpec(memory_spac...  33.4 us
    unnamed x243, local copies, waits for them, and re-layouts  19.9 us
    ppermute x12, waiting for transfers between devices, recv(): return lax.ppermute(value, 'gx', pairs)  14.8 us
    dot_general x12, matrix products, shrink_sides(): jnp.einsum('xyz,zw->xyw', field, pair_matrix(extent_z), precision=EXACT)  9.56 us
    div x1, other arithmetic, make_coefs(): OMEGA / diag  7.62 us
    reduce_sum x7, other arithmetic, coarsen(): planes = field.reshape(extent_x // 2, 2, extent_y, extent_z).sum(axis=1)  7.53 us
    div x5, other arithmetic, make_coefs(): faces = [two_s / (safe + jnp.where(nb > 0, nb, safe)) for nb in near]  7.42 us
  transfers between devices with their start and end apart: 12, of which 4 were waited for; matrix products, arithmetic and copies ran while one was open for 18% of the time, Pallas kernels for 0%

profile of v6, /device:TPU:48, one launch (start us, length us, event | category | flops | bytes accessed | tf_op | source)
XLA Modules:
  0.0 216.2 jit_solution(17862797790498998244)
XLA Ops:
  0.6 2.8 %fusion.599 = (f32[3,256,256]{2,1,0:T(8,128)}, f32[3,256,256]{2,1,0:T(8,128)}) fusion(f32[8,256,256]{2,1,0:T(8,128)} %param.3), kind=kLoop, calls=%fused_computation.873 | loop fusion | bytes 3145728 | tf_op jit(solution)/shard_map/slice | solution.py:322
  3.5 2.0 collective-permute-start.2
  5.5 3.6 %collective-permute-start.3 = (f32[3,256,256]{2,1,0:T(8,128)}, f32[3,256,256]{2,1,0:T(8,128)S(1)}, u32[]{:S(2)}, u32[]{:S(2)}) collective-permute-start(f32[3,256,256]{2,1,0:T(8,128)} %get-tuple-element.44), channel_id=1, source_target_pairs={{1,0},{2,1},{3,2},{4,3},{5,4},{6,5},{7,6},{8,7},{9,8},{10,9},{11,1... | collective-permute-start | bytes 2359304 | tf_op jit(solution)/shard_map/ppermute | solution.py:25
  9.2 1.0 fusion.600
  10.2 2.2 %collective-permute-start = (f32[2,256,256]{2,1,0:T(8,128)}, f32[2,256,256]{2,1,0:T(8,128)}, u32[]{:S(2)}, u32[]{:S(2)}) collective-permute-start(f32[2,256,256]{2,1,0:T(8,128)} %get-tuple-element.47), channel_id=1, source_target_pairs={{0,1},{1,2},{2,3},{3,4},{4,5},{5,6},{6,7},{7,8},{8,9},{9,10},{10,1... | collective-permute-start | bytes 1572872 | tf_op jit(solution)/shard_map/ppermute | solution.py:25
  12.4 3.4 %collective-permute-start.1 = (f32[2,256,256]{2,1,0:T(8,128)}, f32[2,256,256]{2,1,0:T(8,128)S(1)}, u32[]{:S(2)}, u32[]{:S(2)}) collective-permute-start(f32[2,256,256]{2,1,0:T(8,128)} %get-tuple-element.46), channel_id=1, source_target_pairs={{1,0},{2,1},{3,2},{4,3},{5,4},{6,5},{7,6},{8,7},{9,8},{10,9},{11,1... | collective-permute-start | bytes 1572872 | tf_op jit(solution)/shard_map/ppermute | solution.py:25
  20.3 1.1 bitcast_reduce_fusion.3
  25.6 1.5 reshape.485
  27.2 1.1 constant_dynamic-update-slice_fusion.2
  28.2 1.7 constant_dynamic-update-slice_fusion.1
  30.1 1.8 constant_dynamic-update-slice_fusion.5
  33.2 7.6 %broadcast_divide_fusion = (f32[12,256,256]{2,1,0:T(8,128)}, f32[12,256,256]{2,1,0:T(8,128)}, f32[12,256,256]{2,1,0:T(8,128)}) fusion(f32[12,258,1]{2,1,0:T(8,128)S(1)} %get-tuple-element.38, f32[12,1,256]{2,1,0:T(1,128)S(1)} %get-tuple-element.36, f32[12,256,256]{2,1,0:T(8,128)S(1)} %slice.1701, f32[12,1,256]{2,1,0:T(1,128)S(1)} %get-tuple-element.37, ...), kind=kLoop, calls=%fused_computation.38 | loop fusion | flops 33030144 | bytes 22069440 | tf_op jit(solution)/shard_map/div | solution.py:120
  40.8 5.8 %fusion.13 = (f32[12,256,256]{2,1,0:T(8,128)}, f32[12,256,256]{2,1,0:T(8,128)}, f32[12,256,256]{2,1,0:T(8,128)}) fusion(f32[12,258,1]{2,1,0:T(8,128)S(1)} %get-tuple-element.38, f32[12,1,256]{2,1,0:T(1,128)S(1)} %get-tuple-element.36, f32[12,256,256]{2,1,0:T(8,128)S(1)} %slice.1701, f32[12,1,256]{2,1,0:T(1,128)S(1)} %get-tuple-element.37, ...), kind=kLoop, calls=%fused_computation.22 | loop fusion | flops 16515072 | bytes 12632256 | tf_op jit(solution)/shard_map/div | solution.py:109
  46.6 2.5 %divide_select_fusion.kxo_full = f32[13,256,256]{2,1,0:T(8,128)} fusion(f32[14,256,256]{2,1,0:T(8,128)S(1)} %constant_dynamic-update-slice_fusion.3), kind=kLoop, calls=%fused_computation.13 | loop fusion | flops 5111808 | bytes 10223616 | tf_op jit(solution)/shard_map/jit(_where)/select_n | solution.py:113
  49.0 14.2 %shard_map.41 = (f32[8,256,256]{2,1,0:T(8,128)}, f32[3,256,256]{2,1,0:T(8,128)}, f32[3,256,256]{2,1,0:T(8,128)}) custom-call(f32[12,256,256]{2,1,0:T(8,128)} %copy-done.1, f32[13,256,256]{2,1,0:T(8,128)} %divide_select_fusion.kxo_full, f32[12,256,256]{2,1,0:T(8,128)} %get-tuple-element.42.kyl, f32[12,256,256]{2,1,0:T(8,128)} %get-tuple-element.43.kyh, ...), custom_call_target="tpu_custom_call" | custom-call | tf_op jit(solution)/shard_map/pallas_call | solution.py:276
  63.3 2.2 %collective-permute-start.4 = (f32[3,256,256]{2,1,0:T(8,128)}, f32[3,256,256]{2,1,0:T(8,128)}, u32[]{:S(2)}, u32[]{:S(2)}) collective-permute-start(f32[3,256,256]{2,1,0:T(8,128)} %get-tuple-element.8), channel_id=1, source_target_pairs={{0,1},{1,2},{2,3},{3,4},{4,5},{5,6},{6,7},{7,8},{8,9},{9,10},{10,1... | collective-permute-start | bytes 2359304 | tf_op jit(solution)/shard_map/ppermute | solution.py:25
  65.5 4.5 %collective-permute-start.5 = (f32[3,256,256]{2,1,0:T(8,128)}, f32[3,256,256]{2,1,0:T(8,128)}, u32[]{:S(2)}, u32[]{:S(2)}) collective-permute-start(f32[3,256,256]{2,1,0:T(8,128)} %get-tuple-element.9), channel_id=1, source_target_pairs={{1,0},{2,1},{3,2},{4,3},{5,4},{6,5},{7,6},{8,7},{9,8},{10,9},{11,1... | collective-permute-start | bytes 2359304 | tf_op jit(solution)/shard_map/ppermute | solution.py:25
  70.0 1.4 constant_dynamic-update-slice_fusion.44
  71.4 1.5 fusion.21
  73.9 1.4 fusion.23
  75.4 1.8 fusion.609
  77.9 1.8 collective-permute-done.5.fine_r
  79.6 19.2 %shard_map.42 = (f32[8,256,256]{2,1,0:T(8,128)}, f32[8,256,256]{2,1,0:T(8,128)}) custom-call(f32[3,256,256]{2,1,0:T(8,128)} %collective-permute-done.4.fine_l, f32[8,256,256]{2,1,0:T(8,128)} %get-tuple-element.7.fine, f32[3,256,256]{2,1,0:T(8,128)} %collective-permute-done.5.fine_r, f32[12,256,256]{2,1,0:T(8,128)} %copy-done.1, ...), custom_call_target="tpu_custom_call" | custom-call | tf_op jit(solution)/shard_map/pallas_call | solution.py:276
  98.9 2.0 bitcast_reduce_fusion.1
  103.4 1.3 collective-permute-start.6
  104.7 2.3 %collective-permute-start.7 = (f32[142336]{0:T(1024)S(1)}, f32[142336]{0:T(1024)S(1)}, u32[]{:S(2)}, u32[]{:S(2)}) collective-permute-start(f32[142336]{0:T(1024)S(1)} %get-tuple-element.97), channel_id=1, source_target_pairs={{0,127},{1,0},{2,1},{3,2},{4,3},{5,4},{6,5},{7,6},{8,7},{9,8},{10,... | collective-permute-start | bytes 1708040 | tf_op jit(solution)/shard_map/ppermute | solution.py:25
  108.9 5.5 %collective-permute-done.6 = f32[142336]{0:T(1024)S(1)} collective-permute-done((f32[142336]{0:T(1024)S(1)}, f32[142336]{0:T(1024)S(1)}, u32[]{:S(2)}, u32[]{:S(2)}) %collective-permute-start.6) | collective-permute-done | bytes 569376 | tf_op jit(solution)/shard_map/ppermute | solution.py:25
  125.4 4.7 %collective-permute-start.8 = (f32[13312]{0:T(1024)}, f32[13312]{0:T(1024)}, u32[]{:S(2)}, u32[]{:S(2)}) collective-permute-start(f32[13312]{0:T(1024)} %get-tuple-element.89), channel_id=1, source_target_pairs={{0,3},{1,4},{2,5},{3,6},{4,7},{5,8},{6,9},{7,10},{8,11},{9,12},{10... | collective-permute-start | bytes 159752 | tf_op jit(solution)/shard_map/ppermute | solution.py:25
  130.2 13.8 %collective-permute-start.9 = (f32[13312]{0:T(1024)}, f32[13312]{0:T(1024)}, u32[]{:S(2)}, u32[]{:S(2)}) collective-permute-start(f32[13312]{0:T(1024)} %get-tuple-element.88), channel_id=1, source_target_pairs={{0,125},{1,126},{2,127},{3,0},{4,1},{5,2},{6,3},{7,4},{8,5},{9,6},... | collective-permute-start | bytes 159752 | tf_op jit(solution)/shard_map/ppermute | solution.py:25
  154.7 4.8 %collective-permute-start.11 = (f32[27,32,32]{2,1,0:T(8,128)}, f32[27,32,32]{2,1,0:T(8,128)}, u32[]{:S(2)}, u32[]{:S(2)}) collective-permute-start(f32[27,32,32]{2,1,0:T(8,128)} %constant_dynamic-update-slice_fusion.13), channel_id=1, source_target_pairs={{0,119},{1,120},{2,121},{3,122},{4,123},{5,124},{6,125},{7,126},{8... | collective-permute-start | bytes 331784 | tf_op jit(solution)/shard_map/ppermute | solution.py:25
  161.7 1.3 fusion.590
  163.7 6.8 %collective-permute-done.10 = f32[27,32,32]{2,1,0:T(8,128)} collective-permute-done((f32[27,32,32]{2,1,0:T(8,128)}, f32[27,32,32]{2,1,0:T(8,128)}, u32[]{:S(2)}, u32[]{:S(2)}) %collective-permute-start.10) | collective-permute-done | bytes 110624 | tf_op jit(solution)/shard_map/ppermute | solution.py:25
  171.7 1.0 constant_dynamic-update-slice_fusion.20
  175.5 1.7 reduce_sum.117
  177.2 1.5 fusion.539
  183.4 1.7 reduce_sum.119
  185.2 1.7 fusion.534
  187.1 1.2 fusion.199
  188.4 1.9 slice_multiply_fusion.14
  194.4 1.3 fusion.284
  196.6 1.6 convolution_bitcast_fusion
  199.2 1.8 reduce_sum.118
  201.0 1.6 fusion.537
  203.5 1.1 fusion.241
  208.5 1.2 fusion.25
  210.1 1.3 fusion.267
  213.0 1.7 bitcast_add_fusion
  214.7 1.5 broadcast_in_dim.38
  (425 shorter events, 60.8 us)
Async XLA Ops:
  3.5 12.5 %copy-start = (f32[8,256,256]{2,1,0:T(8,128)S(1)}, f32[8,256,256]{2,1,0:T(8,128)}, u32[]{:S(2)}) copy-start(f32[8,256,256]{2,1,0:T(8,128)} %param.3) | copy-start | bytes 6291460
  3.5 26.6 %collective-permute-start.2 = (f32[3,256,256]{2,1,0:T(8,128)}, f32[3,256,256]{2,1,0:T(8,128)}, u32[]{:S(2)}, u32[]{:S(2)}) collective-permute-start(f32[3,256,256]{2,1,0:T(8,128)} %get-tuple-element.45), channel_id=1, source_target_pairs={{0,1},{1,2},{2,3},{3,4},{4,5},{5,6},{6,7},{7,8},{8,9},{9,10},{10,1... | collective-permute-start | bytes 2359304 | tf_op jit(solution)/shard_map/ppermute | solution.py:25
  5.5 26.5 %collective-permute-start.3 = (f32[3,256,256]{2,1,0:T(8,128)}, f32[3,256,256]{2,1,0:T(8,128)S(1)}, u32[]{:S(2)}, u32[]{:S(2)}) collective-permute-start(f32[3,256,256]{2,1,0:T(8,128)} %get-tuple-element.44), channel_id=1, source_target_pairs={{1,0},{2,1},{3,2},{4,3},{5,4},{6,5},{7,6},{8,7},{9,8},{10,9},{11,1... | collective-permute-start | bytes 2359304 | tf_op jit(solution)/shard_map/ppermute | solution.py:25
  10.2 16.9 %collective-permute-start = (f32[2,256,256]{2,1,0:T(8,128)}, f32[2,256,256]{2,1,0:T(8,128)}, u32[]{:S(2)}, u32[]{:S(2)}) collective-permute-start(f32[2,256,256]{2,1,0:T(8,128)} %get-tuple-element.47), channel_id=1, source_target_pairs={{0,1},{1,2},{2,3},{3,4},{4,5},{5,6},{6,7},{7,8},{8,9},{9,10},{10,1... | collective-permute-start | bytes 1572872 | tf_op jit(solution)/shard_map/ppermute | solution.py:25
  12.4 17.6 %collective-permute-start.1 = (f32[2,256,256]{2,1,0:T(8,128)}, f32[2,256,256]{2,1,0:T(8,128)S(1)}, u32[]{:S(2)}, u32[]{:S(2)}) collective-permute-start(f32[2,256,256]{2,1,0:T(8,128)} %get-tuple-element.46), channel_id=1, source_target_pairs={{1,0},{2,1},{3,2},{4,3},{5,4},{6,5},{7,6},{8,7},{9,8},{10,9},{11,1... | collective-permute-start | bytes 1572872 | tf_op jit(solution)/shard_map/ppermute | solution.py:25
  18.3 11.7 %copy-start.60 = (f32[2,64,64]{2,1,0:T(8,128)}, f32[2,64,64]{2,1,0:T(8,128)S(1)}, u32[]{:S(2)}) copy-start(f32[2,64,64]{2,1,0:T(8,128)S(1)} %get-tuple-element.107) | copy-start | bytes 98308
  63.3 14.6 %collective-permute-start.4 = (f32[3,256,256]{2,1,0:T(8,128)}, f32[3,256,256]{2,1,0:T(8,128)}, u32[]{:S(2)}, u32[]{:S(2)}) collective-permute-start(f32[3,256,256]{2,1,0:T(8,128)} %get-tuple-element.8), channel_id=1, source_target_pairs={{0,1},{1,2},{2,3},{3,4},{4,5},{5,6},{6,7},{7,8},{8,9},{9,10},{10,1... | collective-permute-start | bytes 2359304 | tf_op jit(solution)/shard_map/ppermute | solution.py:25
  65.5 14.1 %collective-permute-start.5 = (f32[3,256,256]{2,1,0:T(8,128)}, f32[3,256,256]{2,1,0:T(8,128)}, u32[]{:S(2)}, u32[]{:S(2)}) collective-permute-start(f32[3,256,256]{2,1,0:T(8,128)} %get-tuple-element.9), channel_id=1, source_target_pairs={{1,0},{2,1},{3,2},{4,3},{5,4},{6,5},{7,6},{8,7},{9,8},{10,9},{11,1... | collective-permute-start | bytes 2359304 | tf_op jit(solution)/shard_map/ppermute | solution.py:25
  100.9 14.2 %copy-start.15 = (f32[128,4,128]{2,0,1:T(8,128)S(1)}, f32[128,4,128]{2,0,1:T(8,128)}, u32[]{:S(2)}) copy-start(f32[128,4,128]{2,0,1:T(8,128)} %get-tuple-element.103) | copy-start | bytes 786436
  103.4 10.9 %collective-permute-start.6 = (f32[142336]{0:T(1024)S(1)}, f32[142336]{0:T(1024)S(1)}, u32[]{:S(2)}, u32[]{:S(2)}) collective-permute-start(f32[142336]{0:T(1024)S(1)} %get-tuple-element.96), channel_id=1, source_target_pairs={{0,1},{1,2},{2,3},{3,4},{4,5},{5,6},{6,7},{7,8},{8,9},{9,10},{10,1... | collective-permute-start | bytes 1708040 | tf_op jit(solution)/shard_map/ppermute | solution.py:25
  104.7 10.4 %collective-permute-start.7 = (f32[142336]{0:T(1024)S(1)}, f32[142336]{0:T(1024)S(1)}, u32[]{:S(2)}, u32[]{:S(2)}) collective-permute-start(f32[142336]{0:T(1024)S(1)} %get-tuple-element.97), channel_id=1, source_target_pairs={{0,127},{1,0},{2,1},{3,2},{4,3},{5,4},{6,5},{7,6},{8,7},{9,8},{10,... | collective-permute-start | bytes 1708040 | tf_op jit(solution)/shard_map/ppermute | solution.py:25
  107.7 43.0 %copy-start.75 = (f32[1,32,32]{2,1,0:T(8,128)}, f32[1,32,32]{2,1,0:T(8,128)S(1)}, u32[]{:S(2)}) copy-start(f32[1,32,32]{2,1,0:T(8,128)S(1)} %copy.83) | copy-start | bytes 12292
  108.9 42.4 %copy-start.77 = (f32[1,32,32]{2,1,0:T(8,128)}, f32[1,32,32]{2,1,0:T(8,128)S(1)}, u32[]{:S(2)}) copy-start(f32[1,32,32]{2,1,0:T(8,128)S(1)} %copy.84) | copy-start | bytes 12292
  116.2 27.9 %copy-start.4 = (f32[8,128,128]{2,1,0:T(8,128)}, f32[8,128,128]{2,1,0:T(8,128)S(1)}, u32[]{:S(2)}) copy-start(f32[8,128,128]{2,1,0:T(8,128)S(1)} %get-tuple-element.66) | copy-start | bytes 1572868
  118.6 25.6 %copy-start.7 = (f32[8,128,128]{2,1,0:T(8,128)}, f32[8,128,128]{2,1,0:T(8,128)S(1)}, u32[]{:S(2)}) copy-start(f32[8,128,128]{2,1,0:T(8,128)S(1)} %get-tuple-element.15) | copy-start | bytes 1572868
  118.7 25.3 %copy-start.27 = (f32[128,4,128]{2,0,1:T(8,128)S(1)}, f32[128,4,128]{2,0,1:T(8,128)}, u32[]{:S(2)}) copy-start(f32[128,4,128]{2,0,1:T(8,128)} %copy-done.26) | copy-start | bytes 786436
  124.7 19.4 %copy-start.11 = (f32[8,128,128]{2,1,0:T(8,128)S(1)}, f32[8,128,128]{2,1,0:T(8,128)}, u32[]{:S(2)}) copy-start(f32[8,128,128]{2,1,0:T(8,128)} %copy-done.10) | copy-start | bytes 1572868
  125.4 23.0 %collective-permute-start.8 = (f32[13312]{0:T(1024)}, f32[13312]{0:T(1024)}, u32[]{:S(2)}, u32[]{:S(2)}) collective-permute-start(f32[13312]{0:T(1024)} %get-tuple-element.89), channel_id=1, source_target_pairs={{0,3},{1,4},{2,5},{3,6},{4,7},{5,8},{6,9},{7,10},{8,11},{9,12},{10... | collective-permute-start | bytes 159752 | tf_op jit(solution)/shard_map/ppermute | solution.py:25
  130.2 23.0 %collective-permute-start.9 = (f32[13312]{0:T(1024)}, f32[13312]{0:T(1024)}, u32[]{:S(2)}, u32[]{:S(2)}) collective-permute-start(f32[13312]{0:T(1024)} %get-tuple-element.88), channel_id=1, source_target_pairs={{0,125},{1,126},{2,127},{3,0},{4,1},{5,2},{6,3},{7,4},{8,5},{9,6},... | collective-permute-start | bytes 159752 | tf_op jit(solution)/shard_map/ppermute | solution.py:25
  144.2 16.1 %copy-start.47 = (f32[64,2,64]{2,0,1:T(8,128)S(1)}, f32[64,2,64]{2,0,1:T(8,128)}, u32[]{:S(2)}) copy-start(f32[64,2,64]{2,0,1:T(8,128)} %copy-done.46) | copy-start | bytes 98308
  145.3 16.4 %copy-start.28 = (f32[6,128,128]{2,1,0:T(8,128)}, f32[6,128,128]{2,1,0:T(8,128)S(1)}, u32[]{:S(2)}) copy-start(f32[6,128,128]{2,1,0:T(8,128)S(1)} %fusion.53) | copy-start | bytes 1179652
  147.1 14.7 %copy-start.100 = (f32[6]{0:T(128)S(1)}, f32[6]{0:T(128)}, u32[]{:S(2)}) copy-start(f32[6]{0:T(128)} %and_convert_fusion.2) | copy-start | bytes 76
  149.3 12.4 %copy-start.39 = (f32[9,32,32]{2,1,0:T(8,128)}, f32[9,32,32]{2,1,0:T(8,128)S(1)}, u32[]{:S(2)}) copy-start(f32[9,32,32]{2,1,0:T(8,128)S(1)} %reshape.493) | copy-start | bytes 110596
  154.7 15.8 %collective-permute-start.10 = (f32[27,32,32]{2,1,0:T(8,128)}, f32[27,32,32]{2,1,0:T(8,128)}, u32[]{:S(2)}, u32[]{:S(2)}) collective-permute-start(f32[27,32,32]{2,1,0:T(8,128)} %constant_dynamic-update-slice_fusion.13), channel_id=1, source_target_pairs={{0,9},{1,10},{2,11},{3,12},{4,13},{5,14},{6,15},{7,16},{8,17},{9,1... | collective-permute-start | bytes 331784 | tf_op jit(solution)/shard_map/ppermute | solution.py:25
  154.7 17.0 %collective-permute-start.11 = (f32[27,32,32]{2,1,0:T(8,128)}, f32[27,32,32]{2,1,0:T(8,128)}, u32[]{:S(2)}, u32[]{:S(2)}) collective-permute-start(f32[27,32,32]{2,1,0:T(8,128)} %constant_dynamic-update-slice_fusion.13), channel_id=1, source_target_pairs={{0,119},{1,120},{2,121},{3,122},{4,123},{5,124},{6,125},{7,126},{8... | collective-permute-start | bytes 331784 | tf_op jit(solution)/shard_map/ppermute | solution.py:25
  163.3 9.5 %copy-start.49 = (f32[6,64,64]{2,1,0:T(8,128)}, f32[6,64,64]{2,1,0:T(8,128)S(1)}, u32[]{:S(2)}) copy-start(f32[6,64,64]{2,1,0:T(8,128)S(1)} %get-tuple-element.33) | copy-start | bytes 294916
  163.3 9.5 %copy-start.101 = (f32[27]{0:T(128)S(1)}, f32[27]{0:T(128)}, u32[]{:S(2)}) copy-start(f32[27]{0:T(128)} %and_convert_fusion.4) | copy-start | bytes 328
  163.5 9.5 %copy-start.72 = (f32[4,64,64]{2,1,0:T(8,128)}, f32[4,64,64]{2,1,0:T(8,128)S(1)}, u32[]{:S(2)}) copy-start(f32[4,64,64]{2,1,0:T(8,128)S(1)} %fusion.168) | copy-start | bytes 196612
  182.5 11.9 %slice-start.8 = ((f32[4,64,64]{2,1,0:T(8,128)}), f32[2,64,64]{2,1,0:T(8,128)S(1)}, s32[]{:S(2)}) async-start(f32[4,64,64]{2,1,0:T(8,128)} %copy-done.72), calls=%async_computation.8 | async-start | bytes 131072 | tf_op jit(solution)/shard_map/slice | solution.py:141
  185.1 9.3 %copy-start.73 = (f32[4,64,64]{2,1,0:T(8,128)S(1)}, f32[4,64,64]{2,1,0:T(8,128)}, u32[]{:S(2)}) copy-start(f32[4,64,64]{2,1,0:T(8,128)} %copy-done.72) | copy-start | bytes 196612
  185.2 10.5 %copy-start.94 = (s32[128]{0:T(128)S(1)}, s32[128]{0:T(128)}, u32[]{:S(2)}) copy-start(s32[128]{0:T(128)} %copy-done.92) | copy-start | bytes 1540
  185.2 10.8 %copy-start.5 = (f32[8,128,128]{2,1,0:T(8,128)S(1)}, f32[8,128,128]{2,1,0:T(8,128)}, u32[]{:S(2)}) copy-start(f32[8,128,128]{2,1,0:T(8,128)} %copy-done.4) | copy-start | bytes 1572868
  185.2 10.8 %copy-start.8 = (f32[8,128,128]{2,1,0:T(8,128)S(1)}, f32[8,128,128]{2,1,0:T(8,128)}, u32[]{:S(2)}) copy-start(f32[8,128,128]{2,1,0:T(8,128)} %copy-done.7) | copy-start | bytes 1572868
  185.2 10.8 %copy-start.12 = (f32[8,128,128]{2,1,0:T(8,128)S(1)}, f32[8,128,128]{2,1,0:T(8,128)}, u32[]{:S(2)}) copy-start(f32[8,128,128]{2,1,0:T(8,128)} %copy-done.10) | copy-start | bytes 1572868
  185.2 10.8 %copy-start.25 = (f32[8,128,128]{2,1,0:T(8,128)S(1)}, f32[8,128,128]{2,1,0:T(8,128)}, u32[]{:S(2)}) copy-start(f32[8,128,128]{2,1,0:T(8,128)} %copy-done.24) | copy-start | bytes 1572868
  185.2 10.8 %copy-start.31 = (f32[6,128,128]{2,1,0:T(8,128)S(1)}, f32[6,128,128]{2,1,0:T(8,128)}, u32[]{:S(2)}) copy-start(f32[6,128,128]{2,1,0:T(8,128)} %copy-done.30) | copy-start | bytes 1179652
  185.2 10.8 %slice-start.1 = ((f32[6,128,128]{2,1,0:T(8,128)}), f32[4,128,128]{2,1,0:T(8,128)S(1)}, s32[]{:S(2)}) async-start(f32[6,128,128]{2,1,0:T(8,128)} %copy-done.30), calls=%async_computation.1 | async-start | bytes 524288 | tf_op jit(solution)/shard_map/slice | solution.py:141
  185.2 10.8 %copy-start.88 = (s32[256]{0:T(256)S(1)}, s32[256]{0:T(256)}, u32[]{:S(2)}) copy-start(s32[256]{0:T(256)} %copy-done.86) | copy-start | bytes 3076
  198.2 11.9 %slice-start.7 = ((f32[4,64,64]{2,1,0:T(8,128)}), f32[2,64,64]{2,1,0:T(8,128)S(1)}, s32[]{:S(2)}) async-start(f32[4,64,64]{2,1,0:T(8,128)} %copy-done.70), calls=%async_computation.7 | async-start | bytes 131072 | tf_op jit(solution)/shard_map/slice | solution.py:141
  199.2 9.3 %slice-start.9 = ((f32[3,32,32]{2,1,0:T(8,128)}), f32[1,32,32]{2,1,0:T(8,128)S(1)}, s32[]{:S(2)}) async-start(f32[3,32,32]{2,1,0:T(8,128)} %copy-done.81), calls=%async_computation.9 | async-start | bytes 32768 | tf_op jit(solution)/shard_map/slice | solution.py:141
  200.9 9.2 %copy-start.95 = (s32[128]{0:T(128)S(1)}, s32[128]{0:T(128)}, u32[]{:S(2)}) copy-start(s32[128]{0:T(128)} %copy-done.92) | copy-start | bytes 1540
  200.9 10.8 %copy-start.6 = (f32[8,128,128]{2,1,0:T(8,128)S(1)}, f32[8,128,128]{2,1,0:T(8,128)}, u32[]{:S(2)}) copy-start(f32[8,128,128]{2,1,0:T(8,128)} %copy-done.4) | copy-start | bytes 1572868
  201.0 10.8 %copy-start.9 = (f32[8,128,128]{2,1,0:T(8,128)S(1)}, f32[8,128,128]{2,1,0:T(8,128)}, u32[]{:S(2)}) copy-start(f32[8,128,128]{2,1,0:T(8,128)} %copy-done.7) | copy-start | bytes 1572868
  201.0 10.8 %copy-start.13 = (f32[8,128,128]{2,1,0:T(8,128)S(1)}, f32[8,128,128]{2,1,0:T(8,128)}, u32[]{:S(2)}) copy-start(f32[8,128,128]{2,1,0:T(8,128)} %copy-done.10) | copy-start | bytes 1572868
  201.0 10.8 %copy-start.23 = (f32[8,128,128]{2,1,0:T(8,128)S(1)}, f32[8,128,128]{2,1,0:T(8,128)}, u32[]{:S(2)}) copy-start(f32[8,128,128]{2,1,0:T(8,128)} %copy-done.22) | copy-start | bytes 1572868
  201.0 10.8 %copy-start.29 = (f32[6,128,128]{2,1,0:T(8,128)S(1)}, f32[6,128,128]{2,1,0:T(8,128)}, u32[]{:S(2)}) copy-start(f32[6,128,128]{2,1,0:T(8,128)} %copy-done.28) | copy-start | bytes 1179652
  201.0 10.8 %slice-start = ((f32[6,128,128]{2,1,0:T(8,128)}), f32[4,128,128]{2,1,0:T(8,128)S(1)}, s32[]{:S(2)}) async-start(f32[6,128,128]{2,1,0:T(8,128)} %copy-done.28), calls=%async_computation | async-start | bytes 524288 | tf_op jit(solution)/shard_map/slice | solution.py:141
  201.0 10.8 %copy-start.89 = (s32[256]{0:T(256)S(1)}, s32[256]{0:T(256)}, u32[]{:S(2)}) copy-start(s32[256]{0:T(256)} %copy-done.86) | copy-start | bytes 3076
  (80 other events, 347.8 us)

commit v7 on v5

--- a/solution.py
+++ b/solution.py
@@ -148,7 +148,7 @@
     return update
 
 
-ROWS = 64
+ROWS = 128
 PAD = 8
 VMEM_LIMIT = 64 * 1024 * 1024
 

time: 214 us -> 215 us (level)
  no operation moved by 1% of the time
where the time goes in v7:
time: 215 us; the launch traced here: 213 us
  other arithmetic  47 us (22%)
  local copies, waits for them, and re-layouts  43.1 us (20%)
  starting transfers between devices  35.2 us (16%)
  Pallas kernels  34.2 us (16%)
  matrix products  29.6 us (14%)
  waiting for transfers between devices  20.6 us (10%)
  between operations  3.01 us (1%)
    ppermute x10, starting transfers between devices, recv(): return lax.ppermute(value, 'gx', pairs)  35.2 us
    pallas_call x2, Pallas kernels, _vmem_call(): pl.pallas_call(kernel, out_shape=outs, in_specs=[pl.BlockSpec(memory_spac...  34.2 us
    ppermute x10, waiting for transfers between devices, recv(): return lax.ppermute(value, 'gx', pairs)  20.6 us
    unnamed x239, local copies, waits for them, and re-layouts  15.5 us
    dot_general x12, matrix products, shrink_sides(): jnp.einsum('xyz,zw->xyw', field, pair_matrix(extent_z), precision=EXACT)  9.56 us
    div x1, other arithmetic, make_coefs(): OMEGA / diag  7.61 us
    reduce_sum x7, other arithmetic, coarsen(): planes = field.reshape(extent_x // 2, 2, extent_y, extent_z).sum(axis=1)  7.52 us
    div x5, other arithmetic, make_coefs(): faces = [two_s / (safe + jnp.where(nb > 0, nb, safe)) for nb in near]  7.4 us
  transfers between devices with their start and end apart: 10, of which 6 were waited for; matrix products, arithmetic and copies ran while one was open for 15% of the time, Pallas kernels for 0%

profile of v7, /device:TPU:48, one launch (start us, length us, event | category | flops | bytes accessed | tf_op | source)
XLA Modules:
  0.0 212.7 jit_solution(17598570886755655108)
XLA Ops:
  0.6 1.6 fusion.598
  2.8 1.2 pad_maximum_fusion.11
  3.9 2.0 collective-permute-start
  6.0 1.2 pad_maximum_fusion.12
  7.1 3.6 %collective-permute-start.1 = (f32[5,256,256]{2,1,0:T(8,128)}, f32[5,256,256]{2,1,0:T(8,128)}, u32[]{:S(2)}, u32[]{:S(2)}) collective-permute-start(f32[5,256,256]{2,1,0:T(8,128)} %pad_maximum_fusion.12), channel_id=1, source_target_pairs={{1,0},{2,1},{3,2},{4,3},{5,4},{6,5},{7,6},{8,7},{9,8},{10,9},{11,1... | collective-permute-start | bytes 3932168 | tf_op jit(solution)/shard_map/ppermute | solution.py:25
  11.8 1.1 bitcast_reduce_fusion.3
  19.2 4.1 %collective-permute-done = f32[5,256,256]{2,1,0:T(8,128)} collective-permute-done((f32[5,256,256]{2,1,0:T(8,128)}, f32[5,256,256]{2,1,0:T(8,128)}, u32[]{:S(2)}, u32[]{:S(2)}) %collective-permute-start) | collective-permute-done | bytes 1310752 | tf_op jit(solution)/shard_map/ppermute | solution.py:25
  23.3 1.2 slice.1717
  24.5 1.7 collective-permute-done.1
  26.2 1.2 slice.1718
  28.8 7.6 %broadcast_divide_fusion = (f32[12,256,256]{2,1,0:T(8,128)}, f32[12,256,256]{2,1,0:T(8,128)}, f32[12,256,256]{2,1,0:T(8,128)}) fusion(f32[12,258,1]{2,1,0:T(8,128)S(1)} %get-tuple-element.38, f32[12,1,256]{2,1,0:T(1,128)S(1)} %get-tuple-element.36, f32[12,256,256]{2,1,0:T(8,128)S(1)} %slice.1721, f32[12,1,256]{2,1,0:T(1,128)S(1)} %get-tuple-element.37, ...), kind=kLoop, calls=%fused_computation.40 | loop fusion | flops 33030144 | bytes 22069440 | tf_op jit(solution)/shard_map/div | solution.py:120
  36.4 5.7 %fusion.13 = (f32[12,256,256]{2,1,0:T(8,128)}, f32[12,256,256]{2,1,0:T(8,128)}, f32[12,256,256]{2,1,0:T(8,128)}) fusion(f32[12,258,1]{2,1,0:T(8,128)S(1)} %get-tuple-element.38, f32[12,1,256]{2,1,0:T(1,128)S(1)} %get-tuple-element.36, f32[12,256,256]{2,1,0:T(8,128)S(1)} %slice.1721, f32[12,1,256]{2,1,0:T(1,128)S(1)} %get-tuple-element.37, ...), kind=kLoop, calls=%fused_computation.23 | loop fusion | flops 16515072 | bytes 12632256 | tf_op jit(solution)/shard_map/div | solution.py:109
  42.2 2.5 %divide_select_fusion.kxo_full = f32[13,256,256]{2,1,0:T(8,128)} fusion(f32[14,256,256]{2,1,0:T(8,128)S(1)} %pad_maximum_fusion), kind=kLoop, calls=%fused_computation.14 | loop fusion | flops 5111808 | bytes 10223616 | tf_op jit(solution)/shard_map/jit(_where)/select_n | solution.py:113
  44.6 1.1 slice.1715
  45.7 1.1 slice.1716
  46.8 1.9 pad_maximum_fusion.10.resid.rhs
  48.7 14.4 %shard_map.41 = (f32[8,256,256]{2,1,0:T(8,128)}, f32[3,256,256]{2,1,0:T(8,128)}, f32[3,256,256]{2,1,0:T(8,128)}) custom-call(f32[12,256,256]{2,1,0:T(8,128)} %pad_maximum_fusion.10.resid.rhs, f32[13,256,256]{2,1,0:T(8,128)} %divide_select_fusion.kxo_full, f32[12,256,256]{2,1,0:T(8,128)} %get-tuple-element.42.kyl, f32[12,256,256]{2,1,0:T(8,128)} %get-tuple-element.43.kyh, ...), custom_call_target="tpu_custom_call" | custom-call | tf_op jit(solution)/shard_map/pallas_call | solution.py:276
  63.2 4.1 %collective-permute-start.2 = (f32[3,256,256]{2,1,0:T(8,128)}, f32[3,256,256]{2,1,0:T(8,128)}, u32[]{:S(2)}, u32[]{:S(2)}) collective-permute-start(f32[3,256,256]{2,1,0:T(8,128)} %get-tuple-element.8), channel_id=1, source_target_pairs={{0,1},{1,2},{2,3},{3,4},{4,5},{5,6},{6,7},{7,8},{8,9},{9,10},{10,1... | collective-permute-start | bytes 2359304 | tf_op jit(solution)/shard_map/ppermute | solution.py:25
  67.3 2.1 collective-permute-start.3
  69.4 1.4 constant_dynamic-update-slice_fusion.38
  70.8 1.5 fusion.21
  73.3 1.4 fusion.23
  74.8 1.8 fusion.608
  76.9 2.0 collective-permute-done.3.fine_r
  79.0 19.8 %shard_map.42 = (f32[8,256,256]{2,1,0:T(8,128)}, f32[8,256,256]{2,1,0:T(8,128)}) custom-call(f32[3,256,256]{2,1,0:T(8,128)} %collective-permute-done.2.fine_l, f32[8,256,256]{2,1,0:T(8,128)} %get-tuple-element.7.fine, f32[3,256,256]{2,1,0:T(8,128)} %collective-permute-done.3.fine_r, f32[12,256,256]{2,1,0:T(8,128)} %pad_maximum_fusion.10.resid.rhs, ...), custom_call_target="tpu_custom_call" | custom-call | tf_op jit(solution)/shard_map/pallas_call | solution.py:276
  98.8 2.0 bitcast_reduce_fusion.1
  103.4 2.0 collective-permute-start.4
  107.5 5.5 %collective-permute-done.4 = f32[142336]{0:T(1024)S(1)} collective-permute-done((f32[142336]{0:T(1024)S(1)}, f32[142336]{0:T(1024)S(1)}, u32[]{:S(2)}, u32[]{:S(2)}) %collective-permute-start.4) | collective-permute-done | bytes 569376 | tf_op jit(solution)/shard_map/ppermute | solution.py:25
  124.1 4.6 %collective-permute-start.6 = (f32[13312]{0:T(1024)}, f32[13312]{0:T(1024)}, u32[]{:S(2)}, u32[]{:S(2)}) collective-permute-start(f32[13312]{0:T(1024)} %get-tuple-element.89), channel_id=1, source_target_pairs={{0,3},{1,4},{2,5},{3,6},{4,7},{5,8},{6,9},{7,10},{8,11},{9,12},{10... | collective-permute-start | bytes 159752 | tf_op jit(solution)/shard_map/ppermute | solution.py:25
  128.7 11.7 %collective-permute-start.7 = (f32[13312]{0:T(1024)}, f32[13312]{0:T(1024)}, u32[]{:S(2)}, u32[]{:S(2)}) collective-permute-start(f32[13312]{0:T(1024)} %get-tuple-element.88), channel_id=1, source_target_pairs={{0,125},{1,126},{2,127},{3,0},{4,1},{5,2},{6,3},{7,4},{8,5},{9,6},... | collective-permute-start | bytes 159752 | tf_op jit(solution)/shard_map/ppermute | solution.py:25
  151.2 4.8 %collective-permute-start.9 = (f32[27,32,32]{2,1,0:T(8,128)}, f32[27,32,32]{2,1,0:T(8,128)}, u32[]{:S(2)}, u32[]{:S(2)}) collective-permute-start(f32[27,32,32]{2,1,0:T(8,128)} %constant_dynamic-update-slice_fusion.7), channel_id=1, source_target_pairs={{0,119},{1,120},{2,121},{3,122},{4,123},{5,124},{6,125},{7,126},{8... | collective-permute-start | bytes 331784 | tf_op jit(solution)/shard_map/ppermute | solution.py:25
  158.2 1.3 fusion.590
  160.1 6.8 %collective-permute-done.8 = f32[27,32,32]{2,1,0:T(8,128)} collective-permute-done((f32[27,32,32]{2,1,0:T(8,128)}, f32[27,32,32]{2,1,0:T(8,128)}, u32[]{:S(2)}, u32[]{:S(2)}) %collective-permute-start.8) | collective-permute-done | bytes 110624 | tf_op jit(solution)/shard_map/ppermute | solution.py:25
  172.0 1.7 reduce_sum.117
  173.7 1.5 fusion.539
  179.8 1.7 reduce_sum.119
  181.7 1.7 fusion.534
  183.5 1.2 fusion.199
  184.8 1.9 slice_multiply_fusion.14
  191.0 1.3 fusion.284
  193.2 1.6 convolution_bitcast_fusion
  195.7 1.8 reduce_sum.118
  197.6 1.6 fusion.537
  200.1 1.1 fusion.241
  205.1 1.2 fusion.25
  206.7 1.3 fusion.267
  209.6 1.7 bitcast_add_fusion
  211.2 1.5 broadcast_in_dim.38
  (423 shorter events, 61.1 us)
Async XLA Ops:
  3.9 19.4 %collective-permute-start = (f32[5,256,256]{2,1,0:T(8,128)}, f32[5,256,256]{2,1,0:T(8,128)}, u32[]{:S(2)}, u32[]{:S(2)}) collective-permute-start(f32[5,256,256]{2,1,0:T(8,128)} %pad_maximum_fusion.11), channel_id=1, source_target_pairs={{0,1},{1,2},{2,3},{3,4},{4,5},{5,6},{6,7},{7,8},{8,9},{9,10},{10,1... | collective-permute-start | bytes 3932168 | tf_op jit(solution)/shard_map/ppermute | solution.py:25
  7.1 19.1 %collective-permute-start.1 = (f32[5,256,256]{2,1,0:T(8,128)}, f32[5,256,256]{2,1,0:T(8,128)}, u32[]{:S(2)}, u32[]{:S(2)}) collective-permute-start(f32[5,256,256]{2,1,0:T(8,128)} %pad_maximum_fusion.12), channel_id=1, source_target_pairs={{1,0},{2,1},{3,2},{4,3},{5,4},{6,5},{7,6},{8,7},{9,8},{10,9},{11,1... | collective-permute-start | bytes 3932168 | tf_op jit(solution)/shard_map/ppermute | solution.py:25
  13.4 14.0 %copy-start.46 = (f32[64,2,64]{2,0,1:T(8,128)}, f32[64,2,64]{2,0,1:T(8,128)S(1)}, u32[]{:S(2)}) copy-start(f32[64,2,64]{2,0,1:T(8,128)S(1)} %copy.81) | copy-start | bytes 98308
  14.5 13.2 %copy-start.26 = (f32[128,4,128]{2,0,1:T(8,128)}, f32[128,4,128]{2,0,1:T(8,128)S(1)}, u32[]{:S(2)}) copy-start(f32[128,4,128]{2,0,1:T(8,128)S(1)} %get-tuple-element.99) | copy-start | bytes 786436
  15.6 12.1 %copy-start.60 = (f32[2,64,64]{2,1,0:T(8,128)}, f32[2,64,64]{2,1,0:T(8,128)S(1)}, u32[]{:S(2)}) copy-start(f32[2,64,64]{2,1,0:T(8,128)S(1)} %get-tuple-element.107) | copy-start | bytes 98308
  63.2 13.8 %collective-permute-start.2 = (f32[3,256,256]{2,1,0:T(8,128)}, f32[3,256,256]{2,1,0:T(8,128)}, u32[]{:S(2)}, u32[]{:S(2)}) collective-permute-start(f32[3,256,256]{2,1,0:T(8,128)} %get-tuple-element.8), channel_id=1, source_target_pairs={{0,1},{1,2},{2,3},{3,4},{4,5},{5,6},{6,7},{7,8},{8,9},{9,10},{10,1... | collective-permute-start | bytes 2359304 | tf_op jit(solution)/shard_map/ppermute | solution.py:25
  67.3 11.7 %collective-permute-start.3 = (f32[3,256,256]{2,1,0:T(8,128)}, f32[3,256,256]{2,1,0:T(8,128)}, u32[]{:S(2)}, u32[]{:S(2)}) collective-permute-start(f32[3,256,256]{2,1,0:T(8,128)} %get-tuple-element.9), channel_id=1, source_target_pairs={{1,0},{2,1},{3,2},{4,3},{5,4},{6,5},{7,6},{8,7},{9,8},{10,9},{11,1... | collective-permute-start | bytes 2359304 | tf_op jit(solution)/shard_map/ppermute | solution.py:25
  100.9 13.0 %copy-start.15 = (f32[128,4,128]{2,0,1:T(8,128)S(1)}, f32[128,4,128]{2,0,1:T(8,128)}, u32[]{:S(2)}) copy-start(f32[128,4,128]{2,0,1:T(8,128)} %get-tuple-element.103) | copy-start | bytes 786436
  103.4 9.6 %collective-permute-start.4 = (f32[142336]{0:T(1024)S(1)}, f32[142336]{0:T(1024)S(1)}, u32[]{:S(2)}, u32[]{:S(2)}) collective-permute-start(f32[142336]{0:T(1024)S(1)} %get-tuple-element.96), channel_id=1, source_target_pairs={{0,1},{1,2},{2,3},{3,4},{4,5},{5,6},{6,7},{7,8},{8,9},{9,10},{10,1... | collective-permute-start | bytes 1708040 | tf_op jit(solution)/shard_map/ppermute | solution.py:25
  105.4 8.5 %collective-permute-start.5 = (f32[142336]{0:T(1024)S(1)}, f32[142336]{0:T(1024)S(1)}, u32[]{:S(2)}, u32[]{:S(2)}) collective-permute-start(f32[142336]{0:T(1024)S(1)} %get-tuple-element.97), channel_id=1, source_target_pairs={{0,127},{1,0},{2,1},{3,2},{4,3},{5,4},{6,5},{7,6},{8,7},{9,8},{10,... | collective-permute-start | bytes 1708040 | tf_op jit(solution)/shard_map/ppermute | solution.py:25
  106.3 40.8 %copy-start.75 = (f32[1,32,32]{2,1,0:T(8,128)}, f32[1,32,32]{2,1,0:T(8,128)S(1)}, u32[]{:S(2)}) copy-start(f32[1,32,32]{2,1,0:T(8,128)S(1)} %copy.83) | copy-start | bytes 12292
  107.5 40.2 %copy-start.77 = (f32[1,32,32]{2,1,0:T(8,128)}, f32[1,32,32]{2,1,0:T(8,128)S(1)}, u32[]{:S(2)}) copy-start(f32[1,32,32]{2,1,0:T(8,128)S(1)} %copy.84) | copy-start | bytes 12292
  114.9 25.7 %copy-start.4 = (f32[8,128,128]{2,1,0:T(8,128)}, f32[8,128,128]{2,1,0:T(8,128)S(1)}, u32[]{:S(2)}) copy-start(f32[8,128,128]{2,1,0:T(8,128)S(1)} %get-tuple-element.66) | copy-start | bytes 1572868
  117.3 23.3 %copy-start.7 = (f32[8,128,128]{2,1,0:T(8,128)}, f32[8,128,128]{2,1,0:T(8,128)S(1)}, u32[]{:S(2)}) copy-start(f32[8,128,128]{2,1,0:T(8,128)S(1)} %get-tuple-element.15) | copy-start | bytes 1572868
  117.4 23.0 %copy-start.27 = (f32[128,4,128]{2,0,1:T(8,128)S(1)}, f32[128,4,128]{2,0,1:T(8,128)}, u32[]{:S(2)}) copy-start(f32[128,4,128]{2,0,1:T(8,128)} %copy-done.26) | copy-start | bytes 786436
  123.4 17.2 %copy-start.11 = (f32[8,128,128]{2,1,0:T(8,128)S(1)}, f32[8,128,128]{2,1,0:T(8,128)}, u32[]{:S(2)}) copy-start(f32[8,128,128]{2,1,0:T(8,128)} %copy-done.10) | copy-start | bytes 1572868
  124.1 20.8 %collective-permute-start.6 = (f32[13312]{0:T(1024)}, f32[13312]{0:T(1024)}, u32[]{:S(2)}, u32[]{:S(2)}) collective-permute-start(f32[13312]{0:T(1024)} %get-tuple-element.89), channel_id=1, source_target_pairs={{0,3},{1,4},{2,5},{3,6},{4,7},{5,8},{6,9},{7,10},{8,11},{9,12},{10... | collective-permute-start | bytes 159752 | tf_op jit(solution)/shard_map/ppermute | solution.py:25
  128.7 20.9 %collective-permute-start.7 = (f32[13312]{0:T(1024)}, f32[13312]{0:T(1024)}, u32[]{:S(2)}, u32[]{:S(2)}) collective-permute-start(f32[13312]{0:T(1024)} %get-tuple-element.88), channel_id=1, source_target_pairs={{0,125},{1,126},{2,127},{3,0},{4,1},{5,2},{6,3},{7,4},{8,5},{9,6},... | collective-permute-start | bytes 159752 | tf_op jit(solution)/shard_map/ppermute | solution.py:25
  140.6 16.1 %copy-start.47 = (f32[64,2,64]{2,0,1:T(8,128)S(1)}, f32[64,2,64]{2,0,1:T(8,128)}, u32[]{:S(2)}) copy-start(f32[64,2,64]{2,0,1:T(8,128)} %copy-done.46) | copy-start | bytes 98308
  141.8 16.4 %copy-start.28 = (f32[6,128,128]{2,1,0:T(8,128)}, f32[6,128,128]{2,1,0:T(8,128)S(1)}, u32[]{:S(2)}) copy-start(f32[6,128,128]{2,1,0:T(8,128)S(1)} %fusion.53) | copy-start | bytes 1179652
  143.5 14.7 %copy-start.100 = (f32[6]{0:T(128)S(1)}, f32[6]{0:T(128)}, u32[]{:S(2)}) copy-start(f32[6]{0:T(128)} %and_convert_fusion.2) | copy-start | bytes 76
  145.8 12.4 %copy-start.39 = (f32[9,32,32]{2,1,0:T(8,128)}, f32[9,32,32]{2,1,0:T(8,128)S(1)}, u32[]{:S(2)}) copy-start(f32[9,32,32]{2,1,0:T(8,128)S(1)} %reshape.493) | copy-start | bytes 110596
  151.2 15.8 %collective-permute-start.8 = (f32[27,32,32]{2,1,0:T(8,128)}, f32[27,32,32]{2,1,0:T(8,128)}, u32[]{:S(2)}, u32[]{:S(2)}) collective-permute-start(f32[27,32,32]{2,1,0:T(8,128)} %constant_dynamic-update-slice_fusion.7), channel_id=1, source_target_pairs={{0,9},{1,10},{2,11},{3,12},{4,13},{5,14},{6,15},{7,16},{8,17},{9,1... | collective-permute-start | bytes 331784 | tf_op jit(solution)/shard_map/ppermute | solution.py:25
  151.2 17.0 %collective-permute-start.9 = (f32[27,32,32]{2,1,0:T(8,128)}, f32[27,32,32]{2,1,0:T(8,128)}, u32[]{:S(2)}, u32[]{:S(2)}) collective-permute-start(f32[27,32,32]{2,1,0:T(8,128)} %constant_dynamic-update-slice_fusion.7), channel_id=1, source_target_pairs={{0,119},{1,120},{2,121},{3,122},{4,123},{5,124},{6,125},{7,126},{8... | collective-permute-start | bytes 331784 | tf_op jit(solution)/shard_map/ppermute | solution.py:25
  159.7 9.5 %copy-start.49 = (f32[6,64,64]{2,1,0:T(8,128)}, f32[6,64,64]{2,1,0:T(8,128)S(1)}, u32[]{:S(2)}) copy-start(f32[6,64,64]{2,1,0:T(8,128)S(1)} %get-tuple-element.33) | copy-start | bytes 294916
  159.7 9.5 %copy-start.101 = (f32[27]{0:T(128)S(1)}, f32[27]{0:T(128)}, u32[]{:S(2)}) copy-start(f32[27]{0:T(128)} %and_convert_fusion.4) | copy-start | bytes 328
  159.9 9.5 %copy-start.72 = (f32[4,64,64]{2,1,0:T(8,128)}, f32[4,64,64]{2,1,0:T(8,128)S(1)}, u32[]{:S(2)}) copy-start(f32[4,64,64]{2,1,0:T(8,128)S(1)} %fusion.168) | copy-start | bytes 196612
  179.0 12.0 %slice-start.8 = ((f32[4,64,64]{2,1,0:T(8,128)}), f32[2,64,64]{2,1,0:T(8,128)S(1)}, s32[]{:S(2)}) async-start(f32[4,64,64]{2,1,0:T(8,128)} %copy-done.72), calls=%async_computation.8 | async-start | bytes 131072 | tf_op jit(solution)/shard_map/slice | solution.py:141
  181.6 9.4 %copy-start.73 = (f32[4,64,64]{2,1,0:T(8,128)S(1)}, f32[4,64,64]{2,1,0:T(8,128)}, u32[]{:S(2)}) copy-start(f32[4,64,64]{2,1,0:T(8,128)} %copy-done.72) | copy-start | bytes 196612
  181.6 10.6 %copy-start.94 = (s32[128]{0:T(128)S(1)}, s32[128]{0:T(128)}, u32[]{:S(2)}) copy-start(s32[128]{0:T(128)} %copy-done.92) | copy-start | bytes 1540
  181.6 11.0 %copy-start.5 = (f32[8,128,128]{2,1,0:T(8,128)S(1)}, f32[8,128,128]{2,1,0:T(8,128)}, u32[]{:S(2)}) copy-start(f32[8,128,128]{2,1,0:T(8,128)} %copy-done.4) | copy-start | bytes 1572868
  181.6 11.0 %copy-start.8 = (f32[8,128,128]{2,1,0:T(8,128)S(1)}, f32[8,128,128]{2,1,0:T(8,128)}, u32[]{:S(2)}) copy-start(f32[8,128,128]{2,1,0:T(8,128)} %copy-done.7) | copy-start | bytes 1572868
  181.6 11.0 %copy-start.12 = (f32[8,128,128]{2,1,0:T(8,128)S(1)}, f32[8,128,128]{2,1,0:T(8,128)}, u32[]{:S(2)}) copy-start(f32[8,128,128]{2,1,0:T(8,128)} %copy-done.10) | copy-start | bytes 1572868
  181.6 11.0 %copy-start.25 = (f32[8,128,128]{2,1,0:T(8,128)S(1)}, f32[8,128,128]{2,1,0:T(8,128)}, u32[]{:S(2)}) copy-start(f32[8,128,128]{2,1,0:T(8,128)} %copy-done.24) | copy-start | bytes 1572868
  181.6 11.0 %copy-start.31 = (f32[6,128,128]{2,1,0:T(8,128)S(1)}, f32[6,128,128]{2,1,0:T(8,128)}, u32[]{:S(2)}) copy-start(f32[6,128,128]{2,1,0:T(8,128)} %copy-done.30) | copy-start | bytes 1179652
  181.6 11.0 %slice-start.1 = ((f32[6,128,128]{2,1,0:T(8,128)}), f32[4,128,128]{2,1,0:T(8,128)S(1)}, s32[]{:S(2)}) async-start(f32[6,128,128]{2,1,0:T(8,128)} %copy-done.30), calls=%async_computation.1 | async-start | bytes 524288 | tf_op jit(solution)/shard_map/slice | solution.py:141
  181.7 11.0 %copy-start.88 = (s32[256]{0:T(256)S(1)}, s32[256]{0:T(256)}, u32[]{:S(2)}) copy-start(s32[256]{0:T(256)} %copy-done.86) | copy-start | bytes 3076
  194.8 11.9 %slice-start.7 = ((f32[4,64,64]{2,1,0:T(8,128)}), f32[2,64,64]{2,1,0:T(8,128)S(1)}, s32[]{:S(2)}) async-start(f32[4,64,64]{2,1,0:T(8,128)} %copy-done.70), calls=%async_computation.7 | async-start | bytes 131072 | tf_op jit(solution)/shard_map/slice | solution.py:141
  195.7 9.3 %slice-start.9 = ((f32[3,32,32]{2,1,0:T(8,128)}), f32[1,32,32]{2,1,0:T(8,128)S(1)}, s32[]{:S(2)}) async-start(f32[3,32,32]{2,1,0:T(8,128)} %copy-done.81), calls=%async_computation.9 | async-start | bytes 32768 | tf_op jit(solution)/shard_map/slice | solution.py:141
  197.5 9.2 %copy-start.71 = (f32[4,64,64]{2,1,0:T(8,128)S(1)}, f32[4,64,64]{2,1,0:T(8,128)}, u32[]{:S(2)}) copy-start(f32[4,64,64]{2,1,0:T(8,128)} %copy-done.70) | copy-start | bytes 196612
  197.5 9.2 %copy-start.95 = (s32[128]{0:T(128)S(1)}, s32[128]{0:T(128)}, u32[]{:S(2)}) copy-start(s32[128]{0:T(128)} %copy-done.92) | copy-start | bytes 1540
  197.5 10.8 %copy-start.6 = (f32[8,128,128]{2,1,0:T(8,128)S(1)}, f32[8,128,128]{2,1,0:T(8,128)}, u32[]{:S(2)}) copy-start(f32[8,128,128]{2,1,0:T(8,128)} %copy-done.4) | copy-start | bytes 1572868
  197.5 10.8 %copy-start.9 = (f32[8,128,128]{2,1,0:T(8,128)S(1)}, f32[8,128,128]{2,1,0:T(8,128)}, u32[]{:S(2)}) copy-start(f32[8,128,128]{2,1,0:T(8,128)} %copy-done.7) | copy-start | bytes 1572868
  197.5 10.8 %copy-start.13 = (f32[8,128,128]{2,1,0:T(8,128)S(1)}, f32[8,128,128]{2,1,0:T(8,128)}, u32[]{:S(2)}) copy-start(f32[8,128,128]{2,1,0:T(8,128)} %copy-done.10) | copy-start | bytes 1572868
  197.6 10.8 %copy-start.23 = (f32[8,128,128]{2,1,0:T(8,128)S(1)}, f32[8,128,128]{2,1,0:T(8,128)}, u32[]{:S(2)}) copy-start(f32[8,128,128]{2,1,0:T(8,128)} %copy-done.22) | copy-start | bytes 1572868
  197.6 10.8 %copy-start.29 = (f32[6,128,128]{2,1,0:T(8,128)S(1)}, f32[6,128,128]{2,1,0:T(8,128)}, u32[]{:S(2)}) copy-start(f32[6,128,128]{2,1,0:T(8,128)} %copy-done.28) | copy-start | bytes 1179652
  197.6 10.8 %slice-start = ((f32[6,128,128]{2,1,0:T(8,128)}), f32[4,128,128]{2,1,0:T(8,128)S(1)}, s32[]{:S(2)}) async-start(f32[6,128,128]{2,1,0:T(8,128)} %copy-done.28), calls=%async_computation | async-start | bytes 524288 | tf_op jit(solution)/shard_map/slice | solution.py:141
  197.6 10.8 %copy-start.89 = (s32[256]{0:T(256)S(1)}, s32[256]{0:T(256)}, u32[]{:S(2)}) copy-start(s32[256]{0:T(256)} %copy-done.86) | copy-start | bytes 3076
  (78 other events, 334.0 us)

commit v8 on v5

--- a/solution.py
+++ b/solution.py
@@ -251,22 +251,22 @@
 
         _plane_loop(first, first + src.shape[0], extent_y, copy_in)
 
-    def residual(q, y0):
+    ghosts = SWEEPS - 1
+
+    def residual(q, y0, keep=False):
         rows = pl.ds(y0, ROWS)
         center, off = _neighbour_sum(
             held, q + 1, y0, kxo_full[q, rows, :], kxo_full[q + 1, rows, :],
             kyl[q, rows, :], kyh[q, rows, :], kzl[q, rows, :], kzh[q, rows, :],
         )
-        resid[q, rows, :] = rhs[q, rows, :] - (diag[q, rows, :] * center - off)
-
-    _plane_loop(0, planes - 2, extent_y, residual)
-    ghosts = SWEEPS - 1
-
-    def copy_out(q, y0):
-        rows = pl.ds(y0, ROWS)
-        resid_out[q - ghosts, rows, :] = resid[q, rows, :]
-
-    _plane_loop(ghosts, planes - 2 - ghosts, extent_y, copy_out)
+        value = rhs[q, rows, :] - (diag[q, rows, :] * center - off)
+        resid[q, rows, :] = value
+        if keep:
+            resid_out[q - ghosts, rows, :] = value
+
+    _plane_loop(0, ghosts, extent_y, residual)
+    _plane_loop(ghosts, planes - 2 - ghosts, extent_y, lambda q, y0: residual(q, y0, True))
+    _plane_loop(planes - 2 - ghosts, planes - 2, extent_y, residual)
     _smooth_in_vmem(
         resid, kxo_full.at[1:-1], kyl, kyh, kzl, kzh, w, out, (buf_a, buf_b), SWEEPS
     )

time: 214 us -> 213 us (level)
  no operation moved by 1% of the time
where the time goes in v8:
time: 213 us; the launch traced here: 212 us
  other arithmetic  47 us (22%)
  local copies, waits for them, and re-layouts  43.1 us (20%)
  starting transfers between devices  35.2 us (17%)
  Pallas kernels  33.1 us (16%)
  matrix products  29.6 us (14%)
  waiting for transfers between devices  20.6 us (10%)
  between operations  3.01 us (1%)
    ppermute x10, starting transfers between devices, recv(): return lax.ppermute(value, 'gx', pairs)  35.2 us
    pallas_call x2, Pallas kernels, _vmem_call(): pl.pallas_call(kernel, out_shape=outs, in_specs=[pl.BlockSpec(memory_spac...  33.1 us
    ppermute x10, waiting for transfers between devices, recv(): return lax.ppermute(value, 'gx', pairs)  20.6 us
    unnamed x239, local copies, waits for them, and re-layouts  15.5 us
    dot_general x12, matrix products, shrink_sides(): jnp.einsum('xyz,zw->xyw', field, pair_matrix(extent_z), precision=EXACT)  9.56 us
    div x1, other arithmetic, make_coefs(): OMEGA / diag  7.61 us
    reduce_sum x7, other arithmetic, coarsen(): planes = field.reshape(extent_x // 2, 2, extent_y, extent_z).sum(axis=1)  7.52 us
    div x5, other arithmetic, make_coefs(): faces = [two_s / (safe + jnp.where(nb > 0, nb, safe)) for nb in near]  7.4 us
  transfers between devices with their start and end apart: 10, of which 6 were waited for; matrix products, arithmetic and copies ran while one was open for 15% of the time, Pallas kernels for 0%

profile of v8, /device:TPU:48, one launch (start us, length us, event | category | flops | bytes accessed | tf_op | source)
XLA Modules:
  0.0 211.6 jit_solution(3682698965269149856)
XLA Ops:
  0.6 1.6 fusion.598
  2.8 1.2 pad_maximum_fusion.11
  3.9 2.0 collective-permute-start
  6.0 1.2 pad_maximum_fusion.12
  7.1 3.6 %collective-permute-start.1 = (f32[5,256,256]{2,1,0:T(8,128)}, f32[5,256,256]{2,1,0:T(8,128)}, u32[]{:S(2)}, u32[]{:S(2)}) collective-permute-start(f32[5,256,256]{2,1,0:T(8,128)} %pad_maximum_fusion.12), channel_id=1, source_target_pairs={{1,0},{2,1},{3,2},{4,3},{5,4},{6,5},{7,6},{8,7},{9,8},{10,9},{11,1... | collective-permute-start | bytes 3932168 | tf_op jit(solution)/shard_map/ppermute | solution.py:25
  11.8 1.1 bitcast_reduce_fusion.3
  19.2 4.1 %collective-permute-done = f32[5,256,256]{2,1,0:T(8,128)} collective-permute-done((f32[5,256,256]{2,1,0:T(8,128)}, f32[5,256,256]{2,1,0:T(8,128)}, u32[]{:S(2)}, u32[]{:S(2)}) %collective-permute-start) | collective-permute-done | bytes 1310752 | tf_op jit(solution)/shard_map/ppermute | solution.py:25
  23.3 1.2 slice.1717
  24.5 1.7 collective-permute-done.1
  26.2 1.2 slice.1718
  28.8 7.6 %broadcast_divide_fusion = (f32[12,256,256]{2,1,0:T(8,128)}, f32[12,256,256]{2,1,0:T(8,128)}, f32[12,256,256]{2,1,0:T(8,128)}) fusion(f32[12,258,1]{2,1,0:T(8,128)S(1)} %get-tuple-element.38, f32[12,1,256]{2,1,0:T(1,128)S(1)} %get-tuple-element.36, f32[12,256,256]{2,1,0:T(8,128)S(1)} %slice.1721, f32[12,1,256]{2,1,0:T(1,128)S(1)} %get-tuple-element.37, ...), kind=kLoop, calls=%fused_computation.40 | loop fusion | flops 33030144 | bytes 22069440 | tf_op jit(solution)/shard_map/div | solution.py:120
  36.4 5.7 %fusion.13 = (f32[12,256,256]{2,1,0:T(8,128)}, f32[12,256,256]{2,1,0:T(8,128)}, f32[12,256,256]{2,1,0:T(8,128)}) fusion(f32[12,258,1]{2,1,0:T(8,128)S(1)} %get-tuple-element.38, f32[12,1,256]{2,1,0:T(1,128)S(1)} %get-tuple-element.36, f32[12,256,256]{2,1,0:T(8,128)S(1)} %slice.1721, f32[12,1,256]{2,1,0:T(1,128)S(1)} %get-tuple-element.37, ...), kind=kLoop, calls=%fused_computation.23 | loop fusion | flops 16515072 | bytes 12632256 | tf_op jit(solution)/shard_map/div | solution.py:109
  42.2 2.5 %divide_select_fusion.kxo_full = f32[13,256,256]{2,1,0:T(8,128)} fusion(f32[14,256,256]{2,1,0:T(8,128)S(1)} %pad_maximum_fusion), kind=kLoop, calls=%fused_computation.14 | loop fusion | flops 5111808 | bytes 10223616 | tf_op jit(solution)/shard_map/jit(_where)/select_n | solution.py:113
  44.6 1.1 slice.1715
  45.7 1.1 slice.1716
  46.8 1.9 pad_maximum_fusion.10.resid.rhs
  48.7 14.0 %shard_map.41 = (f32[8,256,256]{2,1,0:T(8,128)}, f32[3,256,256]{2,1,0:T(8,128)}, f32[3,256,256]{2,1,0:T(8,128)}) custom-call(f32[12,256,256]{2,1,0:T(8,128)} %pad_maximum_fusion.10.resid.rhs, f32[13,256,256]{2,1,0:T(8,128)} %divide_select_fusion.kxo_full, f32[12,256,256]{2,1,0:T(8,128)} %get-tuple-element.42.kyl, f32[12,256,256]{2,1,0:T(8,128)} %get-tuple-element.43.kyh, ...), custom_call_target="tpu_custom_call" | custom-call | tf_op jit(solution)/shard_map/pallas_call | solution.py:276
  62.8 4.1 %collective-permute-start.2 = (f32[3,256,256]{2,1,0:T(8,128)}, f32[3,256,256]{2,1,0:T(8,128)}, u32[]{:S(2)}, u32[]{:S(2)}) collective-permute-start(f32[3,256,256]{2,1,0:T(8,128)} %get-tuple-element.8), channel_id=1, source_target_pairs={{0,1},{1,2},{2,3},{3,4},{4,5},{5,6},{6,7},{7,8},{8,9},{9,10},{10,1... | collective-permute-start | bytes 2359304 | tf_op jit(solution)/shard_map/ppermute | solution.py:25
  66.9 2.1 collective-permute-start.3
  69.0 1.4 constant_dynamic-update-slice_fusion.38
  70.4 1.5 fusion.21
  72.9 1.4 fusion.23
  74.4 1.8 fusion.608
  76.6 2.0 collective-permute-done.3.fine_r
  78.6 19.1 %shard_map.42 = (f32[8,256,256]{2,1,0:T(8,128)}, f32[8,256,256]{2,1,0:T(8,128)}) custom-call(f32[3,256,256]{2,1,0:T(8,128)} %collective-permute-done.2.fine_l, f32[8,256,256]{2,1,0:T(8,128)} %get-tuple-element.7.fine, f32[3,256,256]{2,1,0:T(8,128)} %collective-permute-done.3.fine_r, f32[12,256,256]{2,1,0:T(8,128)} %pad_maximum_fusion.10.resid.rhs, ...), custom_call_target="tpu_custom_call" | custom-call | tf_op jit(solution)/shard_map/pallas_call | solution.py:276
  97.7 2.0 bitcast_reduce_fusion.1
  102.3 2.0 collective-permute-start.4
  106.4 5.5 %collective-permute-done.4 = f32[142336]{0:T(1024)S(1)} collective-permute-done((f32[142336]{0:T(1024)S(1)}, f32[142336]{0:T(1024)S(1)}, u32[]{:S(2)}, u32[]{:S(2)}) %collective-permute-start.4) | collective-permute-done | bytes 569376 | tf_op jit(solution)/shard_map/ppermute | solution.py:25
  123.0 4.6 %collective-permute-start.6 = (f32[13312]{0:T(1024)}, f32[13312]{0:T(1024)}, u32[]{:S(2)}, u32[]{:S(2)}) collective-permute-start(f32[13312]{0:T(1024)} %get-tuple-element.89), channel_id=1, source_target_pairs={{0,3},{1,4},{2,5},{3,6},{4,7},{5,8},{6,9},{7,10},{8,11},{9,12},{10... | collective-permute-start | bytes 159752 | tf_op jit(solution)/shard_map/ppermute | solution.py:25
  127.6 11.7 %collective-permute-start.7 = (f32[13312]{0:T(1024)}, f32[13312]{0:T(1024)}, u32[]{:S(2)}, u32[]{:S(2)}) collective-permute-start(f32[13312]{0:T(1024)} %get-tuple-element.88), channel_id=1, source_target_pairs={{0,125},{1,126},{2,127},{3,0},{4,1},{5,2},{6,3},{7,4},{8,5},{9,6},... | collective-permute-start | bytes 159752 | tf_op jit(solution)/shard_map/ppermute | solution.py:25
  150.0 4.8 %collective-permute-start.9 = (f32[27,32,32]{2,1,0:T(8,128)}, f32[27,32,32]{2,1,0:T(8,128)}, u32[]{:S(2)}, u32[]{:S(2)}) collective-permute-start(f32[27,32,32]{2,1,0:T(8,128)} %constant_dynamic-update-slice_fusion.7), channel_id=1, source_target_pairs={{0,119},{1,120},{2,121},{3,122},{4,123},{5,124},{6,125},{7,126},{8... | collective-permute-start | bytes 331784 | tf_op jit(solution)/shard_map/ppermute | solution.py:25
  157.0 1.3 fusion.590
  159.0 6.8 %collective-permute-done.8 = f32[27,32,32]{2,1,0:T(8,128)} collective-permute-done((f32[27,32,32]{2,1,0:T(8,128)}, f32[27,32,32]{2,1,0:T(8,128)}, u32[]{:S(2)}, u32[]{:S(2)}) %collective-permute-start.8) | collective-permute-done | bytes 110624 | tf_op jit(solution)/shard_map/ppermute | solution.py:25
  170.8 1.7 reduce_sum.117
  172.6 1.5 fusion.539
  178.7 1.7 reduce_sum.119
  180.5 1.7 fusion.534
  182.4 1.2 fusion.199
  183.7 1.9 slice_multiply_fusion.14
  189.8 1.3 fusion.284
  192.1 1.6 convolution_bitcast_fusion
  194.6 1.8 reduce_sum.118
  196.5 1.6 fusion.537
  198.9 1.1 fusion.241
  203.9 1.2 fusion.25
  205.6 1.3 fusion.267
  208.4 1.7 bitcast_add_fusion
  210.1 1.5 broadcast_in_dim.38
  (423 shorter events, 61.1 us)
Async XLA Ops:
  3.9 19.4 %collective-permute-start = (f32[5,256,256]{2,1,0:T(8,128)}, f32[5,256,256]{2,1,0:T(8,128)}, u32[]{:S(2)}, u32[]{:S(2)}) collective-permute-start(f32[5,256,256]{2,1,0:T(8,128)} %pad_maximum_fusion.11), channel_id=1, source_target_pairs={{0,1},{1,2},{2,3},{3,4},{4,5},{5,6},{6,7},{7,8},{8,9},{9,10},{10,1... | collective-permute-start | bytes 3932168 | tf_op jit(solution)/shard_map/ppermute | solution.py:25
  7.1 19.1 %collective-permute-start.1 = (f32[5,256,256]{2,1,0:T(8,128)}, f32[5,256,256]{2,1,0:T(8,128)}, u32[]{:S(2)}, u32[]{:S(2)}) collective-permute-start(f32[5,256,256]{2,1,0:T(8,128)} %pad_maximum_fusion.12), channel_id=1, source_target_pairs={{1,0},{2,1},{3,2},{4,3},{5,4},{6,5},{7,6},{8,7},{9,8},{10,9},{11,1... | collective-permute-start | bytes 3932168 | tf_op jit(solution)/shard_map/ppermute | solution.py:25
  13.4 14.0 %copy-start.46 = (f32[64,2,64]{2,0,1:T(8,128)}, f32[64,2,64]{2,0,1:T(8,128)S(1)}, u32[]{:S(2)}) copy-start(f32[64,2,64]{2,0,1:T(8,128)S(1)} %copy.81) | copy-start | bytes 98308
  14.5 13.2 %copy-start.26 = (f32[128,4,128]{2,0,1:T(8,128)}, f32[128,4,128]{2,0,1:T(8,128)S(1)}, u32[]{:S(2)}) copy-start(f32[128,4,128]{2,0,1:T(8,128)S(1)} %get-tuple-element.99) | copy-start | bytes 786436
  15.6 12.1 %copy-start.60 = (f32[2,64,64]{2,1,0:T(8,128)}, f32[2,64,64]{2,1,0:T(8,128)S(1)}, u32[]{:S(2)}) copy-start(f32[2,64,64]{2,1,0:T(8,128)S(1)} %get-tuple-element.107) | copy-start | bytes 98308
  62.8 13.8 %collective-permute-start.2 = (f32[3,256,256]{2,1,0:T(8,128)}, f32[3,256,256]{2,1,0:T(8,128)}, u32[]{:S(2)}, u32[]{:S(2)}) collective-permute-start(f32[3,256,256]{2,1,0:T(8,128)} %get-tuple-element.8), channel_id=1, source_target_pairs={{0,1},{1,2},{2,3},{3,4},{4,5},{5,6},{6,7},{7,8},{8,9},{9,10},{10,1... | collective-permute-start | bytes 2359304 | tf_op jit(solution)/shard_map/ppermute | solution.py:25
  66.9 11.7 %collective-permute-start.3 = (f32[3,256,256]{2,1,0:T(8,128)}, f32[3,256,256]{2,1,0:T(8,128)}, u32[]{:S(2)}, u32[]{:S(2)}) collective-permute-start(f32[3,256,256]{2,1,0:T(8,128)} %get-tuple-element.9), channel_id=1, source_target_pairs={{1,0},{2,1},{3,2},{4,3},{5,4},{6,5},{7,6},{8,7},{9,8},{10,9},{11,1... | collective-permute-start | bytes 2359304 | tf_op jit(solution)/shard_map/ppermute | solution.py:25
  99.7 13.0 %copy-start.15 = (f32[128,4,128]{2,0,1:T(8,128)S(1)}, f32[128,4,128]{2,0,1:T(8,128)}, u32[]{:S(2)}) copy-start(f32[128,4,128]{2,0,1:T(8,128)} %get-tuple-element.103) | copy-start | bytes 786436
  102.3 9.6 %collective-permute-start.4 = (f32[142336]{0:T(1024)S(1)}, f32[142336]{0:T(1024)S(1)}, u32[]{:S(2)}, u32[]{:S(2)}) collective-permute-start(f32[142336]{0:T(1024)S(1)} %get-tuple-element.96), channel_id=1, source_target_pairs={{0,1},{1,2},{2,3},{3,4},{4,5},{5,6},{6,7},{7,8},{8,9},{9,10},{10,1... | collective-permute-start | bytes 1708040 | tf_op jit(solution)/shard_map/ppermute | solution.py:25
  104.2 8.5 %collective-permute-start.5 = (f32[142336]{0:T(1024)S(1)}, f32[142336]{0:T(1024)S(1)}, u32[]{:S(2)}, u32[]{:S(2)}) collective-permute-start(f32[142336]{0:T(1024)S(1)} %get-tuple-element.97), channel_id=1, source_target_pairs={{0,127},{1,0},{2,1},{3,2},{4,3},{5,4},{6,5},{7,6},{8,7},{9,8},{10,... | collective-permute-start | bytes 1708040 | tf_op jit(solution)/shard_map/ppermute | solution.py:25
  105.2 40.8 %copy-start.75 = (f32[1,32,32]{2,1,0:T(8,128)}, f32[1,32,32]{2,1,0:T(8,128)S(1)}, u32[]{:S(2)}) copy-start(f32[1,32,32]{2,1,0:T(8,128)S(1)} %copy.83) | copy-start | bytes 12292
  106.4 40.2 %copy-start.77 = (f32[1,32,32]{2,1,0:T(8,128)}, f32[1,32,32]{2,1,0:T(8,128)S(1)}, u32[]{:S(2)}) copy-start(f32[1,32,32]{2,1,0:T(8,128)S(1)} %copy.84) | copy-start | bytes 12292
  113.8 25.7 %copy-start.4 = (f32[8,128,128]{2,1,0:T(8,128)}, f32[8,128,128]{2,1,0:T(8,128)S(1)}, u32[]{:S(2)}) copy-start(f32[8,128,128]{2,1,0:T(8,128)S(1)} %get-tuple-element.66) | copy-start | bytes 1572868
  116.1 23.3 %copy-start.7 = (f32[8,128,128]{2,1,0:T(8,128)}, f32[8,128,128]{2,1,0:T(8,128)S(1)}, u32[]{:S(2)}) copy-start(f32[8,128,128]{2,1,0:T(8,128)S(1)} %get-tuple-element.15) | copy-start | bytes 1572868
  116.2 23.0 %copy-start.27 = (f32[128,4,128]{2,0,1:T(8,128)S(1)}, f32[128,4,128]{2,0,1:T(8,128)}, u32[]{:S(2)}) copy-start(f32[128,4,128]{2,0,1:T(8,128)} %copy-done.26) | copy-start | bytes 786436
  122.3 17.2 %copy-start.11 = (f32[8,128,128]{2,1,0:T(8,128)S(1)}, f32[8,128,128]{2,1,0:T(8,128)}, u32[]{:S(2)}) copy-start(f32[8,128,128]{2,1,0:T(8,128)} %copy-done.10) | copy-start | bytes 1572868
  123.0 20.8 %collective-permute-start.6 = (f32[13312]{0:T(1024)}, f32[13312]{0:T(1024)}, u32[]{:S(2)}, u32[]{:S(2)}) collective-permute-start(f32[13312]{0:T(1024)} %get-tuple-element.89), channel_id=1, source_target_pairs={{0,3},{1,4},{2,5},{3,6},{4,7},{5,8},{6,9},{7,10},{8,11},{9,12},{10... | collective-permute-start | bytes 159752 | tf_op jit(solution)/shard_map/ppermute | solution.py:25
  127.6 20.9 %collective-permute-start.7 = (f32[13312]{0:T(1024)}, f32[13312]{0:T(1024)}, u32[]{:S(2)}, u32[]{:S(2)}) collective-permute-start(f32[13312]{0:T(1024)} %get-tuple-element.88), channel_id=1, source_target_pairs={{0,125},{1,126},{2,127},{3,0},{4,1},{5,2},{6,3},{7,4},{8,5},{9,6},... | collective-permute-start | bytes 159752 | tf_op jit(solution)/shard_map/ppermute | solution.py:25
  139.5 16.1 %copy-start.47 = (f32[64,2,64]{2,0,1:T(8,128)S(1)}, f32[64,2,64]{2,0,1:T(8,128)}, u32[]{:S(2)}) copy-start(f32[64,2,64]{2,0,1:T(8,128)} %copy-done.46) | copy-start | bytes 98308
  140.6 16.4 %copy-start.28 = (f32[6,128,128]{2,1,0:T(8,128)}, f32[6,128,128]{2,1,0:T(8,128)S(1)}, u32[]{:S(2)}) copy-start(f32[6,128,128]{2,1,0:T(8,128)S(1)} %fusion.53) | copy-start | bytes 1179652
  142.4 14.7 %copy-start.100 = (f32[6]{0:T(128)S(1)}, f32[6]{0:T(128)}, u32[]{:S(2)}) copy-start(f32[6]{0:T(128)} %and_convert_fusion.2) | copy-start | bytes 76
  144.6 12.4 %copy-start.39 = (f32[9,32,32]{2,1,0:T(8,128)}, f32[9,32,32]{2,1,0:T(8,128)S(1)}, u32[]{:S(2)}) copy-start(f32[9,32,32]{2,1,0:T(8,128)S(1)} %reshape.493) | copy-start | bytes 110596
  150.0 15.8 %collective-permute-start.8 = (f32[27,32,32]{2,1,0:T(8,128)}, f32[27,32,32]{2,1,0:T(8,128)}, u32[]{:S(2)}, u32[]{:S(2)}) collective-permute-start(f32[27,32,32]{2,1,0:T(8,128)} %constant_dynamic-update-slice_fusion.7), channel_id=1, source_target_pairs={{0,9},{1,10},{2,11},{3,12},{4,13},{5,14},{6,15},{7,16},{8,17},{9,1... | collective-permute-start | bytes 331784 | tf_op jit(solution)/shard_map/ppermute | solution.py:25
  150.0 17.0 %collective-permute-start.9 = (f32[27,32,32]{2,1,0:T(8,128)}, f32[27,32,32]{2,1,0:T(8,128)}, u32[]{:S(2)}, u32[]{:S(2)}) collective-permute-start(f32[27,32,32]{2,1,0:T(8,128)} %constant_dynamic-update-slice_fusion.7), channel_id=1, source_target_pairs={{0,119},{1,120},{2,121},{3,122},{4,123},{5,124},{6,125},{7,126},{8... | collective-permute-start | bytes 331784 | tf_op jit(solution)/shard_map/ppermute | solution.py:25
  158.6 9.5 %copy-start.49 = (f32[6,64,64]{2,1,0:T(8,128)}, f32[6,64,64]{2,1,0:T(8,128)S(1)}, u32[]{:S(2)}) copy-start(f32[6,64,64]{2,1,0:T(8,128)S(1)} %get-tuple-element.33) | copy-start | bytes 294916
  158.6 9.5 %copy-start.101 = (f32[27]{0:T(128)S(1)}, f32[27]{0:T(128)}, u32[]{:S(2)}) copy-start(f32[27]{0:T(128)} %and_convert_fusion.4) | copy-start | bytes 328
  158.8 9.5 %copy-start.72 = (f32[4,64,64]{2,1,0:T(8,128)}, f32[4,64,64]{2,1,0:T(8,128)S(1)}, u32[]{:S(2)}) copy-start(f32[4,64,64]{2,1,0:T(8,128)S(1)} %fusion.168) | copy-start | bytes 196612
  177.8 12.0 %slice-start.8 = ((f32[4,64,64]{2,1,0:T(8,128)}), f32[2,64,64]{2,1,0:T(8,128)S(1)}, s32[]{:S(2)}) async-start(f32[4,64,64]{2,1,0:T(8,128)} %copy-done.72), calls=%async_computation.8 | async-start | bytes 131072 | tf_op jit(solution)/shard_map/slice | solution.py:141
  180.5 9.4 %copy-start.73 = (f32[4,64,64]{2,1,0:T(8,128)S(1)}, f32[4,64,64]{2,1,0:T(8,128)}, u32[]{:S(2)}) copy-start(f32[4,64,64]{2,1,0:T(8,128)} %copy-done.72) | copy-start | bytes 196612
  180.5 10.6 %copy-start.94 = (s32[128]{0:T(128)S(1)}, s32[128]{0:T(128)}, u32[]{:S(2)}) copy-start(s32[128]{0:T(128)} %copy-done.92) | copy-start | bytes 1540
  180.5 11.0 %copy-start.5 = (f32[8,128,128]{2,1,0:T(8,128)S(1)}, f32[8,128,128]{2,1,0:T(8,128)}, u32[]{:S(2)}) copy-start(f32[8,128,128]{2,1,0:T(8,128)} %copy-done.4) | copy-start | bytes 1572868
  180.5 11.0 %copy-start.8 = (f32[8,128,128]{2,1,0:T(8,128)S(1)}, f32[8,128,128]{2,1,0:T(8,128)}, u32[]{:S(2)}) copy-start(f32[8,128,128]{2,1,0:T(8,128)} %copy-done.7) | copy-start | bytes 1572868
  180.5 11.0 %copy-start.12 = (f32[8,128,128]{2,1,0:T(8,128)S(1)}, f32[8,128,128]{2,1,0:T(8,128)}, u32[]{:S(2)}) copy-start(f32[8,128,128]{2,1,0:T(8,128)} %copy-done.10) | copy-start | bytes 1572868
  180.5 11.0 %copy-start.25 = (f32[8,128,128]{2,1,0:T(8,128)S(1)}, f32[8,128,128]{2,1,0:T(8,128)}, u32[]{:S(2)}) copy-start(f32[8,128,128]{2,1,0:T(8,128)} %copy-done.24) | copy-start | bytes 1572868
  180.5 11.0 %copy-start.31 = (f32[6,128,128]{2,1,0:T(8,128)S(1)}, f32[6,128,128]{2,1,0:T(8,128)}, u32[]{:S(2)}) copy-start(f32[6,128,128]{2,1,0:T(8,128)} %copy-done.30) | copy-start | bytes 1179652
  180.5 11.0 %slice-start.1 = ((f32[6,128,128]{2,1,0:T(8,128)}), f32[4,128,128]{2,1,0:T(8,128)S(1)}, s32[]{:S(2)}) async-start(f32[6,128,128]{2,1,0:T(8,128)} %copy-done.30), calls=%async_computation.1 | async-start | bytes 524288 | tf_op jit(solution)/shard_map/slice | solution.py:141
  180.5 11.0 %copy-start.88 = (s32[256]{0:T(256)S(1)}, s32[256]{0:T(256)}, u32[]{:S(2)}) copy-start(s32[256]{0:T(256)} %copy-done.86) | copy-start | bytes 3076
  193.7 11.9 %slice-start.7 = ((f32[4,64,64]{2,1,0:T(8,128)}), f32[2,64,64]{2,1,0:T(8,128)S(1)}, s32[]{:S(2)}) async-start(f32[4,64,64]{2,1,0:T(8,128)} %copy-done.70), calls=%async_computation.7 | async-start | bytes 131072 | tf_op jit(solution)/shard_map/slice | solution.py:141
  194.6 9.3 %slice-start.9 = ((f32[3,32,32]{2,1,0:T(8,128)}), f32[1,32,32]{2,1,0:T(8,128)S(1)}, s32[]{:S(2)}) async-start(f32[3,32,32]{2,1,0:T(8,128)} %copy-done.81), calls=%async_computation.9 | async-start | bytes 32768 | tf_op jit(solution)/shard_map/slice | solution.py:141
  196.4 9.2 %copy-start.71 = (f32[4,64,64]{2,1,0:T(8,128)S(1)}, f32[4,64,64]{2,1,0:T(8,128)}, u32[]{:S(2)}) copy-start(f32[4,64,64]{2,1,0:T(8,128)} %copy-done.70) | copy-start | bytes 196612
  196.4 9.2 %copy-start.95 = (s32[128]{0:T(128)S(1)}, s32[128]{0:T(128)}, u32[]{:S(2)}) copy-start(s32[128]{0:T(128)} %copy-done.92) | copy-start | bytes 1540
  196.4 10.8 %copy-start.6 = (f32[8,128,128]{2,1,0:T(8,128)S(1)}, f32[8,128,128]{2,1,0:T(8,128)}, u32[]{:S(2)}) copy-start(f32[8,128,128]{2,1,0:T(8,128)} %copy-done.4) | copy-start | bytes 1572868
  196.4 10.8 %copy-start.9 = (f32[8,128,128]{2,1,0:T(8,128)S(1)}, f32[8,128,128]{2,1,0:T(8,128)}, u32[]{:S(2)}) copy-start(f32[8,128,128]{2,1,0:T(8,128)} %copy-done.7) | copy-start | bytes 1572868
  196.4 10.8 %copy-start.13 = (f32[8,128,128]{2,1,0:T(8,128)S(1)}, f32[8,128,128]{2,1,0:T(8,128)}, u32[]{:S(2)}) copy-start(f32[8,128,128]{2,1,0:T(8,128)} %copy-done.10) | copy-start | bytes 1572868
  196.4 10.8 %copy-start.23 = (f32[8,128,128]{2,1,0:T(8,128)S(1)}, f32[8,128,128]{2,1,0:T(8,128)}, u32[]{:S(2)}) copy-start(f32[8,128,128]{2,1,0:T(8,128)} %copy-done.22) | copy-start | bytes 1572868
  196.4 10.8 %copy-start.29 = (f32[6,128,128]{2,1,0:T(8,128)S(1)}, f32[6,128,128]{2,1,0:T(8,128)}, u32[]{:S(2)}) copy-start(f32[6,128,128]{2,1,0:T(8,128)} %copy-done.28) | copy-start | bytes 1179652
  196.4 10.8 %slice-start = ((f32[6,128,128]{2,1,0:T(8,128)}), f32[4,128,128]{2,1,0:T(8,128)S(1)}, s32[]{:S(2)}) async-start(f32[6,128,128]{2,1,0:T(8,128)} %copy-done.28), calls=%async_computation | async-start | bytes 524288 | tf_op jit(solution)/shard_map/slice | solution.py:141
  196.5 10.8 %copy-start.89 = (s32[256]{0:T(256)S(1)}, s32[256]{0:T(256)}, u32[]{:S(2)}) copy-start(s32[256]{0:T(256)} %copy-done.86) | copy-start | bytes 3076
  (78 other events, 334.0 us)

commit v9 on v7

--- a/solution.py
+++ b/solution.py
@@ -148,7 +148,7 @@
     return update
 
 
-ROWS = 128
+ROWS = 32
 PAD = 8
 VMEM_LIMIT = 64 * 1024 * 1024
 

time: 215 us -> 213 us (level)
  no operation moved by 1% of the time
where the time goes in v9:
time: 213 us; the launch traced here: 211 us
  other arithmetic  47 us (22%)
  local copies, waits for them, and re-layouts  43.1 us (20%)
  starting transfers between devices  35.2 us (17%)
  Pallas kernels  32.9 us (15%)
  matrix products  29.5 us (14%)
  waiting for transfers between devices  20.6 us (10%)
  between operations  3.01 us (1%)
    ppermute x10, starting transfers between devices, recv(): return lax.ppermute(value, 'gx', pairs)  35.2 us
    pallas_call x2, Pallas kernels, _vmem_call(): pl.pallas_call(kernel, out_shape=outs, in_specs=[pl.BlockSpec(memory_spac...  32.9 us
    ppermute x10, waiting for transfers between devices, recv(): return lax.ppermute(value, 'gx', pairs)  20.6 us
    unnamed x239, local copies, waits for them, and re-layouts  15.5 us
    dot_general x12, matrix products, shrink_sides(): jnp.einsum('xyz,zw->xyw', field, pair_matrix(extent_z), precision=EXACT)  9.56 us
    div x1, other arithmetic, make_coefs(): OMEGA / diag  7.61 us
    reduce_sum x7, other arithmetic, coarsen(): planes = field.reshape(extent_x // 2, 2, extent_y, extent_z).sum(axis=1)  7.52 us
    div x5, other arithmetic, make_coefs(): faces = [two_s / (safe + jnp.where(nb > 0, nb, safe)) for nb in near]  7.4 us
  transfers between devices with their start and end apart: 10, of which 6 were waited for; matrix products, arithmetic and copies ran while one was open for 15% of the time, Pallas kernels for 0%

profile of v9, /device:TPU:48, one launch (start us, length us, event | category | flops | bytes accessed | tf_op | source)
XLA Modules:
  0.0 211.4 jit_solution(2227952043285005088)
XLA Ops:
  0.6 1.6 fusion.598
  2.8 1.2 pad_maximum_fusion.11
  3.9 2.0 collective-permute-start
  6.0 1.2 pad_maximum_fusion.12
  7.1 3.6 %collective-permute-start.1 = (f32[5,256,256]{2,1,0:T(8,128)}, f32[5,256,256]{2,1,0:T(8,128)}, u32[]{:S(2)}, u32[]{:S(2)}) collective-permute-start(f32[5,256,256]{2,1,0:T(8,128)} %pad_maximum_fusion.12), channel_id=1, source_target_pairs={{1,0},{2,1},{3,2},{4,3},{5,4},{6,5},{7,6},{8,7},{9,8},{10,9},{11,1... | collective-permute-start | bytes 3932168 | tf_op jit(solution)/shard_map/ppermute | solution.py:25
  11.8 1.1 bitcast_reduce_fusion.3
  19.2 4.1 %collective-permute-done = f32[5,256,256]{2,1,0:T(8,128)} collective-permute-done((f32[5,256,256]{2,1,0:T(8,128)}, f32[5,256,256]{2,1,0:T(8,128)}, u32[]{:S(2)}, u32[]{:S(2)}) %collective-permute-start) | collective-permute-done | bytes 1310752 | tf_op jit(solution)/shard_map/ppermute | solution.py:25
  23.3 1.2 slice.1717
  24.5 1.7 collective-permute-done.1
  26.2 1.2 slice.1718
  28.8 7.6 %broadcast_divide_fusion = (f32[12,256,256]{2,1,0:T(8,128)}, f32[12,256,256]{2,1,0:T(8,128)}, f32[12,256,256]{2,1,0:T(8,128)}) fusion(f32[12,258,1]{2,1,0:T(8,128)S(1)} %get-tuple-element.38, f32[12,1,256]{2,1,0:T(1,128)S(1)} %get-tuple-element.36, f32[12,256,256]{2,1,0:T(8,128)S(1)} %slice.1721, f32[12,1,256]{2,1,0:T(1,128)S(1)} %get-tuple-element.37, ...), kind=kLoop, calls=%fused_computation.40 | loop fusion | flops 33030144 | bytes 22069440 | tf_op jit(solution)/shard_map/div | solution.py:120
  36.4 5.7 %fusion.13 = (f32[12,256,256]{2,1,0:T(8,128)}, f32[12,256,256]{2,1,0:T(8,128)}, f32[12,256,256]{2,1,0:T(8,128)}) fusion(f32[12,258,1]{2,1,0:T(8,128)S(1)} %get-tuple-element.38, f32[12,1,256]{2,1,0:T(1,128)S(1)} %get-tuple-element.36, f32[12,256,256]{2,1,0:T(8,128)S(1)} %slice.1721, f32[12,1,256]{2,1,0:T(1,128)S(1)} %get-tuple-element.37, ...), kind=kLoop, calls=%fused_computation.23 | loop fusion | flops 16515072 | bytes 12632256 | tf_op jit(solution)/shard_map/div | solution.py:109
  42.2 2.5 %divide_select_fusion.kxo_full = f32[13,256,256]{2,1,0:T(8,128)} fusion(f32[14,256,256]{2,1,0:T(8,128)S(1)} %pad_maximum_fusion), kind=kLoop, calls=%fused_computation.14 | loop fusion | flops 5111808 | bytes 10223616 | tf_op jit(solution)/shard_map/jit(_where)/select_n | solution.py:113
  44.6 1.1 slice.1715
  45.7 1.1 slice.1716
  46.8 1.9 pad_maximum_fusion.10.resid.rhs
  48.7 13.9 %shard_map.41 = (f32[8,256,256]{2,1,0:T(8,128)}, f32[3,256,256]{2,1,0:T(8,128)}, f32[3,256,256]{2,1,0:T(8,128)}) custom-call(f32[12,256,256]{2,1,0:T(8,128)} %pad_maximum_fusion.10.resid.rhs, f32[13,256,256]{2,1,0:T(8,128)} %divide_select_fusion.kxo_full, f32[12,256,256]{2,1,0:T(8,128)} %get-tuple-element.42.kyl, f32[12,256,256]{2,1,0:T(8,128)} %get-tuple-element.43.kyh, ...), custom_call_target="tpu_custom_call" | custom-call | tf_op jit(solution)/shard_map/pallas_call | solution.py:276
  62.7 4.1 %collective-permute-start.2 = (f32[3,256,256]{2,1,0:T(8,128)}, f32[3,256,256]{2,1,0:T(8,128)}, u32[]{:S(2)}, u32[]{:S(2)}) collective-permute-start(f32[3,256,256]{2,1,0:T(8,128)} %get-tuple-element.8), channel_id=1, source_target_pairs={{0,1},{1,2},{2,3},{3,4},{4,5},{5,6},{6,7},{7,8},{8,9},{9,10},{10,1... | collective-permute-start | bytes 2359304 | tf_op jit(solution)/shard_map/ppermute | solution.py:25
  66.8 2.1 collective-permute-start.3
  68.9 1.4 constant_dynamic-update-slice_fusion.38
  70.3 1.5 fusion.21
  72.8 1.4 fusion.23
  74.3 1.8 fusion.608
  76.5 2.0 collective-permute-done.3.fine_r
  78.5 18.9 %shard_map.42 = (f32[8,256,256]{2,1,0:T(8,128)}, f32[8,256,256]{2,1,0:T(8,128)}) custom-call(f32[3,256,256]{2,1,0:T(8,128)} %collective-permute-done.2.fine_l, f32[8,256,256]{2,1,0:T(8,128)} %get-tuple-element.7.fine, f32[3,256,256]{2,1,0:T(8,128)} %collective-permute-done.3.fine_r, f32[12,256,256]{2,1,0:T(8,128)} %pad_maximum_fusion.10.resid.rhs, ...), custom_call_target="tpu_custom_call" | custom-call | tf_op jit(solution)/shard_map/pallas_call | solution.py:276
  97.5 2.0 bitcast_reduce_fusion.1
  102.0 2.0 collective-permute-start.4
  106.2 5.5 %collective-permute-done.4 = f32[142336]{0:T(1024)S(1)} collective-permute-done((f32[142336]{0:T(1024)S(1)}, f32[142336]{0:T(1024)S(1)}, u32[]{:S(2)}, u32[]{:S(2)}) %collective-permute-start.4) | collective-permute-done | bytes 569376 | tf_op jit(solution)/shard_map/ppermute | solution.py:25
  122.8 4.6 %collective-permute-start.6 = (f32[13312]{0:T(1024)}, f32[13312]{0:T(1024)}, u32[]{:S(2)}, u32[]{:S(2)}) collective-permute-start(f32[13312]{0:T(1024)} %get-tuple-element.89), channel_id=1, source_target_pairs={{0,3},{1,4},{2,5},{3,6},{4,7},{5,8},{6,9},{7,10},{8,11},{9,12},{10... | collective-permute-start | bytes 159752 | tf_op jit(solution)/shard_map/ppermute | solution.py:25
  127.3 11.7 %collective-permute-start.7 = (f32[13312]{0:T(1024)}, f32[13312]{0:T(1024)}, u32[]{:S(2)}, u32[]{:S(2)}) collective-permute-start(f32[13312]{0:T(1024)} %get-tuple-element.88), channel_id=1, source_target_pairs={{0,125},{1,126},{2,127},{3,0},{4,1},{5,2},{6,3},{7,4},{8,5},{9,6},... | collective-permute-start | bytes 159752 | tf_op jit(solution)/shard_map/ppermute | solution.py:25
  149.8 4.8 %collective-permute-start.9 = (f32[27,32,32]{2,1,0:T(8,128)}, f32[27,32,32]{2,1,0:T(8,128)}, u32[]{:S(2)}, u32[]{:S(2)}) collective-permute-start(f32[27,32,32]{2,1,0:T(8,128)} %constant_dynamic-update-slice_fusion.7), channel_id=1, source_target_pairs={{0,119},{1,120},{2,121},{3,122},{4,123},{5,124},{6,125},{7,126},{8... | collective-permute-start | bytes 331784 | tf_op jit(solution)/shard_map/ppermute | solution.py:25
  156.8 1.3 fusion.590
  158.8 6.8 %collective-permute-done.8 = f32[27,32,32]{2,1,0:T(8,128)} collective-permute-done((f32[27,32,32]{2,1,0:T(8,128)}, f32[27,32,32]{2,1,0:T(8,128)}, u32[]{:S(2)}, u32[]{:S(2)}) %collective-permute-start.8) | collective-permute-done | bytes 110624 | tf_op jit(solution)/shard_map/ppermute | solution.py:25
  170.6 1.7 reduce_sum.117
  172.3 1.5 fusion.539
  178.5 1.7 reduce_sum.119
  180.3 1.7 fusion.534
  182.2 1.2 fusion.199
  183.4 1.9 slice_multiply_fusion.14
  189.6 1.3 fusion.284
  191.8 1.6 convolution_bitcast_fusion
  194.4 1.8 reduce_sum.118
  196.2 1.6 fusion.537
  198.7 1.1 fusion.241
  203.7 1.2 fusion.25
  205.4 1.3 fusion.267
  208.2 1.7 bitcast_add_fusion
  209.9 1.5 broadcast_in_dim.38
  (423 shorter events, 61.1 us)
Async XLA Ops:
  3.9 19.4 %collective-permute-start = (f32[5,256,256]{2,1,0:T(8,128)}, f32[5,256,256]{2,1,0:T(8,128)}, u32[]{:S(2)}, u32[]{:S(2)}) collective-permute-start(f32[5,256,256]{2,1,0:T(8,128)} %pad_maximum_fusion.11), channel_id=1, source_target_pairs={{0,1},{1,2},{2,3},{3,4},{4,5},{5,6},{6,7},{7,8},{8,9},{9,10},{10,1... | collective-permute-start | bytes 3932168 | tf_op jit(solution)/shard_map/ppermute | solution.py:25
  7.1 19.1 %collective-permute-start.1 = (f32[5,256,256]{2,1,0:T(8,128)}, f32[5,256,256]{2,1,0:T(8,128)}, u32[]{:S(2)}, u32[]{:S(2)}) collective-permute-start(f32[5,256,256]{2,1,0:T(8,128)} %pad_maximum_fusion.12), channel_id=1, source_target_pairs={{1,0},{2,1},{3,2},{4,3},{5,4},{6,5},{7,6},{8,7},{9,8},{10,9},{11,1... | collective-permute-start | bytes 3932168 | tf_op jit(solution)/shard_map/ppermute | solution.py:25
  13.4 14.0 %copy-start.46 = (f32[64,2,64]{2,0,1:T(8,128)}, f32[64,2,64]{2,0,1:T(8,128)S(1)}, u32[]{:S(2)}) copy-start(f32[64,2,64]{2,0,1:T(8,128)S(1)} %copy.81) | copy-start | bytes 98308
  14.5 13.2 %copy-start.26 = (f32[128,4,128]{2,0,1:T(8,128)}, f32[128,4,128]{2,0,1:T(8,128)S(1)}, u32[]{:S(2)}) copy-start(f32[128,4,128]{2,0,1:T(8,128)S(1)} %get-tuple-element.99) | copy-start | bytes 786436
  15.6 12.1 %copy-start.60 = (f32[2,64,64]{2,1,0:T(8,128)}, f32[2,64,64]{2,1,0:T(8,128)S(1)}, u32[]{:S(2)}) copy-start(f32[2,64,64]{2,1,0:T(8,128)S(1)} %get-tuple-element.107) | copy-start | bytes 98308
  62.7 13.8 %collective-permute-start.2 = (f32[3,256,256]{2,1,0:T(8,128)}, f32[3,256,256]{2,1,0:T(8,128)}, u32[]{:S(2)}, u32[]{:S(2)}) collective-permute-start(f32[3,256,256]{2,1,0:T(8,128)} %get-tuple-element.8), channel_id=1, source_target_pairs={{0,1},{1,2},{2,3},{3,4},{4,5},{5,6},{6,7},{7,8},{8,9},{9,10},{10,1... | collective-permute-start | bytes 2359304 | tf_op jit(solution)/shard_map/ppermute | solution.py:25
  66.8 11.7 %collective-permute-start.3 = (f32[3,256,256]{2,1,0:T(8,128)}, f32[3,256,256]{2,1,0:T(8,128)}, u32[]{:S(2)}, u32[]{:S(2)}) collective-permute-start(f32[3,256,256]{2,1,0:T(8,128)} %get-tuple-element.9), channel_id=1, source_target_pairs={{1,0},{2,1},{3,2},{4,3},{5,4},{6,5},{7,6},{8,7},{9,8},{10,9},{11,1... | collective-permute-start | bytes 2359304 | tf_op jit(solution)/shard_map/ppermute | solution.py:25
  99.5 13.0 %copy-start.15 = (f32[128,4,128]{2,0,1:T(8,128)S(1)}, f32[128,4,128]{2,0,1:T(8,128)}, u32[]{:S(2)}) copy-start(f32[128,4,128]{2,0,1:T(8,128)} %get-tuple-element.103) | copy-start | bytes 786436
  102.0 9.6 %collective-permute-start.4 = (f32[142336]{0:T(1024)S(1)}, f32[142336]{0:T(1024)S(1)}, u32[]{:S(2)}, u32[]{:S(2)}) collective-permute-start(f32[142336]{0:T(1024)S(1)} %get-tuple-element.96), channel_id=1, source_target_pairs={{0,1},{1,2},{2,3},{3,4},{4,5},{5,6},{6,7},{7,8},{8,9},{9,10},{10,1... | collective-permute-start | bytes 1708040 | tf_op jit(solution)/shard_map/ppermute | solution.py:25
  104.0 8.5 %collective-permute-start.5 = (f32[142336]{0:T(1024)S(1)}, f32[142336]{0:T(1024)S(1)}, u32[]{:S(2)}, u32[]{:S(2)}) collective-permute-start(f32[142336]{0:T(1024)S(1)} %get-tuple-element.97), channel_id=1, source_target_pairs={{0,127},{1,0},{2,1},{3,2},{4,3},{5,4},{6,5},{7,6},{8,7},{9,8},{10,... | collective-permute-start | bytes 1708040 | tf_op jit(solution)/shard_map/ppermute | solution.py:25
  105.0 40.8 %copy-start.75 = (f32[1,32,32]{2,1,0:T(8,128)}, f32[1,32,32]{2,1,0:T(8,128)S(1)}, u32[]{:S(2)}) copy-start(f32[1,32,32]{2,1,0:T(8,128)S(1)} %copy.83) | copy-start | bytes 12292
  106.2 40.2 %copy-start.77 = (f32[1,32,32]{2,1,0:T(8,128)}, f32[1,32,32]{2,1,0:T(8,128)S(1)}, u32[]{:S(2)}) copy-start(f32[1,32,32]{2,1,0:T(8,128)S(1)} %copy.84) | copy-start | bytes 12292
  113.6 25.7 %copy-start.4 = (f32[8,128,128]{2,1,0:T(8,128)}, f32[8,128,128]{2,1,0:T(8,128)S(1)}, u32[]{:S(2)}) copy-start(f32[8,128,128]{2,1,0:T(8,128)S(1)} %get-tuple-element.66) | copy-start | bytes 1572868
  115.9 23.3 %copy-start.7 = (f32[8,128,128]{2,1,0:T(8,128)}, f32[8,128,128]{2,1,0:T(8,128)S(1)}, u32[]{:S(2)}) copy-start(f32[8,128,128]{2,1,0:T(8,128)S(1)} %get-tuple-element.15) | copy-start | bytes 1572868
  116.0 23.0 %copy-start.27 = (f32[128,4,128]{2,0,1:T(8,128)S(1)}, f32[128,4,128]{2,0,1:T(8,128)}, u32[]{:S(2)}) copy-start(f32[128,4,128]{2,0,1:T(8,128)} %copy-done.26) | copy-start | bytes 786436
  122.1 17.2 %copy-start.11 = (f32[8,128,128]{2,1,0:T(8,128)S(1)}, f32[8,128,128]{2,1,0:T(8,128)}, u32[]{:S(2)}) copy-start(f32[8,128,128]{2,1,0:T(8,128)} %copy-done.10) | copy-start | bytes 1572868
  122.8 20.8 %collective-permute-start.6 = (f32[13312]{0:T(1024)}, f32[13312]{0:T(1024)}, u32[]{:S(2)}, u32[]{:S(2)}) collective-permute-start(f32[13312]{0:T(1024)} %get-tuple-element.89), channel_id=1, source_target_pairs={{0,3},{1,4},{2,5},{3,6},{4,7},{5,8},{6,9},{7,10},{8,11},{9,12},{10... | collective-permute-start | bytes 159752 | tf_op jit(solution)/shard_map/ppermute | solution.py:25
  127.3 20.9 %collective-permute-start.7 = (f32[13312]{0:T(1024)}, f32[13312]{0:T(1024)}, u32[]{:S(2)}, u32[]{:S(2)}) collective-permute-start(f32[13312]{0:T(1024)} %get-tuple-element.88), channel_id=1, source_target_pairs={{0,125},{1,126},{2,127},{3,0},{4,1},{5,2},{6,3},{7,4},{8,5},{9,6},... | collective-permute-start | bytes 159752 | tf_op jit(solution)/shard_map/ppermute | solution.py:25
  139.2 16.1 %copy-start.47 = (f32[64,2,64]{2,0,1:T(8,128)S(1)}, f32[64,2,64]{2,0,1:T(8,128)}, u32[]{:S(2)}) copy-start(f32[64,2,64]{2,0,1:T(8,128)} %copy-done.46) | copy-start | bytes 98308
  140.4 16.4 %copy-start.28 = (f32[6,128,128]{2,1,0:T(8,128)}, f32[6,128,128]{2,1,0:T(8,128)S(1)}, u32[]{:S(2)}) copy-start(f32[6,128,128]{2,1,0:T(8,128)S(1)} %fusion.53) | copy-start | bytes 1179652
  142.1 14.7 %copy-start.100 = (f32[6]{0:T(128)S(1)}, f32[6]{0:T(128)}, u32[]{:S(2)}) copy-start(f32[6]{0:T(128)} %and_convert_fusion.2) | copy-start | bytes 76
  144.4 12.4 %copy-start.39 = (f32[9,32,32]{2,1,0:T(8,128)}, f32[9,32,32]{2,1,0:T(8,128)S(1)}, u32[]{:S(2)}) copy-start(f32[9,32,32]{2,1,0:T(8,128)S(1)} %reshape.493) | copy-start | bytes 110596
  149.8 15.8 %collective-permute-start.8 = (f32[27,32,32]{2,1,0:T(8,128)}, f32[27,32,32]{2,1,0:T(8,128)}, u32[]{:S(2)}, u32[]{:S(2)}) collective-permute-start(f32[27,32,32]{2,1,0:T(8,128)} %constant_dynamic-update-slice_fusion.7), channel_id=1, source_target_pairs={{0,9},{1,10},{2,11},{3,12},{4,13},{5,14},{6,15},{7,16},{8,17},{9,1... | collective-permute-start | bytes 331784 | tf_op jit(solution)/shard_map/ppermute | solution.py:25
  149.8 17.0 %collective-permute-start.9 = (f32[27,32,32]{2,1,0:T(8,128)}, f32[27,32,32]{2,1,0:T(8,128)}, u32[]{:S(2)}, u32[]{:S(2)}) collective-permute-start(f32[27,32,32]{2,1,0:T(8,128)} %constant_dynamic-update-slice_fusion.7), channel_id=1, source_target_pairs={{0,119},{1,120},{2,121},{3,122},{4,123},{5,124},{6,125},{7,126},{8... | collective-permute-start | bytes 331784 | tf_op jit(solution)/shard_map/ppermute | solution.py:25
  158.4 9.5 %copy-start.49 = (f32[6,64,64]{2,1,0:T(8,128)}, f32[6,64,64]{2,1,0:T(8,128)S(1)}, u32[]{:S(2)}) copy-start(f32[6,64,64]{2,1,0:T(8,128)S(1)} %get-tuple-element.33) | copy-start | bytes 294916
  158.4 9.5 %copy-start.101 = (f32[27]{0:T(128)S(1)}, f32[27]{0:T(128)}, u32[]{:S(2)}) copy-start(f32[27]{0:T(128)} %and_convert_fusion.4) | copy-start | bytes 328
  158.6 9.5 %copy-start.72 = (f32[4,64,64]{2,1,0:T(8,128)}, f32[4,64,64]{2,1,0:T(8,128)S(1)}, u32[]{:S(2)}) copy-start(f32[4,64,64]{2,1,0:T(8,128)S(1)} %fusion.168) | copy-start | bytes 196612
  177.6 12.0 %slice-start.8 = ((f32[4,64,64]{2,1,0:T(8,128)}), f32[2,64,64]{2,1,0:T(8,128)S(1)}, s32[]{:S(2)}) async-start(f32[4,64,64]{2,1,0:T(8,128)} %copy-done.72), calls=%async_computation.8 | async-start | bytes 131072 | tf_op jit(solution)/shard_map/slice | solution.py:141
  180.2 9.4 %copy-start.73 = (f32[4,64,64]{2,1,0:T(8,128)S(1)}, f32[4,64,64]{2,1,0:T(8,128)}, u32[]{:S(2)}) copy-start(f32[4,64,64]{2,1,0:T(8,128)} %copy-done.72) | copy-start | bytes 196612
  180.2 10.6 %copy-start.94 = (s32[128]{0:T(128)S(1)}, s32[128]{0:T(128)}, u32[]{:S(2)}) copy-start(s32[128]{0:T(128)} %copy-done.92) | copy-start | bytes 1540
  180.2 11.0 %copy-start.5 = (f32[8,128,128]{2,1,0:T(8,128)S(1)}, f32[8,128,128]{2,1,0:T(8,128)}, u32[]{:S(2)}) copy-start(f32[8,128,128]{2,1,0:T(8,128)} %copy-done.4) | copy-start | bytes 1572868
  180.3 11.0 %copy-start.8 = (f32[8,128,128]{2,1,0:T(8,128)S(1)}, f32[8,128,128]{2,1,0:T(8,128)}, u32[]{:S(2)}) copy-start(f32[8,128,128]{2,1,0:T(8,128)} %copy-done.7) | copy-start | bytes 1572868
  180.3 11.0 %copy-start.12 = (f32[8,128,128]{2,1,0:T(8,128)S(1)}, f32[8,128,128]{2,1,0:T(8,128)}, u32[]{:S(2)}) copy-start(f32[8,128,128]{2,1,0:T(8,128)} %copy-done.10) | copy-start | bytes 1572868
  180.3 11.0 %copy-start.25 = (f32[8,128,128]{2,1,0:T(8,128)S(1)}, f32[8,128,128]{2,1,0:T(8,128)}, u32[]{:S(2)}) copy-start(f32[8,128,128]{2,1,0:T(8,128)} %copy-done.24) | copy-start | bytes 1572868
  180.3 11.0 %copy-start.31 = (f32[6,128,128]{2,1,0:T(8,128)S(1)}, f32[6,128,128]{2,1,0:T(8,128)}, u32[]{:S(2)}) copy-start(f32[6,128,128]{2,1,0:T(8,128)} %copy-done.30) | copy-start | bytes 1179652
  180.3 11.0 %slice-start.1 = ((f32[6,128,128]{2,1,0:T(8,128)}), f32[4,128,128]{2,1,0:T(8,128)S(1)}, s32[]{:S(2)}) async-start(f32[6,128,128]{2,1,0:T(8,128)} %copy-done.30), calls=%async_computation.1 | async-start | bytes 524288 | tf_op jit(solution)/shard_map/slice | solution.py:141
  180.3 11.0 %copy-start.88 = (s32[256]{0:T(256)S(1)}, s32[256]{0:T(256)}, u32[]{:S(2)}) copy-start(s32[256]{0:T(256)} %copy-done.86) | copy-start | bytes 3076
  193.4 11.9 %slice-start.7 = ((f32[4,64,64]{2,1,0:T(8,128)}), f32[2,64,64]{2,1,0:T(8,128)S(1)}, s32[]{:S(2)}) async-start(f32[4,64,64]{2,1,0:T(8,128)} %copy-done.70), calls=%async_computation.7 | async-start | bytes 131072 | tf_op jit(solution)/shard_map/slice | solution.py:141
  194.4 9.3 %slice-start.9 = ((f32[3,32,32]{2,1,0:T(8,128)}), f32[1,32,32]{2,1,0:T(8,128)S(1)}, s32[]{:S(2)}) async-start(f32[3,32,32]{2,1,0:T(8,128)} %copy-done.81), calls=%async_computation.9 | async-start | bytes 32768 | tf_op jit(solution)/shard_map/slice | solution.py:141
  196.2 9.2 %copy-start.71 = (f32[4,64,64]{2,1,0:T(8,128)S(1)}, f32[4,64,64]{2,1,0:T(8,128)}, u32[]{:S(2)}) copy-start(f32[4,64,64]{2,1,0:T(8,128)} %copy-done.70) | copy-start | bytes 196612
  196.2 9.2 %copy-start.95 = (s32[128]{0:T(128)S(1)}, s32[128]{0:T(128)}, u32[]{:S(2)}) copy-start(s32[128]{0:T(128)} %copy-done.92) | copy-start | bytes 1540
  196.2 10.8 %copy-start.6 = (f32[8,128,128]{2,1,0:T(8,128)S(1)}, f32[8,128,128]{2,1,0:T(8,128)}, u32[]{:S(2)}) copy-start(f32[8,128,128]{2,1,0:T(8,128)} %copy-done.4) | copy-start | bytes 1572868
  196.2 10.8 %copy-start.9 = (f32[8,128,128]{2,1,0:T(8,128)S(1)}, f32[8,128,128]{2,1,0:T(8,128)}, u32[]{:S(2)}) copy-start(f32[8,128,128]{2,1,0:T(8,128)} %copy-done.7) | copy-start | bytes 1572868
  196.2 10.8 %copy-start.13 = (f32[8,128,128]{2,1,0:T(8,128)S(1)}, f32[8,128,128]{2,1,0:T(8,128)}, u32[]{:S(2)}) copy-start(f32[8,128,128]{2,1,0:T(8,128)} %copy-done.10) | copy-start | bytes 1572868
  196.2 10.8 %copy-start.23 = (f32[8,128,128]{2,1,0:T(8,128)S(1)}, f32[8,128,128]{2,1,0:T(8,128)}, u32[]{:S(2)}) copy-start(f32[8,128,128]{2,1,0:T(8,128)} %copy-done.22) | copy-start | bytes 1572868
  196.2 10.8 %copy-start.29 = (f32[6,128,128]{2,1,0:T(8,128)S(1)}, f32[6,128,128]{2,1,0:T(8,128)}, u32[]{:S(2)}) copy-start(f32[6,128,128]{2,1,0:T(8,128)} %copy-done.28) | copy-start | bytes 1179652
  196.2 10.8 %slice-start = ((f32[6,128,128]{2,1,0:T(8,128)}), f32[4,128,128]{2,1,0:T(8,128)S(1)}, s32[]{:S(2)}) async-start(f32[6,128,128]{2,1,0:T(8,128)} %copy-done.28), calls=%async_computation | async-start | bytes 524288 | tf_op jit(solution)/shard_map/slice | solution.py:141
  196.2 10.8 %copy-start.89 = (s32[256]{0:T(256)S(1)}, s32[256]{0:T(256)}, u32[]{:S(2)}) copy-start(s32[256]{0:T(256)} %copy-done.86) | copy-start | bytes 3076
  (78 other events, 334.0 us)
